TPU v7x, 512 devices: a whole 4x8x8 slice. The times are simulated.
512 devices in a mesh: tm: 16 (over z, y_hi), space: 32 (over x, y_lo, core).
Axes of the slice: x: 4, y: 8 (y_hi: 2, y_lo: 4; y = y_hi * 4 + y_lo), z: 8, core: 2. Of those that a mesh axis runs over, the one named last changes fastest.
Arguments:
- state: float32 [16, 5, 256, 32, 128], P('tm', None, 'space'), may hold values from -6 to 6
- base: float32 [16, 5, 256, 32, 128], P('tm', None, 'space'), may hold values from -6 to 6
- pseudo_step: float32 [256, 32, 128], P('space'), may hold values from 0.05 to 0.3
- eddy_visc: float32 [256, 32, 128], P('space'), may hold values from 0.02 to 0.2
- jacobians: float32 [3, 5, 5], replicated, may hold values from -2.5 to 2.5
- partner_radial: int32 [2, 256, 128], P(None, 'space'), may hold values from 0 to 127, each once within a row
- partner_instance: int32 [16, 2, 256, 128], P('tm', None, 'space'), may hold values from 0 to 15, as said below
Outputs:
- updated: float32 [16, 5, 256, 32, 128], P('tm', None, 'space')
Inputs may be any that keep to these rules, and one draw needn't show every extreme that they name: partner_radial[s, i, :] is a permutation of the radial indices 0..127: the partner cells on the opposite periodic face in the same axial plane. partner_instance[n, 0, i, k] = (n + L_i) mod 16 and partner_instance[n, 1, i, k] = (n - L_i) mod 16 for a lag L_i in 1..15 that depends only on the axial plane i.
All inputs are finite; a program needn't handle non-finite values.
Results may differ from a plain program's by a relative error of at most 0.00005.
Values sent between devices are 32-bit elements; how exact they have to be, the bound alone decides.
No kernel may reach another device: no remote copies, remote signals or barrier semaphores. Data moves between devices by JAX's collectives and lax.ppermute only.
A program may use at most 64 MiB of HBM per device.

v0:
```python
import math

import jax
import jax.numpy as jnp
from jax import lax
from jax.sharding import PartitionSpec as P

SECTION_ALPHA = 0.5
PITCH_ANGLE = 2.0 * math.pi / 36.0
NYQUIST_DAMP = 2.0


def shifted(value, axis, by):
    devices = lax.axis_size(axis)
    return lax.ppermute(value, axis, [(i, (i + by) % devices) for i in range(devices)])


def extended_2(block, sides, width):
    for axis, dim in sides:
        count = lax.axis_size(axis)
        forward = [(i, i + 1) for i in range(count - 1)]
        backward = [(target, source) for source, target in forward]
        low = lax.ppermute(
            lax.slice_in_dim(block, block.shape[dim] - width, None, axis=dim), axis, forward
        )
        high = lax.ppermute(lax.slice_in_dim(block, 0, width, axis=dim), axis, backward)
        block = jnp.concatenate([low, block, high], axis=dim)
    return block


def time_weights(offset, count):
    offset = offset % count
    angle = math.pi * offset.astype(jnp.float32) / count
    parity = jnp.where(offset % 2 == 1, 1.0, -1.0).astype(jnp.float32)
    sine = jnp.where(offset == 0, 1.0, jnp.sin(angle))
    spectral = 0.5 * parity * jnp.cos(angle) / sine - NYQUIST_DAMP * parity / count
    return jnp.where(offset == 0, NYQUIST_DAMP / count, spectral)


def rotate_velocity(values, turn):
    cosine = math.cos(PITCH_ANGLE)
    sine = turn * math.sin(PITCH_ANGLE)
    second = values[:, 2]
    third = values[:, 3]
    return jnp.stack(
        [
            values[:, 0],
            values[:, 1],
            cosine * second - sine * third,
            sine * second + cosine * third,
            values[:, 4],
        ],
        axis=1,
    )


def section_update(
    state, base, pseudo_step, eddy_visc, jacobians, up_i, down_i, low_ghost, high_ghost, time_term
):
    up_j = jnp.concatenate([state[:, :, :, 1:], high_ghost[:, :, :, None]], axis=3)
    down_j = jnp.concatenate([low_ghost[:, :, :, None], state[:, :, :, :-1]], axis=3)
    zeros = jnp.zeros(state.shape[:4] + (1,), state.dtype)
    up_k = jnp.concatenate([state[..., 1:], zeros], axis=4)
    down_k = jnp.concatenate([zeros, state[..., :-1]], axis=4)
    diffs = jnp.stack([up_i - down_i, up_j - down_j, up_k - down_k], axis=0) * 0.5
    flux = jnp.einsum("dab,dnbijk->naijk", jacobians, diffs, precision=lax.Precision.HIGHEST)
    laplace = up_i + down_i + up_j + down_j + up_k + down_k - 6.0 * state
    spatial = flux - eddy_visc[None, None] * laplace
    return base - SECTION_ALPHA * pseudo_step[None, None] * (spatial + time_term)


def radial_table(partner_radial):
    radial_count = partner_radial.shape[2]
    radial_ids = jnp.arange(radial_count, dtype=jnp.int32)
    return (partner_radial[..., None] == radial_ids).astype(jnp.float32)


def per_device(state, base, pseudo_step, eddy_visc, jacobians, partner_radial, partner_instance):
    local_count = state.shape[0]
    cycle_size = lax.axis_size("tm")
    total_count = local_count * cycle_size
    position = lax.axis_index("tm")
    local_ids = jnp.arange(local_count, dtype=jnp.int32)
    own_ids = position * local_count + local_ids
    flattened = state.reshape(local_count, -1)
    start_weights = time_weights(own_ids[:, None] - own_ids[None, :], total_count)
    initial = jnp.dot(start_weights, flattened, precision=lax.Precision.HIGHEST)

    def one_turn(turn_index, carry):
        moving, accumulated = carry
        moving = shifted(moving, "tm", 1)
        anchor = (position - turn_index) % cycle_size
        source_ids = anchor * local_count + local_ids
        weights = time_weights(own_ids[:, None] - source_ids[None, :], total_count)
        return (moving, accumulated + jnp.dot(weights, moving, precision=lax.Precision.HIGHEST))

    moved_last, accumulated = lax.fori_loop(1, cycle_size, one_turn, (flattened, initial))
    time_term = accumulated.reshape(state.shape)
    radial_hot = radial_table(partner_radial)
    face_planes = jnp.stack([state[:, :, :, -1, :], state[:, :, :, 0, :]], axis=1)
    all_faces = lax.all_gather(face_planes, "tm", axis=0, tiled=True)
    instance_ids = jnp.arange(total_count, dtype=jnp.int32)
    instance_hot = (partner_instance[:, :, :, 0][..., None] == instance_ids).astype(jnp.float32)
    picked = jnp.einsum(
        "nsim,msvik->nsvik", instance_hot, all_faces, precision=lax.Precision.HIGHEST
    )
    remapped = jnp.einsum("nsvir,sikr->nsvik", picked, radial_hot, precision=lax.Precision.HIGHEST)
    low_ghost = rotate_velocity(remapped[:, 0], -1.0)
    high_ghost = rotate_velocity(remapped[:, 1], 1.0)
    extended = extended_2(state, (("space", 2),), 1)
    up_i = extended[:, :, 2:]
    down_i = extended[:, :, :-2]
    return section_update(
        state,
        base,
        pseudo_step,
        eddy_visc,
        jacobians,
        up_i,
        down_i,
        low_ghost,
        high_ghost,
        time_term,
    )


def solution(mesh):
    return jax.shard_map(
        per_device,
        mesh=mesh,
        in_specs=(
            P("tm", None, "space", None, None),
            P("tm", None, "space", None, None),
            P("space", None, None),
            P("space", None, None),
            P(),
            P(None, "space", None),
            P("tm", None, "space", None),
        ),
        out_specs=P("tm", None, "space", None, None),
        check_vma=False,
    )
```

profile of v0, /device:TPU:64, one launch (start us, length us, event | category | flops | bytes accessed | tf_op | source)
XLA Modules:
  0.0 639.7 jit_solution(3489502226336061569)
XLA Ops:
  7.9 75.3 %all_gather.3 = f32[16,2,5,8,128]{4,3,2,1,0:T(8,128)S(1)} all-gather(f32[1,2,5,8,128]{4,3,2,1,0:T(8,128)S(1)} %pad_maximum_fusion.4), channel_id=1, replica_groups=mesh['tm'=16,'space'=32] {'tm'}, dimensions={0}, use_global_device_ids=true | all-gather | bytes 696320 | tf_op jit(solution)/shard_map/all_gather | solution.py:101
  89.6 2.7 pad_subtract_fusion
  94.7 536.5 %while.18 = (s32[]{:T(128)}, f32[1,163840]{1,0:T(1,128)}, f32[1,163840]{1,0:T(1,128)S(1)}, s32[]{:T(128)}, s32[]{:T(128)}, /*index=5*/s32[]{:T(128)}, s32[]{:T(1...) while((s32[]{:T(128)}, f32[1,163840]{1,0:T(1,128)}, ...), condition=%wide.region_1.2_spmd, body=%wide.region_0.1_spmd.sunk | while | flops 327729 | bytes 5898953 | solution.py:97
  96.8 21.0 %collective-permute-done = f32[1,163840]{1,0:T(1,128)S(1)} collective-permute-done((f32[1,163840]{1,0:T(1,128)}, f32[1,163840]{1,0:T(1,128)S(1)}, u32[]{:S(2)}, u32[]{:S(2)}) %collective-permute-start) | collective-permute-done | bytes 655392 | tf_op jit(solution)/shard_map/while/body/eval_jaxpr/ppermute | solution.py:15
  121.6 25.5 %collective-permute-done = f32[1,163840]{1,0:T(1,128)S(1)} collective-permute-done((f32[1,163840]{1,0:T(1,128)}, f32[1,163840]{1,0:T(1,128)S(1)}, u32[]{:S(2)}, u32[]{:S(2)}) %collective-permute-start) | collective-permute-done | bytes 655392 | tf_op jit(solution)/shard_map/while/body/eval_jaxpr/ppermute | solution.py:15
  148.7 3.7 collective-permute-start
  152.6 24.9 %collective-permute-done = f32[1,163840]{1,0:T(1,128)S(1)} collective-permute-done((f32[1,163840]{1,0:T(1,128)}, f32[1,163840]{1,0:T(1,128)S(1)}, u32[]{:S(2)}, u32[]{:S(2)}) %collective-permute-start) | collective-permute-done | bytes 655392 | tf_op jit(solution)/shard_map/while/body/eval_jaxpr/ppermute | solution.py:15
  179.1 4.9 collective-permute-start
  184.2 19.7 %collective-permute-done = f32[1,163840]{1,0:T(1,128)S(1)} collective-permute-done((f32[1,163840]{1,0:T(1,128)}, f32[1,163840]{1,0:T(1,128)S(1)}, u32[]{:S(2)}, u32[]{:S(2)}) %collective-permute-start) | collective-permute-done | bytes 655392 | tf_op jit(solution)/shard_map/while/body/eval_jaxpr/ppermute | solution.py:15
  205.6 8.2 %collective-permute-start = (f32[1,163840]{1,0:T(1,128)}, f32[1,163840]{1,0:T(1,128)S(1)}, u32[]{:S(2)}, u32[]{:S(2)}) collective-permute-start(f32[1,163840]{1,0:T(1,128)} %get-tuple-element.213), channel_id=1, source_target_pairs={{0,32},{32,64},{64,96},{96,128},{128,160},{160,192},{192,224},{224... | collective-permute-start | bytes 1966088 | tf_op jit(solution)/shard_map/while/body/eval_jaxpr/ppermute | solution.py:15
  214.1 36.3 %collective-permute-done = f32[1,163840]{1,0:T(1,128)S(1)} collective-permute-done((f32[1,163840]{1,0:T(1,128)}, f32[1,163840]{1,0:T(1,128)S(1)}, u32[]{:S(2)}, u32[]{:S(2)}) %collective-permute-start) | collective-permute-done | bytes 655392 | tf_op jit(solution)/shard_map/while/body/eval_jaxpr/ppermute | solution.py:15
  254.1 27.1 %collective-permute-done = f32[1,163840]{1,0:T(1,128)S(1)} collective-permute-done((f32[1,163840]{1,0:T(1,128)}, f32[1,163840]{1,0:T(1,128)S(1)}, u32[]{:S(2)}, u32[]{:S(2)}) %collective-permute-start) | collective-permute-done | bytes 655392 | tf_op jit(solution)/shard_map/while/body/eval_jaxpr/ppermute | solution.py:15
  282.8 8.3 %collective-permute-start = (f32[1,163840]{1,0:T(1,128)}, f32[1,163840]{1,0:T(1,128)S(1)}, u32[]{:S(2)}, u32[]{:S(2)}) collective-permute-start(f32[1,163840]{1,0:T(1,128)} %get-tuple-element.213), channel_id=1, source_target_pairs={{0,32},{32,64},{64,96},{96,128},{128,160},{160,192},{192,224},{224... | collective-permute-start | bytes 1966088 | tf_op jit(solution)/shard_map/while/body/eval_jaxpr/ppermute | solution.py:15
  291.4 42.6 %collective-permute-done = f32[1,163840]{1,0:T(1,128)S(1)} collective-permute-done((f32[1,163840]{1,0:T(1,128)}, f32[1,163840]{1,0:T(1,128)S(1)}, u32[]{:S(2)}, u32[]{:S(2)}) %collective-permute-start) | collective-permute-done | bytes 655392 | tf_op jit(solution)/shard_map/while/body/eval_jaxpr/ppermute | solution.py:15
  337.8 37.0 %collective-permute-done = f32[1,163840]{1,0:T(1,128)S(1)} collective-permute-done((f32[1,163840]{1,0:T(1,128)}, f32[1,163840]{1,0:T(1,128)S(1)}, u32[]{:S(2)}, u32[]{:S(2)}) %collective-permute-start) | collective-permute-done | bytes 655392 | tf_op jit(solution)/shard_map/while/body/eval_jaxpr/ppermute | solution.py:15
  376.4 8.2 %collective-permute-start = (f32[1,163840]{1,0:T(1,128)}, f32[1,163840]{1,0:T(1,128)S(1)}, u32[]{:S(2)}, u32[]{:S(2)}) collective-permute-start(f32[1,163840]{1,0:T(1,128)} %get-tuple-element.213), channel_id=1, source_target_pairs={{0,32},{32,64},{64,96},{96,128},{128,160},{160,192},{192,224},{224... | collective-permute-start | bytes 1966088 | tf_op jit(solution)/shard_map/while/body/eval_jaxpr/ppermute | solution.py:15
  384.9 40.9 %collective-permute-done = f32[1,163840]{1,0:T(1,128)S(1)} collective-permute-done((f32[1,163840]{1,0:T(1,128)}, f32[1,163840]{1,0:T(1,128)S(1)}, u32[]{:S(2)}, u32[]{:S(2)}) %collective-permute-start) | collective-permute-done | bytes 655392 | tf_op jit(solution)/shard_map/while/body/eval_jaxpr/ppermute | solution.py:15
  429.6 35.7 %collective-permute-done = f32[1,163840]{1,0:T(1,128)S(1)} collective-permute-done((f32[1,163840]{1,0:T(1,128)}, f32[1,163840]{1,0:T(1,128)S(1)}, u32[]{:S(2)}, u32[]{:S(2)}) %collective-permute-start) | collective-permute-done | bytes 655392 | tf_op jit(solution)/shard_map/while/body/eval_jaxpr/ppermute | solution.py:15
  469.1 25.5 %collective-permute-done = f32[1,163840]{1,0:T(1,128)S(1)} collective-permute-done((f32[1,163840]{1,0:T(1,128)}, f32[1,163840]{1,0:T(1,128)S(1)}, u32[]{:S(2)}, u32[]{:S(2)}) %collective-permute-start) | collective-permute-done | bytes 655392 | tf_op jit(solution)/shard_map/while/body/eval_jaxpr/ppermute | solution.py:15
  498.4 36.0 %collective-permute-done = f32[1,163840]{1,0:T(1,128)S(1)} collective-permute-done((f32[1,163840]{1,0:T(1,128)}, f32[1,163840]{1,0:T(1,128)S(1)}, u32[]{:S(2)}, u32[]{:S(2)}) %collective-permute-start) | collective-permute-done | bytes 655392 | tf_op jit(solution)/shard_map/while/body/eval_jaxpr/ppermute | solution.py:15
  538.2 28.6 %collective-permute-done = f32[1,163840]{1,0:T(1,128)S(1)} collective-permute-done((f32[1,163840]{1,0:T(1,128)}, f32[1,163840]{1,0:T(1,128)S(1)}, u32[]{:S(2)}, u32[]{:S(2)}) %collective-permute-start) | collective-permute-done | bytes 655392 | tf_op jit(solution)/shard_map/while/body/eval_jaxpr/ppermute | solution.py:15
  570.5 35.1 %collective-permute-done = f32[1,163840]{1,0:T(1,128)S(1)} collective-permute-done((f32[1,163840]{1,0:T(1,128)}, f32[1,163840]{1,0:T(1,128)S(1)}, u32[]{:S(2)}, u32[]{:S(2)}) %collective-permute-start) | collective-permute-done | bytes 655392 | tf_op jit(solution)/shard_map/while/body/eval_jaxpr/ppermute | solution.py:15
  609.4 20.2 %collective-permute-done = f32[1,163840]{1,0:T(1,128)S(1)} collective-permute-done((f32[1,163840]{1,0:T(1,128)}, f32[1,163840]{1,0:T(1,128)S(1)}, u32[]{:S(2)}, u32[]{:S(2)}) %collective-permute-start) | collective-permute-done | bytes 655392 | tf_op jit(solution)/shard_map/while/body/eval_jaxpr/ppermute | solution.py:15
  631.2 7.5 %fusion.10 = f32[1,5,8,32,128]{4,1,0,3,2:T(8,128)S(1)} fusion(f32[1,5,8,32,128]{4,1,0,3,2:T(8,128)} %pad_subtract_fusion, f32[1,5,8,32,128]{4,1,0,3,2:T(8,128)} %fusion.12, f32[1,5,8,32,128]{4,1,0,3,2:T(8,128)} %fusion.13, f32[1,5,8,32,128]{4,3,2,1,0:T(8,128)} %param.10, f32[1,5,8,32,128]{4,3,2,1,0:T(8,128)S(1)} %bitcast.55, ...), kind=kOutput, calls=%fused_computation.12 | convolution fusion | flops 33587200 | bytes 7625004 | tf_op jit(solution)/shard_map/dab,dnbijk->naijk/dot_general | solution.py:66
  (87 shorter events, 60.4 us)
Async XLA Ops:
  0.0 631.2 %copy-start = (f32[3,5,5]{2,0,1:T(4,128)S(1)}, f32[3,5,5]{2,0,1:T(4,128)}, u32[]{:S(2)}) copy-start(f32[3,5,5]{2,0,1:T(4,128)} %param.13) | copy-start | bytes 904
  2.0 5.6 copy-start.7
  3.5 80.2 %copy-start.8 = (s32[2,8,128]{2,1,0:T(8,128)S(1)}, s32[2,8,128]{2,1,0:T(8,128)}, u32[]{:S(2)}) copy-start(s32[2,8,128]{2,1,0:T(8,128)} %param.14) | copy-start | bytes 24580
  3.5 90.0 %collective-permute-start.2 = (f32[1,5,1,32,128]{4,1,0,3,2:T(8,128)S(1)}, f32[1,5,1,32,128]{4,1,0,3,2:T(8,128)S(1)}, u32[]{:S(2)}, u32[]{:S(2)}) collective-permute-start(f32[1,5,1,32,128]{4,1,0,3,2:T(8,128)S(1)} %get-tuple-element.150), channel_id=1, source_target_pairs={{0,1},{1,2},{2,3},{3,4},{4,5},{5,6},{6,7},{7,8},{8,9},{9,10},{10,1... | collective-permute-start | bytes 245768 | tf_op jit(solution)/shard_map/ppermute | solution.py:23
  5.3 88.2 %collective-permute-start.1 = (f32[1,5,1,32,128]{4,1,0,3,2:T(8,128)S(1)}, f32[1,5,1,32,128]{4,1,0,3,2:T(8,128)S(1)}, u32[]{:S(2)}, u32[]{:S(2)}) collective-permute-start(f32[1,5,1,32,128]{4,1,0,3,2:T(8,128)S(1)} %get-tuple-element.151), channel_id=1, source_target_pairs={{1,0},{2,1},{3,2},{4,3},{5,4},{6,5},{7,6},{8,7},{9,8},{10,9},{11,1... | collective-permute-start | bytes 245768 | tf_op jit(solution)/shard_map/ppermute | solution.py:26
  89.6 2.8 copy-start.4
  89.6 2.7 copy-start.5
  89.6 2.7 copy-start.1
  89.6 2.7 copy-start.2
  94.7 23.2 %collective-permute-start = (f32[1,163840]{1,0:T(1,128)}, f32[1,163840]{1,0:T(1,128)S(1)}, u32[]{:S(2)}, u32[]{:S(2)}) collective-permute-start(f32[1,163840]{1,0:T(1,128)} %get-tuple-element.213), channel_id=1, source_target_pairs={{0,32},{32,64},{64,96},{96,128},{128,160},{160,192},{192,224},{224... | collective-permute-start | bytes 1966088 | tf_op jit(solution)/shard_map/while/body/eval_jaxpr/ppermute | solution.py:15
  119.5 27.7 %collective-permute-start = (f32[1,163840]{1,0:T(1,128)}, f32[1,163840]{1,0:T(1,128)S(1)}, u32[]{:S(2)}, u32[]{:S(2)}) collective-permute-start(f32[1,163840]{1,0:T(1,128)} %get-tuple-element.213), channel_id=1, source_target_pairs={{0,32},{32,64},{64,96},{96,128},{128,160},{160,192},{192,224},{224... | collective-permute-start | bytes 1966088 | tf_op jit(solution)/shard_map/while/body/eval_jaxpr/ppermute | solution.py:15
  148.7 28.8 %collective-permute-start = (f32[1,163840]{1,0:T(1,128)}, f32[1,163840]{1,0:T(1,128)S(1)}, u32[]{:S(2)}, u32[]{:S(2)}) collective-permute-start(f32[1,163840]{1,0:T(1,128)} %get-tuple-element.213), channel_id=1, source_target_pairs={{0,32},{32,64},{64,96},{96,128},{128,160},{160,192},{192,224},{224... | collective-permute-start | bytes 1966088 | tf_op jit(solution)/shard_map/while/body/eval_jaxpr/ppermute | solution.py:15
  179.1 24.9 %collective-permute-start = (f32[1,163840]{1,0:T(1,128)}, f32[1,163840]{1,0:T(1,128)S(1)}, u32[]{:S(2)}, u32[]{:S(2)}) collective-permute-start(f32[1,163840]{1,0:T(1,128)} %get-tuple-element.213), channel_id=1, source_target_pairs={{0,32},{32,64},{64,96},{96,128},{128,160},{160,192},{192,224},{224... | collective-permute-start | bytes 1966088 | tf_op jit(solution)/shard_map/while/body/eval_jaxpr/ppermute | solution.py:15
  205.6 44.8 %collective-permute-start = (f32[1,163840]{1,0:T(1,128)}, f32[1,163840]{1,0:T(1,128)S(1)}, u32[]{:S(2)}, u32[]{:S(2)}) collective-permute-start(f32[1,163840]{1,0:T(1,128)} %get-tuple-element.213), channel_id=1, source_target_pairs={{0,32},{32,64},{64,96},{96,128},{128,160},{160,192},{192,224},{224... | collective-permute-start | bytes 1966088 | tf_op jit(solution)/shard_map/while/body/eval_jaxpr/ppermute | solution.py:15
  251.9 29.3 %collective-permute-start = (f32[1,163840]{1,0:T(1,128)}, f32[1,163840]{1,0:T(1,128)S(1)}, u32[]{:S(2)}, u32[]{:S(2)}) collective-permute-start(f32[1,163840]{1,0:T(1,128)} %get-tuple-element.213), channel_id=1, source_target_pairs={{0,32},{32,64},{64,96},{96,128},{128,160},{160,192},{192,224},{224... | collective-permute-start | bytes 1966088 | tf_op jit(solution)/shard_map/while/body/eval_jaxpr/ppermute | solution.py:15
  282.8 51.2 %collective-permute-start = (f32[1,163840]{1,0:T(1,128)}, f32[1,163840]{1,0:T(1,128)S(1)}, u32[]{:S(2)}, u32[]{:S(2)}) collective-permute-start(f32[1,163840]{1,0:T(1,128)} %get-tuple-element.213), channel_id=1, source_target_pairs={{0,32},{32,64},{64,96},{96,128},{128,160},{160,192},{192,224},{224... | collective-permute-start | bytes 1966088 | tf_op jit(solution)/shard_map/while/body/eval_jaxpr/ppermute | solution.py:15
  335.6 39.2 %collective-permute-start = (f32[1,163840]{1,0:T(1,128)}, f32[1,163840]{1,0:T(1,128)S(1)}, u32[]{:S(2)}, u32[]{:S(2)}) collective-permute-start(f32[1,163840]{1,0:T(1,128)} %get-tuple-element.213), channel_id=1, source_target_pairs={{0,32},{32,64},{64,96},{96,128},{128,160},{160,192},{192,224},{224... | collective-permute-start | bytes 1966088 | tf_op jit(solution)/shard_map/while/body/eval_jaxpr/ppermute | solution.py:15
  376.4 49.4 %collective-permute-start = (f32[1,163840]{1,0:T(1,128)}, f32[1,163840]{1,0:T(1,128)S(1)}, u32[]{:S(2)}, u32[]{:S(2)}) collective-permute-start(f32[1,163840]{1,0:T(1,128)} %get-tuple-element.213), channel_id=1, source_target_pairs={{0,32},{32,64},{64,96},{96,128},{128,160},{160,192},{192,224},{224... | collective-permute-start | bytes 1966088 | tf_op jit(solution)/shard_map/while/body/eval_jaxpr/ppermute | solution.py:15
  427.5 37.9 %collective-permute-start = (f32[1,163840]{1,0:T(1,128)}, f32[1,163840]{1,0:T(1,128)S(1)}, u32[]{:S(2)}, u32[]{:S(2)}) collective-permute-start(f32[1,163840]{1,0:T(1,128)} %get-tuple-element.213), channel_id=1, source_target_pairs={{0,32},{32,64},{64,96},{96,128},{128,160},{160,192},{192,224},{224... | collective-permute-start | bytes 1966088 | tf_op jit(solution)/shard_map/while/body/eval_jaxpr/ppermute | solution.py:15
  467.0 27.6 %collective-permute-start = (f32[1,163840]{1,0:T(1,128)}, f32[1,163840]{1,0:T(1,128)S(1)}, u32[]{:S(2)}, u32[]{:S(2)}) collective-permute-start(f32[1,163840]{1,0:T(1,128)} %get-tuple-element.213), channel_id=1, source_target_pairs={{0,32},{32,64},{64,96},{96,128},{128,160},{160,192},{192,224},{224... | collective-permute-start | bytes 1966088 | tf_op jit(solution)/shard_map/while/body/eval_jaxpr/ppermute | solution.py:15
  496.2 38.2 %collective-permute-start = (f32[1,163840]{1,0:T(1,128)}, f32[1,163840]{1,0:T(1,128)S(1)}, u32[]{:S(2)}, u32[]{:S(2)}) collective-permute-start(f32[1,163840]{1,0:T(1,128)} %get-tuple-element.213), channel_id=1, source_target_pairs={{0,32},{32,64},{64,96},{96,128},{128,160},{160,192},{192,224},{224... | collective-permute-start | bytes 1966088 | tf_op jit(solution)/shard_map/while/body/eval_jaxpr/ppermute | solution.py:15
  536.0 30.7 %collective-permute-start = (f32[1,163840]{1,0:T(1,128)}, f32[1,163840]{1,0:T(1,128)S(1)}, u32[]{:S(2)}, u32[]{:S(2)}) collective-permute-start(f32[1,163840]{1,0:T(1,128)} %get-tuple-element.213), channel_id=1, source_target_pairs={{0,32},{32,64},{64,96},{96,128},{128,160},{160,192},{192,224},{224... | collective-permute-start | bytes 1966088 | tf_op jit(solution)/shard_map/while/body/eval_jaxpr/ppermute | solution.py:15
  568.4 37.2 %collective-permute-start = (f32[1,163840]{1,0:T(1,128)}, f32[1,163840]{1,0:T(1,128)S(1)}, u32[]{:S(2)}, u32[]{:S(2)}) collective-permute-start(f32[1,163840]{1,0:T(1,128)} %get-tuple-element.213), channel_id=1, source_target_pairs={{0,32},{32,64},{64,96},{96,128},{128,160},{160,192},{192,224},{224... | collective-permute-start | bytes 1966088 | tf_op jit(solution)/shard_map/while/body/eval_jaxpr/ppermute | solution.py:15
  607.2 22.4 %collective-permute-start = (f32[1,163840]{1,0:T(1,128)}, f32[1,163840]{1,0:T(1,128)S(1)}, u32[]{:S(2)}, u32[]{:S(2)}) collective-permute-start(f32[1,163840]{1,0:T(1,128)} %get-tuple-element.213), channel_id=1, source_target_pairs={{0,32},{32,64},{64,96},{96,128},{128,160},{160,192},{192,224},{224... | collective-permute-start | bytes 1966088 | tf_op jit(solution)/shard_map/while/body/eval_jaxpr/ppermute | solution.py:15
  (2 other events, 2.5 us)
where the time goes:
time: 640 us
  waiting for transfers between devices  456 us (71%)
  blocking collectives  75.3 us (12%)
  starting transfers between devices  55.5 us (9%)
  local copies, waits for them, and re-layouts  21 us (3%)
  other arithmetic  18.1 us (3%)
  matrix products  9.23 us (1%)
    ppermute x15, waiting for transfers between devices, shifted(): lax.ppermute(value, axis, [(i, (i + by) % devices) for i in range(devices)])  456 us
    all_gather x1, blocking collectives, per_device(): all_faces = lax.all_gather(face_planes, 'tm', axis=0, tiled=True)  75.3 us
    ppermute x15, starting transfers between devices, shifted(): lax.ppermute(value, axis, [(i, (i + by) % devices) for i in range(devices)])  52.5 us
  transfers between devices with their start and end apart: 17, of which 15 were waited for; matrix products, arithmetic and copies ran while one was open for 2% of the time, Pallas kernels for 0%

commit v1 on v0

v1 whole, which is shorter than its diff:
```python
import math

import jax
import jax.numpy as jnp
from jax import lax
from jax.sharding import Mesh
from jax.sharding import PartitionSpec as P

SECTION_ALPHA = 0.5
PITCH_ANGLE = 2.0 * math.pi / 36.0
NYQUIST_DAMP = 2.0
Y_PARTS = 2


def extended_2(block, sides, width):
    for axis, dim in sides:
        count = lax.axis_size(axis)
        forward = [(i, i + 1) for i in range(count - 1)]
        backward = [(target, source) for source, target in forward]
        low = lax.ppermute(
            lax.slice_in_dim(block, block.shape[dim] - width, None, axis=dim), axis, forward
        )
        high = lax.ppermute(lax.slice_in_dim(block, 0, width, axis=dim), axis, backward)
        block = jnp.concatenate([low, block, high], axis=dim)
    return block


def time_weights(offset, count):
    offset = offset % count
    angle = math.pi * offset.astype(jnp.float32) / count
    parity = jnp.where(offset % 2 == 1, 1.0, -1.0).astype(jnp.float32)
    sine = jnp.where(offset == 0, 1.0, jnp.sin(angle))
    spectral = 0.5 * parity * jnp.cos(angle) / sine - NYQUIST_DAMP * parity / count
    return jnp.where(offset == 0, NYQUIST_DAMP / count, spectral)


def rotate_velocity(values, turn):
    cosine = math.cos(PITCH_ANGLE)
    sine = turn * math.sin(PITCH_ANGLE)
    second = values[:, 2]
    third = values[:, 3]
    return jnp.stack(
        [
            values[:, 0],
            values[:, 1],
            cosine * second - sine * third,
            sine * second + cosine * third,
            values[:, 4],
        ],
        axis=1,
    )


def section_update(
    state, base, pseudo_step, eddy_visc, jacobians, up_i, down_i, low_ghost, high_ghost, time_term
):
    up_j = jnp.concatenate([state[:, :, :, 1:], high_ghost[:, :, :, None]], axis=3)
    down_j = jnp.concatenate([low_ghost[:, :, :, None], state[:, :, :, :-1]], axis=3)
    zeros = jnp.zeros(state.shape[:4] + (1,), state.dtype)
    up_k = jnp.concatenate([state[..., 1:], zeros], axis=4)
    down_k = jnp.concatenate([zeros, state[..., :-1]], axis=4)
    diffs = jnp.stack([up_i - down_i, up_j - down_j, up_k - down_k], axis=0) * 0.5
    flux = jnp.einsum("dab,dnbijk->naijk", jacobians, diffs, precision=lax.Precision.HIGHEST)
    laplace = up_i + down_i + up_j + down_j + up_k + down_k - 6.0 * state
    spatial = flux - eddy_visc[None, None] * laplace
    return base - SECTION_ALPHA * pseudo_step[None, None] * (spatial + time_term)


def per_device(state, base, pseudo_step, eddy_visc, jacobians, partner_radial, partner_instance):
    ring = lax.axis_size("tz")
    total_count = ring * Y_PARTS
    z = lax.axis_index("tz")
    y = lax.axis_index("ty")
    own = Y_PARTS * z + y
    partner = own + 1 - 2 * y
    flattened = state.reshape(1, -1)
    gathered = lax.all_gather(flattened, "tz", axis=0, tiled=True)
    held_ids = Y_PARTS * jnp.arange(ring, dtype=jnp.int32) + y
    targets = jnp.stack([own, partner])
    weights = time_weights(targets[:, None] - held_ids[None, :], total_count)
    partial = jnp.dot(weights, gathered, precision=lax.Precision.HIGHEST)

    held = gathered.reshape((ring,) + state.shape[1:])
    faces = jnp.stack([held[:, :, :, -1, :], held[:, :, :, 0, :]], axis=0)
    radial_count = partner_radial.shape[2]
    radial_hot = (partner_radial[..., None] == jnp.arange(radial_count, dtype=jnp.int32)).astype(
        jnp.float32
    )
    remapped = jnp.einsum("szvir,sikr->szvik", faces, radial_hot, precision=lax.Precision.HIGHEST)
    shifts = (targets - own)[:, None, None, None]
    sources = (partner_instance[0][None] + shifts) % total_count
    instance_hot = (sources[..., None] == held_ids).astype(jnp.float32)
    picked = jnp.sum(instance_hot[:, :, None] * jnp.moveaxis(remapped, 1, -1)[None], axis=-1)

    message = jnp.concatenate([partial[1], picked[1].reshape(-1)])
    received = lax.ppermute(message, "ty", [(i, Y_PARTS - 1 - i) for i in range(Y_PARTS)])
    split = partial.shape[1]
    time_term = (partial[0] + received[:split]).reshape(state.shape)
    ghosts = picked[0] + received[split:].reshape(picked.shape[1:])
    low_ghost = rotate_velocity(ghosts[0][None], -1.0)
    high_ghost = rotate_velocity(ghosts[1][None], 1.0)

    extended = extended_2(state, (("space", 2),), 1)
    up_i = extended[:, :, 2:]
    down_i = extended[:, :, :-2]
    return section_update(
        state,
        base,
        pseudo_step,
        eddy_visc,
        jacobians,
        up_i,
        down_i,
        low_ghost,
        high_ghost,
        time_term,
    )


def solution(mesh):
    devices = mesh.devices
    cells = devices.shape[1]
    split_mesh = Mesh(
        devices.reshape(devices.shape[0] // Y_PARTS, Y_PARTS, cells), ("tz", "ty", "space")
    )
    time_axes = ("tz", "ty")
    return jax.shard_map(
        per_device,
        mesh=split_mesh,
        in_specs=(
            P(time_axes, None, "space", None, None),
            P(time_axes, None, "space", None, None),
            P("space", None, None),
            P("space", None, None),
            P(),
            P(None, "space", None),
            P(time_axes, None, "space", None),
        ),
        out_specs=P(time_axes, None, "space", None, None),
        check_vma=False,
    )
```

time: 640 us -> 148 us (0.23)
  the two profiles are of different devices: /device:TPU:64 before, /device:TPU:17 now
where the time goes in v1:
time: 148 us
  waiting for transfers between devices  98.3 us (66%)
  matrix products  16.2 us (11%)
  between operations  13.7 us (9%)
  starting transfers between devices  11.1 us (8%)
  local copies, waits for them, and re-layouts  6.91 us (5%)
  other arithmetic  1.85 us (1%)
    all_gather x1, waiting for transfers between devices, per_device(): gathered = lax.all_gather(flattened, 'tz', axis=0, tiled=True)  65.7 us
    ppermute x1, waiting for transfers between devices, per_device(): lax.ppermute(message, 'ty', [(i, Y_PARTS - 1 - i) for i in range(Y_PARTS)])  31.8 us
    dot_general x1, matrix products, per_device(): partial = jnp.dot(weights, gathered, precision=lax.Precision.HIGHEST)  10 us
    ppermute x1, starting transfers between devices, per_device(): lax.ppermute(message, 'ty', [(i, Y_PARTS - 1 - i) for i in range(Y_PARTS)])  5.47 us
    dot_general x1, matrix products, section_update(): jnp.einsum('dab,dnbijk->naijk', jacobians, diffs, precision=lax.Precision...  4.78 us
    ppermute x1, starting transfers between devices, extended_2(): lax.ppermute(lax.slice_in_dim(block, block.shape[dim] - width, None, axis...  3.75 us
  transfers between devices with their start and end apart: 4, of which 2 were waited for; matrix products, arithmetic and copies ran while one was open for 13% of the time, Pallas kernels for 0%

profile of v1, /device:TPU:17, one launch (start us, length us, event | category | flops | bytes accessed | tf_op | source)
XLA Modules:
  0.0 148.1 jit_solution(6438422158685116744)
XLA Ops:
  6.5 0.7 all-gather.3.cloned.1.call-update
  7.3 1.5 %copy.85 = f32[1,5,8,32,128]{4,1,0,3,2:T(8,128)S(1)} copy(f32[1,5,8,32,128]{4,3,2,1,0:T(8,128)} %param.7) | data formatting | bytes 1310720 | tf_op args[0]
  8.8 0.7 fusion.66
  9.5 3.8 %collective-permute-start.1 = (f32[1,5,1,32,128]{4,1,0,3,2:T(8,128)}, f32[1,5,1,32,128]{4,1,0,3,2:T(8,128)S(1)}, u32[]{:S(2)}, u32[]{:S(2)}) collective-permute-start(f32[1,5,1,32,128]{4,1,0,3,2:T(8,128)} %get-tuple-element.11), channel_id=1, source_target_pairs={{0,1},{1,2},{2,3},{3,4},{4,5},{5,6},{6,7},{7,8},{8,9},{9,10},{10,1... | collective-permute-start | bytes 245768 | tf_op jit(solution)/shard_map/ppermute | solution.py:20
  13.3 1.9 %collective-permute-start = (f32[1,5,1,32,128]{4,1,0,3,2:T(8,128)}, f32[1,5,1,32,128]{4,1,0,3,2:T(8,128)S(1)}, u32[]{:S(2)}, u32[]{:S(2)}) collective-permute-start(f32[1,5,1,32,128]{4,1,0,3,2:T(8,128)} %get-tuple-element.12), channel_id=1, source_target_pairs={{1,0},{2,1},{3,2},{4,3},{5,4},{6,5},{7,6},{8,7},{9,8},{10,9},{11,1... | collective-permute-start | bytes 245768 | tf_op jit(solution)/shard_map/ppermute | solution.py:23
  15.2 0.1 broadcast_subtract_fusion
  15.3 0.8 add_select_fusion.1
  16.1 0.1 compare_convert_fusion
  16.1 0.1 fusion.67
  16.3 65.7 %all-gather.3.cloned.1.call-done = f32[8,1,163840]{2,1,0:T(1,128)} async-done(((f32[1,1,163840]{2,1,0:T(1,128)}), f32[8,1,163840]{2,1,0:T(1,128)}) %all-gather.3.cloned.1.call-update) | async-done | bytes 5242896 | tf_op jit(solution)/shard_map/all_gather | solution.py:77
  82.0 2.0 %fusion.64 = (f32[8,5,8,1,128]{4,3,2,1,0:T(1,128)S(1)}, f32[8,5,8,1,128]{4,3,2,1,0:T(1,128)S(1)}) fusion(f32[8,5,8,32,128]{4,3,2,1,0:T(8,128)} %bitcast.48), kind=kLoop, calls=%fused_computation.101 | loop fusion | bytes 655360 | tf_op jit(solution)/shard_map/slice | solution.py:84
  84.1 0.1 copy_bitcast_fusion
  84.1 1.4 convolution_bitcast_fusion
  85.6 0.2 multiply_reduce_fusion
  85.8 10.0 %fusion = f32[2,163840]{1,0:T(2,128)S(1)} fusion(f32[8,1,163840]{2,1,0:T(1,128)} %all-gather.3.cloned.1.call-done, s32[8]{0:T(128)S(1)} %multiply_add_fusion.2, s32[2]{0:T(128)S(1)} %get-tuple-element.6), kind=kOutput, calls=%fused_computation | convolution fusion | flops 31457840 | bytes 6553640 | tf_op jit(solution)/shard_map/dot_general | solution.py:81
  95.8 1.1 fusion.65
  96.9 5.5 %collective-permute-start.2 = (f32[174080]{0:T(1024)S(1)}, f32[174080]{0:T(1024)S(1)}, u32[]{:S(2)}, u32[]{:S(2)}) collective-permute-start(f32[174080]{0:T(1024)S(1)} %pad_maximum_fusion.4), channel_id=1, source_target_pairs={{0,32},{32,0},{1,33},{33,1},{2,34},{34,2},{3,35},{35,3},{4,36},{36... | collective-permute-start | bytes 2088968 | tf_op jit(solution)/shard_map/ppermute | solution.py:96
  102.4 0.3 fusion.68
  102.8 0.3 pad_subtract_fusion
  103.2 0.1 fusion.17
  103.3 31.8 %collective-permute-done.2 = f32[174080]{0:T(1024)S(1)} collective-permute-done((f32[174080]{0:T(1024)S(1)}, f32[174080]{0:T(1024)S(1)}, u32[]{:S(2)}, u32[]{:S(2)}) %collective-permute-start.2) | collective-permute-done | bytes 696352 | tf_op jit(solution)/shard_map/ppermute | solution.py:96
  135.2 0.2 fusion.16
  135.5 4.8 %fusion.13 = f32[1,5,8,32,128]{4,1,0,3,2:T(8,128)S(1)} fusion(f32[1,5,8,32,128]{4,1,0,3,2:T(8,128)S(1)} %pad_subtract_fusion, f32[1,5,8,32,128]{4,1,0,3,2:T(8,128)S(1)} %fusion.16, f32[1,5,8,32,128]{4,1,0,3,2:T(8,128)S(1)} %fusion.17, f32[1,5,8,32,128]{4,3,2,1,0:T(8,128)S(1)} %copy-done.1, f32[1,5,8,32,128]{4,3,2,1,0:T(8,128)S(1)} %bitcast.50, ...), kind=kOutput, calls=%fused_computation.14 | convolution fusion | flops 33751040 | bytes 8280364 | tf_op jit(solution)/shard_map/dab,dnbijk->naijk/dot_general | solution.py:63
  140.3 1.0 copy.102
  (26 shorter events, 0.2 us)
Async XLA Ops:
  6.5 128.9 %copy-start = (f32[3,5,5]{2,0,1:T(4,128)S(1)}, f32[3,5,5]{2,0,1:T(4,128)}, u32[]{:S(2)}) copy-start(f32[3,5,5]{2,0,1:T(4,128)} %param.11) | copy-start | bytes 904
  6.5 75.5 %all-gather.3.cloned.1.call-start = ((), (), s32[]{:S(2)}) async-start(), calls=%async_computation | async-start | bytes 5898240 | tf_op jit(solution)/shard_map/all_gather | solution.py:77
  8.7 75.4 %copy-start.4 = (s32[2,8,128]{2,1,0:T(8,128)S(1)}, s32[2,8,128]{2,1,0:T(8,128)}, u32[]{:S(2)}) copy-start(s32[2,8,128]{2,1,0:T(8,128)} %param.12) | copy-start | bytes 24580
  9.5 93.7 %collective-permute-start.1 = (f32[1,5,1,32,128]{4,1,0,3,2:T(8,128)}, f32[1,5,1,32,128]{4,1,0,3,2:T(8,128)S(1)}, u32[]{:S(2)}, u32[]{:S(2)}) collective-permute-start(f32[1,5,1,32,128]{4,1,0,3,2:T(8,128)} %get-tuple-element.11), channel_id=1, source_target_pairs={{0,1},{1,2},{2,3},{3,4},{4,5},{5,6},{6,7},{7,8},{8,9},{9,10},{10,1... | collective-permute-start | bytes 245768 | tf_op jit(solution)/shard_map/ppermute | solution.py:20
  13.3 89.9 %collective-permute-start = (f32[1,5,1,32,128]{4,1,0,3,2:T(8,128)}, f32[1,5,1,32,128]{4,1,0,3,2:T(8,128)S(1)}, u32[]{:S(2)}, u32[]{:S(2)}) collective-permute-start(f32[1,5,1,32,128]{4,1,0,3,2:T(8,128)} %get-tuple-element.12), channel_id=1, source_target_pairs={{1,0},{2,1},{3,2},{4,3},{5,4},{6,5},{7,6},{8,7},{9,8},{10,9},{11,1... | collective-permute-start | bytes 245768 | tf_op jit(solution)/shard_map/ppermute | solution.py:23
  95.8 6.6 %copy-start.3 = (f32[8,32,128]{2,1,0:T(8,128)S(1)}, f32[8,32,128]{2,1,0:T(8,128)}, u32[]{:S(2)}) copy-start(f32[8,32,128]{2,1,0:T(8,128)} %param.9) | copy-start | bytes 393220
  96.9 38.2 %collective-permute-start.2 = (f32[174080]{0:T(1024)S(1)}, f32[174080]{0:T(1024)S(1)}, u32[]{:S(2)}, u32[]{:S(2)}) collective-permute-start(f32[174080]{0:T(1024)S(1)} %pad_maximum_fusion.4), channel_id=1, source_target_pairs={{0,32},{32,0},{1,33},{33,1},{2,34},{34,2},{3,35},{35,3},{4,36},{36... | collective-permute-start | bytes 2088968 | tf_op jit(solution)/shard_map/ppermute | solution.py:96
  103.1 32.4 %copy-start.1 = (f32[1,5,8,32,128]{4,3,2,1,0:T(8,128)S(1)}, f32[1,5,8,32,128]{4,3,2,1,0:T(8,128)}, u32[]{:S(2)}) copy-start(f32[1,5,8,32,128]{4,3,2,1,0:T(8,128)} %param.8) | copy-start | bytes 1966084
  103.2 32.3 %copy-start.2 = (f32[8,32,128]{2,1,0:T(8,128)S(1)}, f32[8,32,128]{2,1,0:T(8,128)}, u32[]{:S(2)}) copy-start(f32[8,32,128]{2,1,0:T(8,128)} %param.10) | copy-start | bytes 393220
Sparse Core Ops, SparseCore 0:
  9.4 72.5 all-gather.2

commit v2 on v1

--- a/solution.py
+++ b/solution.py
@@ -66,37 +66,93 @@
     return base - SECTION_ALPHA * pseudo_step[None, None] * (spatial + time_term)
 
 
-def per_device(state, base, pseudo_step, eddy_visc, jacobians, partner_radial, partner_instance):
+CHUNKS = 2
+
+
+def gathered_along_z(block):
+    ring = lax.axis_size("tz")
+    forward = [(i, (i + 1) % ring) for i in range(ring)]
+    backward = [(i, (i - 1) % ring) for i in range(ring)]
+    held = [block] + [None] * (ring - 1)
+    ahead = block
+    behind = block
+    for step in range(1, (ring + 1) // 2):
+        ahead = lax.ppermute(ahead, "tz", forward)
+        behind = lax.ppermute(behind, "tz", backward)
+        held[ring - step] = ahead
+        held[step] = behind
+    if ring % 2 == 0:
+        middle = block.shape[3] // 2
+        first = lax.ppermute(ahead[:, :, :, :middle], "tz", forward)
+        second = lax.ppermute(behind[:, :, :, middle:], "tz", backward)
+        held[ring // 2] = jnp.concatenate([first, second], axis=3)
+    return jnp.concatenate(held, axis=0)
+
+
+def chunk_exchange(block, pick_radial, pick_instance, own, partner):
     ring = lax.axis_size("tz")
     total_count = ring * Y_PARTS
     z = lax.axis_index("tz")
     y = lax.axis_index("ty")
-    own = Y_PARTS * z + y
-    partner = own + 1 - 2 * y
-    flattened = state.reshape(1, -1)
-    gathered = lax.all_gather(flattened, "tz", axis=0, tiled=True)
-    held_ids = Y_PARTS * jnp.arange(ring, dtype=jnp.int32) + y
+    held = gathered_along_z(block)
+    held_ids = Y_PARTS * ((z + jnp.arange(ring, dtype=jnp.int32)) % ring) + y
     targets = jnp.stack([own, partner])
     weights = time_weights(targets[:, None] - held_ids[None, :], total_count)
-    partial = jnp.dot(weights, gathered, precision=lax.Precision.HIGHEST)
+    partial = jnp.sum(weights.reshape((2, ring) + (1,) * (held.ndim - 1)) * held[None], axis=1)
 
-    held = gathered.reshape((ring,) + state.shape[1:])
     faces = jnp.stack([held[:, :, :, -1, :], held[:, :, :, 0, :]], axis=0)
-    radial_count = partner_radial.shape[2]
-    radial_hot = (partner_radial[..., None] == jnp.arange(radial_count, dtype=jnp.int32)).astype(
+    radial_count = pick_radial.shape[2]
+    radial_hot = (pick_radial[..., None] == jnp.arange(radial_count, dtype=jnp.int32)).astype(
         jnp.float32
     )
     remapped = jnp.einsum("szvir,sikr->szvik", faces, radial_hot, precision=lax.Precision.HIGHEST)
     shifts = (targets - own)[:, None, None, None]
-    sources = (partner_instance[0][None] + shifts) % total_count
+    sources = (pick_instance[None] + shifts) % total_count
     instance_hot = (sources[..., None] == held_ids).astype(jnp.float32)
     picked = jnp.sum(instance_hot[:, :, None] * jnp.moveaxis(remapped, 1, -1)[None], axis=-1)
 
-    message = jnp.concatenate([partial[1], picked[1].reshape(-1)])
+    message = jnp.concatenate([partial[1].reshape(-1), picked[1].reshape(-1)])
+    return partial, picked, message
+
+
+def chunk_settle(partial, picked, message):
     received = lax.ppermute(message, "ty", [(i, Y_PARTS - 1 - i) for i in range(Y_PARTS)])
-    split = partial.shape[1]
-    time_term = (partial[0] + received[:split]).reshape(state.shape)
+    split = partial[0].size
+    time_term = partial[:1] + received[:split].reshape((1,) + partial.shape[1:])
     ghosts = picked[0] + received[split:].reshape(picked.shape[1:])
+    return time_term, ghosts
+
+
+def per_device(state, base, pseudo_step, eddy_visc, jacobians, partner_radial, partner_instance):
+    z = lax.axis_index("tz")
+    y = lax.axis_index("ty")
+    own = Y_PARTS * z + y
+    partner = own + 1 - 2 * y
+    planes = state.shape[2]
+    width = planes // CHUNKS
+    time_parts = []
+    ghost_parts = []
+    message = None
+    for chunk in range(CHUNKS):
+        window = slice(chunk * width, (chunk + 1) * width)
+        block = state[:, :, window]
+        if message is not None:
+            message, block = lax.optimization_barrier((message, block))
+            time_part, ghost_part = chunk_settle(partial, picked, message)
+            time_parts.append(time_part)
+            ghost_parts.append(ghost_part)
+        partial, picked, message = chunk_exchange(
+            block,
+            partner_radial[:, window],
+            partner_instance[0][:, window],
+            own,
+            partner,
+        )
+    time_part, ghost_part = chunk_settle(partial, picked, message)
+    time_parts.append(time_part)
+    ghost_parts.append(ghost_part)
+    time_term = jnp.concatenate(time_parts, axis=2)
+    ghosts = jnp.concatenate(ghost_parts, axis=2)
     low_ghost = rotate_velocity(ghosts[0][None], -1.0)
     high_ghost = rotate_velocity(ghosts[1][None], 1.0)
 

time: 148 us -> 167 us (1.13)
  the two profiles are of different devices: /device:TPU:17 before, /device:TPU:6 now
where the time goes in v2:
time: 167 us; the launch traced here: 164 us
  starting transfers between devices  80.8 us (48%)
  local copies, waits for them, and re-layouts  33.9 us (20%)
  waiting for transfers between devices  33 us (20%)
  other arithmetic  8.48 us (5%)
  matrix products  6.83 us (4%)
    ppermute x6, starting transfers between devices, gathered_along_z(): behind = lax.ppermute(behind, 'tz', backward)  34.7 us
    concatenate x4, local copies, waits for them, and re-layouts, gathered_along_z(): return jnp.concatenate(held, axis=0)  19.4 us
    ppermute x6, waiting for transfers between devices, gathered_along_z(): ahead = lax.ppermute(ahead, 'tz', forward)  17 us
    ppermute x6, starting transfers between devices, gathered_along_z(): ahead = lax.ppermute(ahead, 'tz', forward)  13.8 us
    ppermute x2, waiting for transfers between devices, chunk_settle(): lax.ppermute(message, 'ty', [(i, Y_PARTS - 1 - i) for i in range(Y_PARTS)])  13.3 us
    ppermute x2, starting transfers between devices, gathered_along_z(): second = lax.ppermute(behind[:, :, :, middle:], 'tz', backward)  10.3 us
    ppermute x2, starting transfers between devices, chunk_settle(): lax.ppermute(message, 'ty', [(i, Y_PARTS - 1 - i) for i in range(Y_PARTS)])  9.92 us
    ppermute x1, starting transfers between devices, extended_2(): lax.ppermute(lax.slice_in_dim(block, 0, width, axis=dim), axis, backward)  6.34 us
  transfers between devices with their start and end apart: 20, of which 8 were waited for; matrix products, arithmetic and copies ran while one was open for 15% of the time, Pallas kernels for 0%

profile of v2, /device:TPU:6, one launch (start us, length us, event | category | flops | bytes accessed | tf_op | source)
XLA Modules:
  0.0 163.8 jit_solution(8074658298514013100)
XLA Ops:
  1.5 4.3 %collective-permute-start.5 = (f32[1,5,4,32,128]{4,0,1,2,3:T(1,128)S(1)}, f32[1,5,4,32,128]{4,0,1,2,3:T(1,128)S(1)}, u32[]{:S(2)}, u32[]{:S(2)}) collective-permute-start(f32[1,5,4,32,128]{4,0,1,2,3:T(1,128)S(1)} %copy.111), channel_id=1, source_target_pairs={{0,64},{64,128},{128,192},{192,256},{256,320},{320,384},{384,448},... | collective-permute-start | bytes 983048 | tf_op jit(solution)/shard_map/ppermute | solution.py:80
  5.8 8.6 %collective-permute-start.2 = (f32[1,5,4,32,128]{4,0,1,2,3:T(1,128)S(1)}, f32[1,5,4,32,128]{4,0,1,2,3:T(1,128)S(1)}, u32[]{:S(2)}, u32[]{:S(2)}) collective-permute-start(f32[1,5,4,32,128]{4,0,1,2,3:T(1,128)S(1)} %copy.111), channel_id=1, source_target_pairs={{0,448},{64,0},{128,64},{192,128},{256,192},{320,256},{384,320},{4... | collective-permute-start | bytes 983048 | tf_op jit(solution)/shard_map/ppermute | solution.py:81
  16.1 4.0 %collective-permute-done.5 = f32[1,5,4,32,128]{4,0,1,2,3:T(1,128)S(1)} collective-permute-done((f32[1,5,4,32,128]{4,0,1,2,3:T(1,128)S(1)}, f32[1,5,4,32,128]{4,0,1,2,3:T(1,128)S(1)}, u32[]{:S(2)}, u32[]{:S(2)}) %collective-permute-start.5) | collective-permute-done | bytes 327712 | tf_op jit(solution)/shard_map/ppermute | solution.py:80
  22.1 5.1 %collective-permute-start.3 = (f32[1,5,4,32,128]{4,0,1,2,3:T(1,128)S(1)}, f32[1,5,4,32,128]{4,0,1,2,3:T(1,128)S(1)}, u32[]{:S(2)}, u32[]{:S(2)}) collective-permute-start(f32[1,5,4,32,128]{4,0,1,2,3:T(1,128)S(1)} %collective-permute-done.2), channel_id=1, source_target_pairs={{0,448},{64,0},{128,64},{192,128},{256,192},{320,256},{384,320},{4... | collective-permute-start | bytes 983048 | tf_op jit(solution)/shard_map/ppermute | solution.py:81
  27.4 4.7 %collective-permute-done.6 = f32[1,5,4,32,128]{4,0,1,2,3:T(1,128)S(1)} collective-permute-done((f32[1,5,4,32,128]{4,0,1,2,3:T(1,128)S(1)}, f32[1,5,4,32,128]{4,0,1,2,3:T(1,128)S(1)}, u32[]{:S(2)}, u32[]{:S(2)}) %collective-permute-start.6) | collective-permute-done | bytes 327712 | tf_op jit(solution)/shard_map/ppermute | solution.py:80
  34.1 5.1 %collective-permute-start.4 = (f32[1,5,4,32,128]{4,0,1,2,3:T(1,128)S(1)}, f32[1,5,4,32,128]{4,0,1,2,3:T(1,128)S(1)}, u32[]{:S(2)}, u32[]{:S(2)}) collective-permute-start(f32[1,5,4,32,128]{4,0,1,2,3:T(1,128)S(1)} %collective-permute-done.3), channel_id=1, source_target_pairs={{0,448},{64,0},{128,64},{192,128},{256,192},{320,256},{384,320},{4... | collective-permute-start | bytes 983048 | tf_op jit(solution)/shard_map/ppermute | solution.py:81
  39.3 3.9 %collective-permute-done.7 = f32[1,5,4,32,128]{4,0,1,2,3:T(1,128)S(1)} collective-permute-done((f32[1,5,4,32,128]{4,0,1,2,3:T(1,128)S(1)}, f32[1,5,4,32,128]{4,0,1,2,3:T(1,128)S(1)}, u32[]{:S(2)}, u32[]{:S(2)}) %collective-permute-start.7) | collective-permute-done | bytes 327712 | tf_op jit(solution)/shard_map/ppermute | solution.py:80
  44.0 1.9 %collective-permute-start.8 = (f32[1,5,4,16,128]{4,0,1,2,3:T(1,128)S(1)}, f32[1,5,4,16,128]{4,0,1,2,3:T(1,128)S(1)}, u32[]{:S(2)}, u32[]{:S(2)}) collective-permute-start(f32[1,5,4,16,128]{4,0,1,2,3:T(1,128)S(1)} %slice.212), channel_id=1, source_target_pairs={{0,64},{64,128},{128,192},{192,256},{256,320},{320,384},{384,448},... | collective-permute-start | bytes 491528 | tf_op jit(solution)/shard_map/ppermute | solution.py:86
  46.7 5.1 %collective-permute-start.9 = (f32[1,5,4,16,128]{4,0,1,2,3:T(1,128)S(1)}, f32[1,5,4,16,128]{4,0,1,2,3:T(1,128)S(1)}, u32[]{:S(2)}, u32[]{:S(2)}) collective-permute-start(f32[1,5,4,16,128]{4,0,1,2,3:T(1,128)S(1)} %slice.213), channel_id=1, source_target_pairs={{0,448},{64,0},{128,64},{192,128},{256,192},{320,256},{384,320},{4... | collective-permute-start | bytes 491528 | tf_op jit(solution)/shard_map/ppermute | solution.py:87
  52.4 2.3 %collective-permute-done.9 = f32[1,5,4,16,128]{4,0,1,2,3:T(1,128)S(1)} collective-permute-done((f32[1,5,4,16,128]{4,0,1,2,3:T(1,128)S(1)}, f32[1,5,4,16,128]{4,0,1,2,3:T(1,128)S(1)}, u32[]{:S(2)}, u32[]{:S(2)}) %collective-permute-start.9) | collective-permute-done | bytes 163872 | tf_op jit(solution)/shard_map/ppermute | solution.py:87
  55.7 6.7 %concatenate.77 = f32[8,5,4,32,128]{4,0,1,2,3:T(8,128)S(1)} concatenate(f32[1,5,4,32,128]{4,0,1,2,3:T(1,128)S(1)} %copy.111, f32[1,5,4,32,128]{4,0,1,2,3:T(1,128)} %copy-done.11, f32[1,5,4,32,128]{4,0,1,2,3:T(1,128)} %copy-done.17, f32[1,5,4,32,128]{4,0,1,2,3:T(1,128)} %copy-done.8, f32[1,5,4,32,128]{4,0,1,2,3:T(1,128)} %pad_maximum_fusion.6, f32[1,5,4,32,128]{4,0,1,2,3:T(1,128)} %copy-done.6, ...), dimensions={0} | concatenate | bytes 5242880 | tf_op jit(solution)/shard_map/concatenate | solution.py:89
  68.7 5.6 %collective-permute-start.11 = (f32[1,5,4,32,128]{4,0,1,2,3:T(1,128)S(1)}, f32[1,5,4,32,128]{4,0,1,2,3:T(1,128)S(1)}, u32[]{:S(2)}, u32[]{:S(2)}) collective-permute-start(f32[1,5,4,32,128]{4,0,1,2,3:T(1,128)S(1)} %copy.112), channel_id=1, source_target_pairs={{0,448},{64,0},{128,64},{192,128},{256,192},{320,256},{384,320},{4... | collective-permute-start | bytes 983048 | tf_op jit(solution)/shard_map/ppermute | solution.py:81
  74.3 3.1 %collective-permute-done.14 = f32[1,5,4,32,128]{4,0,1,2,3:T(1,128)S(1)} collective-permute-done((f32[1,5,4,32,128]{4,0,1,2,3:T(1,128)S(1)}, f32[1,5,4,32,128]{4,0,1,2,3:T(1,128)S(1)}, u32[]{:S(2)}, u32[]{:S(2)}) %collective-permute-start.14) | collective-permute-done | bytes 327712 | tf_op jit(solution)/shard_map/ppermute | solution.py:80
  79.3 5.1 %collective-permute-start.12 = (f32[1,5,4,32,128]{4,0,1,2,3:T(1,128)S(1)}, f32[1,5,4,32,128]{4,0,1,2,3:T(1,128)S(1)}, u32[]{:S(2)}, u32[]{:S(2)}) collective-permute-start(f32[1,5,4,32,128]{4,0,1,2,3:T(1,128)S(1)} %collective-permute-done.11), channel_id=1, source_target_pairs={{0,448},{64,0},{128,64},{192,128},{256,192},{320,256},{384,320},{4... | collective-permute-start | bytes 983048 | tf_op jit(solution)/shard_map/ppermute | solution.py:81
  87.5 6.3 %collective-permute-start = (f32[1,5,1,32,128]{4,1,0,3,2:T(8,128)}, f32[1,5,1,32,128]{4,1,0,3,2:T(8,128)}, u32[]{:S(2)}, u32[]{:S(2)}) collective-permute-start(f32[1,5,1,32,128]{4,1,0,3,2:T(8,128)} %get-tuple-element.16), channel_id=1, source_target_pairs={{1,0},{2,1},{3,2},{4,3},{5,4},{6,5},{7,6},{8,7},{9,8},{10,9},{11,1... | collective-permute-start | bytes 245768 | tf_op jit(solution)/shard_map/ppermute | solution.py:23
  93.9 1.9 %collective-permute-start.16 = (f32[1,5,4,32,128]{4,0,1,2,3:T(1,128)S(1)}, f32[1,5,4,32,128]{4,0,1,2,3:T(1,128)S(1)}, u32[]{:S(2)}, u32[]{:S(2)}) collective-permute-start(f32[1,5,4,32,128]{4,0,1,2,3:T(1,128)S(1)} %collective-permute-done.15), channel_id=1, source_target_pairs={{0,64},{64,128},{128,192},{192,256},{256,320},{320,384},{384,448},... | collective-permute-start | bytes 983048 | tf_op jit(solution)/shard_map/ppermute | solution.py:80
  95.9 5.1 %collective-permute-start.13 = (f32[1,5,4,32,128]{4,0,1,2,3:T(1,128)S(1)}, f32[1,5,4,32,128]{4,0,1,2,3:T(1,128)S(1)}, u32[]{:S(2)}, u32[]{:S(2)}) collective-permute-start(f32[1,5,4,32,128]{4,0,1,2,3:T(1,128)S(1)} %collective-permute-done.12), channel_id=1, source_target_pairs={{0,448},{64,0},{128,64},{192,128},{256,192},{320,256},{384,320},{4... | collective-permute-start | bytes 983048 | tf_op jit(solution)/shard_map/ppermute | solution.py:81
  107.6 5.1 %collective-permute-start.18 = (f32[1,5,4,16,128]{4,0,1,2,3:T(1,128)S(1)}, f32[1,5,4,16,128]{4,0,1,2,3:T(1,128)S(1)}, u32[]{:S(2)}, u32[]{:S(2)}) collective-permute-start(f32[1,5,4,16,128]{4,0,1,2,3:T(1,128)S(1)} %slice.222), channel_id=1, source_target_pairs={{0,448},{64,0},{128,64},{192,128},{256,192},{320,256},{384,320},{4... | collective-permute-start | bytes 491528 | tf_op jit(solution)/shard_map/ppermute | solution.py:87
  114.8 7.7 %collective-permute-start.10 = (f32[87040]{0:T(1024)}, f32[87040]{0:T(1024)}, u32[]{:S(2)}, u32[]{:S(2)}) collective-permute-start(f32[87040]{0:T(1024)} %pad_maximum_fusion.4), channel_id=1, source_target_pairs={{0,32},{32,0},{1,33},{33,1},{2,34},{34,2},{3,35},{35,3},{4,36},{36... | collective-permute-start | bytes 1044488 | tf_op jit(solution)/shard_map/ppermute | solution.py:119
  123.6 7.9 %concatenate.80 = f32[8,5,4,32,128]{4,0,1,2,3:T(8,128)} concatenate(f32[1,5,4,32,128]{4,0,1,2,3:T(1,128)S(1)} %copy.112, f32[1,5,4,32,128]{4,0,1,2,3:T(1,128)} %copy-done.13, f32[1,5,4,32,128]{4,0,1,2,3:T(1,128)} %copy-done.16, f32[1,5,4,32,128]{4,0,1,2,3:T(1,128)} %copy-done.9, f32[1,5,4,32,128]{4,0,1,2,3:T(1,128)} %pad_maximum_fusion.7, f32[1,5,4,32,128]{4,0,1,2,3:T(1,128)} %copy-done.7, ...), dimensions={0} | concatenate | bytes 5242880 | tf_op jit(solution)/shard_map/concatenate | solution.py:89
  132.4 3.3 %copy.91 = f32[8,5,4,32,128]{4,3,2,1,0:T(8,128)S(1)} copy(f32[8,5,4,32,128]{4,0,1,2,3:T(8,128)} %concatenate.80) | data formatting | bytes 5242880 | tf_op jit(solution)/shard_map/concatenate | solution.py:89
  137.2 2.2 %collective-permute-start.19 = (f32[87040]{0:T(1024)S(1)}, f32[87040]{0:T(1024)S(1)}, u32[]{:S(2)}, u32[]{:S(2)}) collective-permute-start(f32[87040]{0:T(1024)S(1)} %pad_maximum_fusion.5), channel_id=1, source_target_pairs={{0,32},{32,0},{1,33},{33,1},{2,34},{34,2},{3,35},{35,3},{4,36},{36... | collective-permute-start | bytes 1044488 | tf_op jit(solution)/shard_map/ppermute | solution.py:119
  142.5 13.3 %collective-permute-done.19 = f32[87040]{0:T(1024)S(1)} collective-permute-done((f32[87040]{0:T(1024)S(1)}, f32[87040]{0:T(1024)S(1)}, u32[]{:S(2)}, u32[]{:S(2)}) %collective-permute-start.19) | collective-permute-done | bytes 348192 | tf_op jit(solution)/shard_map/ppermute | solution.py:119
  157.4 5.4 %fusion.10 = f32[1,5,8,32,128]{4,1,0,3,2:T(8,128)S(1)} fusion(f32[1,5,8,32,128]{4,1,0,3,2:T(8,128)S(1)} %copy-done.5, f32[1,5,8,32,128]{4,1,0,3,2:T(8,128)S(1)} %fusion.11, f32[1,5,8,32,128]{4,1,0,3,2:T(8,128)S(1)} %fusion.12, f32[1,5,4,32,128]{4,1,0,3,2:T(8,128)S(1)} %get-tuple-element.44, f32[1,5,4,32,128]{4,1,0,3,2:T(8,128)S(1)} %get-tuple-element.45, ...), kind=kOutput, calls=%fused_computation.13 | convolution fusion | flops 33751040 | bytes 7625004 | tf_op jit(solution)/shard_map/dab,dnbijk->naijk/dot_general | solution.py:63
  (124 shorter events, 39.0 us)
Async XLA Ops:
  0.0 157.0 %copy-start = (f32[3,5,5]{2,0,1:T(4,128)S(1)}, f32[3,5,5]{2,0,1:T(4,128)}, u32[]{:S(2)}) copy-start(f32[3,5,5]{2,0,1:T(4,128)} %param.11) | copy-start | bytes 904
  1.5 18.6 %collective-permute-start.5 = (f32[1,5,4,32,128]{4,0,1,2,3:T(1,128)S(1)}, f32[1,5,4,32,128]{4,0,1,2,3:T(1,128)S(1)}, u32[]{:S(2)}, u32[]{:S(2)}) collective-permute-start(f32[1,5,4,32,128]{4,0,1,2,3:T(1,128)S(1)} %copy.111), channel_id=1, source_target_pairs={{0,64},{64,128},{128,192},{192,256},{256,320},{320,384},{384,448},... | collective-permute-start | bytes 983048 | tf_op jit(solution)/shard_map/ppermute | solution.py:80
  5.8 16.3 %collective-permute-start.2 = (f32[1,5,4,32,128]{4,0,1,2,3:T(1,128)S(1)}, f32[1,5,4,32,128]{4,0,1,2,3:T(1,128)S(1)}, u32[]{:S(2)}, u32[]{:S(2)}) collective-permute-start(f32[1,5,4,32,128]{4,0,1,2,3:T(1,128)S(1)} %copy.111), channel_id=1, source_target_pairs={{0,448},{64,0},{128,64},{192,128},{256,192},{320,256},{384,320},{4... | collective-permute-start | bytes 983048 | tf_op jit(solution)/shard_map/ppermute | solution.py:81
  20.2 34.5 %copy-start.10 = (f32[1,5,4,32,128]{4,0,1,2,3:T(1,128)}, f32[1,5,4,32,128]{4,0,1,2,3:T(1,128)S(1)}, u32[]{:S(2)}) copy-start(f32[1,5,4,32,128]{4,0,1,2,3:T(1,128)S(1)} %collective-permute-done.5) | copy-start | bytes 983044
  20.2 12.0 %collective-permute-start.6 = (f32[1,5,4,32,128]{4,0,1,2,3:T(1,128)S(1)}, f32[1,5,4,32,128]{4,0,1,2,3:T(1,128)S(1)}, u32[]{:S(2)}, u32[]{:S(2)}) collective-permute-start(f32[1,5,4,32,128]{4,0,1,2,3:T(1,128)S(1)} %collective-permute-done.5), channel_id=1, source_target_pairs={{0,64},{64,128},{128,192},{192,256},{256,320},{320,384},{384,448},... | collective-permute-start | bytes 983048 | tf_op jit(solution)/shard_map/ppermute | solution.py:80
  22.1 32.6 %copy-start.11 = (f32[1,5,4,32,128]{4,0,1,2,3:T(1,128)}, f32[1,5,4,32,128]{4,0,1,2,3:T(1,128)S(1)}, u32[]{:S(2)}) copy-start(f32[1,5,4,32,128]{4,0,1,2,3:T(1,128)S(1)} %collective-permute-done.2) | copy-start | bytes 983044
  22.1 12.0 %collective-permute-start.3 = (f32[1,5,4,32,128]{4,0,1,2,3:T(1,128)S(1)}, f32[1,5,4,32,128]{4,0,1,2,3:T(1,128)S(1)}, u32[]{:S(2)}, u32[]{:S(2)}) collective-permute-start(f32[1,5,4,32,128]{4,0,1,2,3:T(1,128)S(1)} %collective-permute-done.2), channel_id=1, source_target_pairs={{0,448},{64,0},{128,64},{192,128},{256,192},{320,256},{384,320},{4... | collective-permute-start | bytes 983048 | tf_op jit(solution)/shard_map/ppermute | solution.py:81
  32.2 11.1 %collective-permute-start.7 = (f32[1,5,4,32,128]{4,0,1,2,3:T(1,128)S(1)}, f32[1,5,4,32,128]{4,0,1,2,3:T(1,128)S(1)}, u32[]{:S(2)}, u32[]{:S(2)}) collective-permute-start(f32[1,5,4,32,128]{4,0,1,2,3:T(1,128)S(1)} %collective-permute-done.6), channel_id=1, source_target_pairs={{0,64},{64,128},{128,192},{192,256},{256,320},{320,384},{384,448},... | collective-permute-start | bytes 983048 | tf_op jit(solution)/shard_map/ppermute | solution.py:80
  34.1 11.8 %collective-permute-start.4 = (f32[1,5,4,32,128]{4,0,1,2,3:T(1,128)S(1)}, f32[1,5,4,32,128]{4,0,1,2,3:T(1,128)S(1)}, u32[]{:S(2)}, u32[]{:S(2)}) collective-permute-start(f32[1,5,4,32,128]{4,0,1,2,3:T(1,128)S(1)} %collective-permute-done.3), channel_id=1, source_target_pairs={{0,448},{64,0},{128,64},{192,128},{256,192},{320,256},{384,320},{4... | collective-permute-start | bytes 983048 | tf_op jit(solution)/shard_map/ppermute | solution.py:81
  44.0 8.4 %collective-permute-start.8 = (f32[1,5,4,16,128]{4,0,1,2,3:T(1,128)S(1)}, f32[1,5,4,16,128]{4,0,1,2,3:T(1,128)S(1)}, u32[]{:S(2)}, u32[]{:S(2)}) collective-permute-start(f32[1,5,4,16,128]{4,0,1,2,3:T(1,128)S(1)} %slice.212), channel_id=1, source_target_pairs={{0,64},{64,128},{128,192},{192,256},{256,320},{320,384},{384,448},... | collective-permute-start | bytes 491528 | tf_op jit(solution)/shard_map/ppermute | solution.py:86
  46.7 8.0 %collective-permute-start.9 = (f32[1,5,4,16,128]{4,0,1,2,3:T(1,128)S(1)}, f32[1,5,4,16,128]{4,0,1,2,3:T(1,128)S(1)}, u32[]{:S(2)}, u32[]{:S(2)}) collective-permute-start(f32[1,5,4,16,128]{4,0,1,2,3:T(1,128)S(1)} %slice.213), channel_id=1, source_target_pairs={{0,448},{64,0},{128,64},{192,128},{256,192},{320,256},{384,320},{4... | collective-permute-start | bytes 491528 | tf_op jit(solution)/shard_map/ppermute | solution.py:87
  66.0 35.0 %copy-start.18 = (f32[2,2,5,4,128]{4,3,2,1,0:T(4,128)}, f32[2,2,5,4,128]{4,3,2,1,0:T(4,128)S(1)}, u32[]{:S(2)}) copy-start(f32[2,2,5,4,128]{4,3,2,1,0:T(4,128)S(1)} %multiply_reduce_fusion.3) | copy-start | bytes 122884
  66.8 10.6 %collective-permute-start.14 = (f32[1,5,4,32,128]{4,0,1,2,3:T(1,128)S(1)}, f32[1,5,4,32,128]{4,0,1,2,3:T(1,128)S(1)}, u32[]{:S(2)}, u32[]{:S(2)}) collective-permute-start(f32[1,5,4,32,128]{4,0,1,2,3:T(1,128)S(1)} %copy.112), channel_id=1, source_target_pairs={{0,64},{64,128},{128,192},{192,256},{256,320},{320,384},{384,448},... | collective-permute-start | bytes 983048 | tf_op jit(solution)/shard_map/ppermute | solution.py:80
  68.7 10.6 %collective-permute-start.11 = (f32[1,5,4,32,128]{4,0,1,2,3:T(1,128)S(1)}, f32[1,5,4,32,128]{4,0,1,2,3:T(1,128)S(1)}, u32[]{:S(2)}, u32[]{:S(2)}) collective-permute-start(f32[1,5,4,32,128]{4,0,1,2,3:T(1,128)S(1)} %copy.112), channel_id=1, source_target_pairs={{0,448},{64,0},{128,64},{192,128},{256,192},{320,256},{384,320},{4... | collective-permute-start | bytes 983048 | tf_op jit(solution)/shard_map/ppermute | solution.py:81
  77.4 16.5 %collective-permute-start.15 = (f32[1,5,4,32,128]{4,0,1,2,3:T(1,128)S(1)}, f32[1,5,4,32,128]{4,0,1,2,3:T(1,128)S(1)}, u32[]{:S(2)}, u32[]{:S(2)}) collective-permute-start(f32[1,5,4,32,128]{4,0,1,2,3:T(1,128)S(1)} %collective-permute-done.14), channel_id=1, source_target_pairs={{0,64},{64,128},{128,192},{192,256},{256,320},{320,384},{384,448},... | collective-permute-start | bytes 983048 | tf_op jit(solution)/shard_map/ppermute | solution.py:80
  79.3 16.5 %collective-permute-start.12 = (f32[1,5,4,32,128]{4,0,1,2,3:T(1,128)S(1)}, f32[1,5,4,32,128]{4,0,1,2,3:T(1,128)S(1)}, u32[]{:S(2)}, u32[]{:S(2)}) collective-permute-start(f32[1,5,4,32,128]{4,0,1,2,3:T(1,128)S(1)} %collective-permute-done.11), channel_id=1, source_target_pairs={{0,448},{64,0},{128,64},{192,128},{256,192},{320,256},{384,320},{4... | collective-permute-start | bytes 983048 | tf_op jit(solution)/shard_map/ppermute | solution.py:81
  85.6 53.8 %collective-permute-start.1 = (f32[1,5,1,32,128]{4,1,0,3,2:T(8,128)}, f32[1,5,1,32,128]{4,1,0,3,2:T(8,128)}, u32[]{:S(2)}, u32[]{:S(2)}) collective-permute-start(f32[1,5,1,32,128]{4,1,0,3,2:T(8,128)} %get-tuple-element.15), channel_id=1, source_target_pairs={{0,1},{1,2},{2,3},{3,4},{4,5},{5,6},{6,7},{7,8},{8,9},{9,10},{10,1... | collective-permute-start | bytes 245768 | tf_op jit(solution)/shard_map/ppermute | solution.py:20
  87.5 51.9 %collective-permute-start = (f32[1,5,1,32,128]{4,1,0,3,2:T(8,128)}, f32[1,5,1,32,128]{4,1,0,3,2:T(8,128)}, u32[]{:S(2)}, u32[]{:S(2)}) collective-permute-start(f32[1,5,1,32,128]{4,1,0,3,2:T(8,128)} %get-tuple-element.16), channel_id=1, source_target_pairs={{1,0},{2,1},{3,2},{4,3},{5,4},{6,5},{7,6},{8,7},{9,8},{10,9},{11,1... | collective-permute-start | bytes 245768 | tf_op jit(solution)/shard_map/ppermute | solution.py:23
  93.9 10.2 %collective-permute-start.16 = (f32[1,5,4,32,128]{4,0,1,2,3:T(1,128)S(1)}, f32[1,5,4,32,128]{4,0,1,2,3:T(1,128)S(1)}, u32[]{:S(2)}, u32[]{:S(2)}) collective-permute-start(f32[1,5,4,32,128]{4,0,1,2,3:T(1,128)S(1)} %collective-permute-done.15), channel_id=1, source_target_pairs={{0,64},{64,128},{128,192},{192,256},{256,320},{320,384},{384,448},... | collective-permute-start | bytes 983048 | tf_op jit(solution)/shard_map/ppermute | solution.py:80
  95.9 10.9 %collective-permute-start.13 = (f32[1,5,4,32,128]{4,0,1,2,3:T(1,128)S(1)}, f32[1,5,4,32,128]{4,0,1,2,3:T(1,128)S(1)}, u32[]{:S(2)}, u32[]{:S(2)}) collective-permute-start(f32[1,5,4,32,128]{4,0,1,2,3:T(1,128)S(1)} %collective-permute-done.12), channel_id=1, source_target_pairs={{0,448},{64,0},{128,64},{192,128},{256,192},{320,256},{384,320},{4... | collective-permute-start | bytes 983048 | tf_op jit(solution)/shard_map/ppermute | solution.py:81
  104.9 17.6 %collective-permute-start.17 = (f32[1,5,4,16,128]{4,0,1,2,3:T(1,128)S(1)}, f32[1,5,4,16,128]{4,0,1,2,3:T(1,128)S(1)}, u32[]{:S(2)}, u32[]{:S(2)}) collective-permute-start(f32[1,5,4,16,128]{4,0,1,2,3:T(1,128)S(1)} %slice.221), channel_id=1, source_target_pairs={{0,64},{64,128},{128,192},{192,256},{256,320},{320,384},{384,448},... | collective-permute-start | bytes 491528 | tf_op jit(solution)/shard_map/ppermute | solution.py:86
  107.6 14.9 %collective-permute-start.18 = (f32[1,5,4,16,128]{4,0,1,2,3:T(1,128)S(1)}, f32[1,5,4,16,128]{4,0,1,2,3:T(1,128)S(1)}, u32[]{:S(2)}, u32[]{:S(2)}) collective-permute-start(f32[1,5,4,16,128]{4,0,1,2,3:T(1,128)S(1)} %slice.222), channel_id=1, source_target_pairs={{0,448},{64,0},{128,64},{192,128},{256,192},{320,256},{384,320},{4... | collective-permute-start | bytes 491528 | tf_op jit(solution)/shard_map/ppermute | solution.py:87
  114.8 25.8 %collective-permute-start.10 = (f32[87040]{0:T(1024)}, f32[87040]{0:T(1024)}, u32[]{:S(2)}, u32[]{:S(2)}) collective-permute-start(f32[87040]{0:T(1024)} %pad_maximum_fusion.4), channel_id=1, source_target_pairs={{0,32},{32,0},{1,33},{33,1},{2,34},{34,2},{3,35},{35,3},{4,36},{36... | collective-permute-start | bytes 1044488 | tf_op jit(solution)/shard_map/ppermute | solution.py:119
  137.2 18.6 %collective-permute-start.19 = (f32[87040]{0:T(1024)S(1)}, f32[87040]{0:T(1024)S(1)}, u32[]{:S(2)}, u32[]{:S(2)}) collective-permute-start(f32[87040]{0:T(1024)S(1)} %pad_maximum_fusion.5), channel_id=1, source_target_pairs={{0,32},{32,0},{1,33},{33,1},{2,34},{34,2},{3,35},{35,3},{4,36},{36... | collective-permute-start | bytes 1044488 | tf_op jit(solution)/shard_map/ppermute | solution.py:119
  (22 other events, 199.7 us)

commit v3 on v1

--- a/solution.py
+++ b/solution.py
@@ -73,14 +73,25 @@
     y = lax.axis_index("ty")
     own = Y_PARTS * z + y
     partner = own + 1 - 2 * y
-    flattened = state.reshape(1, -1)
-    gathered = lax.all_gather(flattened, "tz", axis=0, tiled=True)
-    held_ids = Y_PARTS * jnp.arange(ring, dtype=jnp.int32) + y
+    swap = [(i, Y_PARTS - 1 - i) for i in range(Y_PARTS)]
+    ring_ids = Y_PARTS * jnp.arange(ring, dtype=jnp.int32) + y
+    pitch = state.shape[3]
+    edge = pitch // 4
+
+    inner = state[:, :, :, edge : pitch - edge]
+    other = lax.ppermute(inner, "ty", swap)
+    expand = (ring,) + (1,) * (inner.ndim - 1)
+    own_weights = time_weights(ring_ids - own, total_count).reshape(expand)
+    partner_weights = time_weights(ring_ids - partner, total_count).reshape(expand)
+    contributions = own_weights * inner + partner_weights * other
+    inner_term = lax.psum_scatter(contributions, "tz", scatter_dimension=0, tiled=True)
+
+    outer = jnp.concatenate([state[:, :, :, :edge], state[:, :, :, pitch - edge :]], axis=3)
+    held = lax.all_gather(outer, "tz", axis=0, tiled=True)
     targets = jnp.stack([own, partner])
-    weights = time_weights(targets[:, None] - held_ids[None, :], total_count)
-    partial = jnp.dot(weights, gathered, precision=lax.Precision.HIGHEST)
+    weights = time_weights(targets[:, None] - ring_ids[None, :], total_count)
+    partial = jnp.sum(weights.reshape((2, ring) + (1,) * (held.ndim - 1)) * held[None], axis=1)
 
-    held = gathered.reshape((ring,) + state.shape[1:])
     faces = jnp.stack([held[:, :, :, -1, :], held[:, :, :, 0, :]], axis=0)
     radial_count = partner_radial.shape[2]
     radial_hot = (partner_radial[..., None] == jnp.arange(radial_count, dtype=jnp.int32)).astype(
@@ -89,14 +100,17 @@
     remapped = jnp.einsum("szvir,sikr->szvik", faces, radial_hot, precision=lax.Precision.HIGHEST)
     shifts = (targets - own)[:, None, None, None]
     sources = (partner_instance[0][None] + shifts) % total_count
-    instance_hot = (sources[..., None] == held_ids).astype(jnp.float32)
+    instance_hot = (sources[..., None] == ring_ids).astype(jnp.float32)
     picked = jnp.sum(instance_hot[:, :, None] * jnp.moveaxis(remapped, 1, -1)[None], axis=-1)
 
-    message = jnp.concatenate([partial[1], picked[1].reshape(-1)])
-    received = lax.ppermute(message, "ty", [(i, Y_PARTS - 1 - i) for i in range(Y_PARTS)])
-    split = partial.shape[1]
-    time_term = (partial[0] + received[:split]).reshape(state.shape)
+    message = jnp.concatenate([partial[1].reshape(-1), picked[1].reshape(-1)])
+    received = lax.ppermute(message, "ty", swap)
+    split = partial[0].size
+    outer_term = partial[:1] + received[:split].reshape((1,) + partial.shape[1:])
     ghosts = picked[0] + received[split:].reshape(picked.shape[1:])
+    time_term = jnp.concatenate(
+        [outer_term[:, :, :, :edge], inner_term, outer_term[:, :, :, edge:]], axis=3
+    )
     low_ghost = rotate_velocity(ghosts[0][None], -1.0)
     high_ghost = rotate_velocity(ghosts[1][None], 1.0)
 

time: 148 us -> 124 us (0.84)
  the two profiles are of different devices: /device:TPU:17 before, /device:TPU:6 now
where the time goes in v3:
time: 124 us
  waiting for transfers between devices  59.3 us (48%)
  starting transfers between devices  23.4 us (19%)
  between operations  13.7 us (11%)
  local copies, waits for them, and re-layouts  10.4 us (8%)
  matrix products  8.89 us (7%)
  other arithmetic  8.45 us (7%)
    all_gather x1, waiting for transfers between devices, per_device(): held = lax.all_gather(outer, 'tz', axis=0, tiled=True)  26.7 us
    reduce_scatter x1, waiting for transfers between devices, per_device(): lax.psum_scatter(contributions, 'tz', scatter_dimension=0, tiled=True)  23.5 us
    ppermute x1, starting transfers between devices, per_device(): other = lax.ppermute(inner, 'ty', swap)  7.73 us
    ppermute x1, starting transfers between devices, per_device(): received = lax.ppermute(message, 'ty', swap)  7.39 us
    ppermute x1, waiting for transfers between devices, per_device(): received = lax.ppermute(message, 'ty', swap)  6.9 us
    dot_general x1, matrix products, section_update(): jnp.einsum('dab,dnbijk->naijk', jacobians, diffs, precision=lax.Precision...  6.76 us
    ppermute x1, starting transfers between devices, extended_2(): lax.ppermute(lax.slice_in_dim(block, 0, width, axis=dim), axis, backward)  6.34 us
  transfers between devices with their start and end apart: 6, of which 4 were waited for; matrix products, arithmetic and copies ran while one was open for 14% of the time, Pallas kernels for 0%

profile of v3, /device:TPU:6, one launch (start us, length us, event | category | flops | bytes accessed | tf_op | source)
XLA Modules:
  0.0 124.1 jit_solution(13513811073420872048)
XLA Ops:
  6.5 1.1 fusion.38
  7.6 0.7 pad_maximum_fusion.5
  8.5 1.0 slice_bitcast_fusion.1
  9.5 7.7 %collective-permute-start.3 = (f32[1,5,8,16,128]{4,3,2,1,0:T(8,128)S(1)}, f32[1,5,8,16,128]{4,3,2,1,0:T(8,128)S(1)}, u32[]{:S(2)}, u32[]{:S(2)}) collective-permute-start(f32[1,5,8,16,128]{4,3,2,1,0:T(8,128)S(1)} %get-tuple-element.16), channel_id=1, source_target_pairs={{0,32},{32,0},{1,33},{33,1},{2,34},{34,2},{3,35},{35,3},{4,36},{36... | collective-permute-start | bytes 983048 | tf_op jit(solution)/shard_map/ppermute | solution.py:82
  17.7 0.7 fusion.34
  18.4 1.9 %collective-permute-start.1 = (f32[1,5,1,32,128]{4,1,0,3,2:T(8,128)}, f32[1,5,1,32,128]{4,1,0,3,2:T(8,128)S(1)}, u32[]{:S(2)}, u32[]{:S(2)}) collective-permute-start(f32[1,5,1,32,128]{4,1,0,3,2:T(8,128)} %get-tuple-element.9), channel_id=1, source_target_pairs={{0,1},{1,2},{2,3},{3,4},{4,5},{5,6},{6,7},{7,8},{8,9},{9,10},{10,1... | collective-permute-start | bytes 245768 | tf_op jit(solution)/shard_map/ppermute | solution.py:20
  20.3 6.3 %collective-permute-start = (f32[1,5,1,32,128]{4,1,0,3,2:T(8,128)}, f32[1,5,1,32,128]{4,1,0,3,2:T(8,128)S(1)}, u32[]{:S(2)}, u32[]{:S(2)}) collective-permute-start(f32[1,5,1,32,128]{4,1,0,3,2:T(8,128)} %get-tuple-element.10), channel_id=1, source_target_pairs={{1,0},{2,1},{3,2},{4,3},{5,4},{6,5},{7,6},{8,7},{9,8},{10,9},{11,1... | collective-permute-start | bytes 245768 | tf_op jit(solution)/shard_map/ppermute | solution.py:23
  27.0 1.5 %fusion.35 = (f32[1,5,8,31,128]{4,1,0,3,2:T(8,128)}, f32[1,5,8,31,128]{4,1,0,3,2:T(8,128)}) fusion(f32[1,5,8,32,128]{4,1,0,3,2:T(8,128)S(1)} %copy.93), kind=kLoop, calls=%fused_computation.95 | loop fusion | bytes 2539520 | tf_op jit(solution)/shard_map/slice | solution.py:57
  28.5 2.1 %collective-permute-done.3 = f32[1,5,8,16,128]{4,3,2,1,0:T(8,128)S(1)} collective-permute-done((f32[1,5,8,16,128]{4,3,2,1,0:T(8,128)S(1)}, f32[1,5,8,16,128]{4,3,2,1,0:T(8,128)S(1)}, u32[]{:S(2)}, u32[]{:S(2)}) %collective-permute-start.3) | collective-permute-done | bytes 327712 | tf_op jit(solution)/shard_map/ppermute | solution.py:82
  30.6 2.0 %multiply_add_fusion = f32[8,5,8,16,128]{4,3,2,1,0:T(8,128)} fusion(f32[5,8,16,128]{3,2,1,0:T(8,128)S(1)} %bitcast.47, f32[8]{0:T(128)S(1)} %get-tuple-element.33, f32[5,8,16,128]{3,2,1,0:T(8,128)S(1)} %get-tuple-element.15, f32[8]{0:T(128)S(1)} %get-tuple-element.34), kind=kLoop, calls=%fused_computation.7 | loop fusion | flops 1966080 | bytes 3276864 | tf_op jit(solution)/shard_map/add | solution.py:86
  33.1 26.7 %all-gather.2.cloned.1.call-done = f32[8,5,8,16,128]{4,3,2,1,0:T(8,128)} async-done(((f32[1,5,8,16,128]{4,3,2,1,0:T(8,128)}), f32[8,5,8,16,128]{4,3,2,1,0:T(8,128)}) %all-gather.2.cloned.1.call-update) | async-done | bytes 2621456 | tf_op jit(solution)/shard_map/all_gather | solution.py:90
  59.8 2.2 %fusion.33 = (f32[8,5,8,1,128]{4,3,2,1,0:T(1,128)S(1)}, f32[8,5,8,1,128]{4,3,2,1,0:T(1,128)S(1)}) fusion(f32[8,5,8,16,128]{4,3,2,1,0:T(8,128)} %all-gather.2.cloned.1.call-done), kind=kLoop, calls=%fused_computation.93 | loop fusion | bytes 655360 | tf_op jit(solution)/shard_map/slice | solution.py:95
  62.0 2.1 %convolution_bitcast_fusion = f32[2,5,8,128,8]{3,4,1,2,0:T(8,128)S(1)} fusion(s32[2,8,128]{2,1,0:T(8,128)} %param.12, f32[1,8,5,8,128]{4,1,2,3,0:T(8,128)S(1)} %get-tuple-element.31, f32[1,8,5,8,128]{4,1,2,3,0:T(8,128)S(1)} %get-tuple-element.32), kind=kOutput, calls=%fused_computation.14 | convolution fusion | flops 126173184 | bytes 663552 | tf_op jit(solution)/shard_map/szvir,sikr->szvik/dot_general | solution.py:100
  64.9 7.4 %collective-permute-start.2 = (f32[92160]{0:T(1024)S(1)}, f32[92160]{0:T(1024)S(1)}, u32[]{:S(2)}, u32[]{:S(2)}) collective-permute-start(f32[92160]{0:T(1024)S(1)} %pad_maximum_fusion.4), channel_id=1, source_target_pairs={{0,32},{32,0},{1,33},{33,1},{2,34},{34,2},{3,35},{35,3},{4,36},{36... | collective-permute-start | bytes 1105928 | tf_op jit(solution)/shard_map/ppermute | solution.py:107
  72.4 0.7 broadcast_multiply_fusion
  73.0 1.3 %pad_subtract_fusion = f32[1,5,8,32,128]{4,1,0,3,2:T(8,128)} fusion(f32[1,5,8,32,127]{4,1,0,3,2:T(8,128)S(1)} %get-tuple-element.14, f32[1,5,8,32,127]{4,1,0,3,2:T(8,128)S(1)} %get-tuple-element.13), kind=kLoop, calls=%fused_computation.21 | loop fusion | flops 163840 | bytes 1955840 | tf_op jit(solution)/shard_map/sub | solution.py:62
  74.4 1.1 fusion.14
  75.5 6.9 %collective-permute-done.2 = f32[92160]{0:T(1024)S(1)} collective-permute-done((f32[92160]{0:T(1024)S(1)}, f32[92160]{0:T(1024)S(1)}, u32[]{:S(2)}, u32[]{:S(2)}) %collective-permute-start.2) | collective-permute-done | bytes 368672 | tf_op jit(solution)/shard_map/ppermute | solution.py:107
  82.5 1.1 fusion.13
  84.1 0.7 fusion.39
  84.8 23.5 %reduce-scatter.2.cloned.1.call-done = f32[1,5,8,16,128]{4,3,2,1,0:T(8,128)} async-done(((f32[8,5,8,16,128]{4,3,2,1,0:T(8,128)}), f32[1,5,8,16,128]{4,3,2,1,0:T(8,128)}) %reduce-scatter.2.cloned.1.call-update) | async-done | bytes 327696 | tf_op jit(solution)/shard_map/reduce_scatter | solution.py:87
  108.3 1.2 copy.109
  109.5 6.8 %fusion.10 = f32[1,5,8,32,128]{4,1,0,3,2:T(8,128)S(1)} fusion(f32[1,5,8,32,128]{4,1,0,3,2:T(8,128)} %pad_subtract_fusion, f32[1,5,8,32,128]{4,1,0,3,2:T(8,128)} %fusion.13, f32[1,5,8,32,128]{4,1,0,3,2:T(8,128)} %fusion.14, f32[1,5,8,8,128]{4,1,0,3,2:T(8,128)} %get-tuple-element.22, f32[1,5,8,16,128]{4,1,0,3,2:T(8,128)S(1)} %copy.109, ...), kind=kOutput, calls=%fused_computation.13 | convolution fusion | flops 33914880 | bytes 7625004 | tf_op jit(solution)/shard_map/dab,dnbijk->naijk/dot_general | solution.py:63
  116.3 1.0 copy.111
  (48 shorter events, 2.5 us)
Async XLA Ops:
  6.5 103.0 %copy-start = (f32[3,5,5]{2,0,1:T(4,128)S(1)}, f32[3,5,5]{2,0,1:T(4,128)}, u32[]{:S(2)}) copy-start(f32[3,5,5]{2,0,1:T(4,128)} %param.11) | copy-start | bytes 904
  6.5 10.7 %copy-start.4 = (f32[1,5,8,32,128]{4,3,2,1,0:T(8,128)S(1)}, f32[1,5,8,32,128]{4,3,2,1,0:T(8,128)}, u32[]{:S(2)}) copy-start(f32[1,5,8,32,128]{4,3,2,1,0:T(8,128)} %param.7) | copy-start | bytes 1966084
  6.5 20.2 %copy-start.8 = (s32[1,2,8,128]{3,2,1,0:T(8,128)S(1)}, s32[1,2,8,128]{3,2,1,0:T(8,128)}, u32[]{:S(2)}) copy-start(s32[1,2,8,128]{3,2,1,0:T(8,128)} %param.13) | copy-start | bytes 24580
  6.5 53.3 %all-gather.2.cloned.1.call-start = ((), (), s32[]{:S(2)}) async-start(), calls=%async_computation.1 | async-start | bytes 2949120 | tf_op jit(solution)/shard_map/all_gather | solution.py:90
  8.4 99.9 %reduce-scatter.2.cloned.1.call-start = ((), (), s32[]{:S(2)}) async-start(), calls=%async_computation.2 | async-start | bytes 2949120 | tf_op jit(solution)/shard_map/reduce_scatter | solution.py:87
  9.5 21.1 %collective-permute-start.3 = (f32[1,5,8,16,128]{4,3,2,1,0:T(8,128)S(1)}, f32[1,5,8,16,128]{4,3,2,1,0:T(8,128)S(1)}, u32[]{:S(2)}, u32[]{:S(2)}) collective-permute-start(f32[1,5,8,16,128]{4,3,2,1,0:T(8,128)S(1)} %get-tuple-element.16), channel_id=1, source_target_pairs={{0,32},{32,0},{1,33},{33,1},{2,34},{34,2},{3,35},{35,3},{4,36},{36... | collective-permute-start | bytes 983048 | tf_op jit(solution)/shard_map/ppermute | solution.py:82
  18.4 56.0 %collective-permute-start.1 = (f32[1,5,1,32,128]{4,1,0,3,2:T(8,128)}, f32[1,5,1,32,128]{4,1,0,3,2:T(8,128)S(1)}, u32[]{:S(2)}, u32[]{:S(2)}) collective-permute-start(f32[1,5,1,32,128]{4,1,0,3,2:T(8,128)} %get-tuple-element.9), channel_id=1, source_target_pairs={{0,1},{1,2},{2,3},{3,4},{4,5},{5,6},{6,7},{7,8},{8,9},{9,10},{10,1... | collective-permute-start | bytes 245768 | tf_op jit(solution)/shard_map/ppermute | solution.py:20
  20.3 54.1 %collective-permute-start = (f32[1,5,1,32,128]{4,1,0,3,2:T(8,128)}, f32[1,5,1,32,128]{4,1,0,3,2:T(8,128)S(1)}, u32[]{:S(2)}, u32[]{:S(2)}) collective-permute-start(f32[1,5,1,32,128]{4,1,0,3,2:T(8,128)} %get-tuple-element.10), channel_id=1, source_target_pairs={{1,0},{2,1},{3,2},{4,3},{5,4},{6,5},{7,6},{8,7},{9,8},{10,9},{11,1... | collective-permute-start | bytes 245768 | tf_op jit(solution)/shard_map/ppermute | solution.py:23
  59.8 4.6 %copy-start.3 = (f32[8,5,8,16,128]{4,3,2,1,0:T(8,128)S(1)}, f32[8,5,8,16,128]{4,3,2,1,0:T(8,128)}, u32[]{:S(2)}) copy-start(f32[8,5,8,16,128]{4,3,2,1,0:T(8,128)} %all-gather.2.cloned.1.call-done) | copy-start | bytes 7864324
  64.4 8.0 %copy-start.7 = (f32[8,32,128]{2,1,0:T(8,128)S(1)}, f32[8,32,128]{2,1,0:T(8,128)}, u32[]{:S(2)}) copy-start(f32[8,32,128]{2,1,0:T(8,128)} %param.9) | copy-start | bytes 393220
  64.9 17.4 %collective-permute-start.2 = (f32[92160]{0:T(1024)S(1)}, f32[92160]{0:T(1024)S(1)}, u32[]{:S(2)}, u32[]{:S(2)}) collective-permute-start(f32[92160]{0:T(1024)S(1)} %pad_maximum_fusion.4), channel_id=1, source_target_pairs={{0,32},{32,0},{1,33},{33,1},{2,34},{34,2},{3,35},{35,3},{4,36},{36... | collective-permute-start | bytes 1105928 | tf_op jit(solution)/shard_map/ppermute | solution.py:107
  73.0 9.5 %copy-start.1 = (f32[1,5,8,31,128]{4,1,0,3,2:T(8,128)S(1)}, f32[1,5,8,31,128]{4,1,0,3,2:T(8,128)}, u32[]{:S(2)}) copy-start(f32[1,5,8,31,128]{4,1,0,3,2:T(8,128)} %get-tuple-element.11) | copy-start | bytes 1904644
  73.0 9.5 %copy-start.2 = (f32[1,5,8,31,128]{4,1,0,3,2:T(8,128)S(1)}, f32[1,5,8,31,128]{4,1,0,3,2:T(8,128)}, u32[]{:S(2)}) copy-start(f32[1,5,8,31,128]{4,1,0,3,2:T(8,128)} %get-tuple-element.12) | copy-start | bytes 1904644
  74.4 9.3 %copy-start.5 = (f32[1,5,1,32,128]{4,1,0,3,2:T(8,128)}, f32[1,5,1,32,128]{4,1,0,3,2:T(8,128)S(1)}, u32[]{:S(2)}) copy-start(f32[1,5,1,32,128]{4,1,0,3,2:T(8,128)S(1)} %collective-permute-done.1) | copy-start | bytes 245764
  74.4 8.1 %copy-start.6 = (f32[1,5,1,32,128]{4,1,0,3,2:T(8,128)}, f32[1,5,1,32,128]{4,1,0,3,2:T(8,128)S(1)}, u32[]{:S(2)}) copy-start(f32[1,5,1,32,128]{4,1,0,3,2:T(8,128)S(1)} %collective-permute-done) | copy-start | bytes 245764
Sparse Core Ops, SparseCore 0:
  9.4 50.3 all-gather.1
  62.6 45.6 reduce-scatter.1

commit v4 on v3

--- a/solution.py
+++ b/solution.py
@@ -66,6 +66,39 @@
     return base - SECTION_ALPHA * pseudo_step[None, None] * (spatial + time_term)
 
 
+def reduced_along_z(own_block, partner_block, y, total_count):
+    ring = lax.axis_size("tz")
+    forward = [(i, (i + 1) % ring) for i in range(ring)]
+    backward = [(i, (i - 1) % ring) for i in range(ring)]
+    offsets = jnp.arange(ring, dtype=jnp.int32)
+    own_weights = time_weights(Y_PARTS * offsets, total_count)
+    partner_weights = time_weights(Y_PARTS * offsets + 2 * y - 1, total_count)
+    half = own_block.shape[2] // 2
+    pieces = (slice(0, half), slice(half, None))
+
+    def contribution(offset, piece):
+        k = offset % ring
+        return own_weights[k] * own_block[:, :, piece] + partner_weights[k] * partner_block[:, :, piece]
+
+    depth = ring // 2
+    depths = {(1, 0): depth, (1, 1): depth - 1, (-1, 0): depth - 1, (-1, 1): depth}
+    running = {key: None for key in depths}
+    for step in range(1, depth + 1):
+        for direction, perm in ((1, forward), (-1, backward)):
+            keys = [key for key in depths if key[0] == direction and step <= depths[key]]
+            sends = []
+            for key in keys:
+                term = contribution(direction * (depths[key] - step + 1), pieces[key[1]])
+                sends.append(term if running[key] is None else running[key] + term)
+            arrived = lax.ppermute(tuple(sends), "tz", perm)
+            for key, value in zip(keys, arrived):
+                running[key] = value
+    halves = [
+        running[(1, part)] + running[(-1, part)] for part in range(2)
+    ]
+    return contribution(0, slice(None)) + jnp.concatenate(halves, axis=2)
+
+
 def per_device(state, base, pseudo_step, eddy_visc, jacobians, partner_radial, partner_instance):
     ring = lax.axis_size("tz")
     total_count = ring * Y_PARTS
@@ -80,11 +113,7 @@
 
     inner = state[:, :, :, edge : pitch - edge]
     other = lax.ppermute(inner, "ty", swap)
-    expand = (ring,) + (1,) * (inner.ndim - 1)
-    own_weights = time_weights(ring_ids - own, total_count).reshape(expand)
-    partner_weights = time_weights(ring_ids - partner, total_count).reshape(expand)
-    contributions = own_weights * inner + partner_weights * other
-    inner_term = lax.psum_scatter(contributions, "tz", scatter_dimension=0, tiled=True)
+    inner_term = reduced_along_z(inner, other, y, total_count)
 
     outer = jnp.concatenate([state[:, :, :, :edge], state[:, :, :, pitch - edge :]], axis=3)
     held = lax.all_gather(outer, "tz", axis=0, tiled=True)

time: 124 us -> 190 us (1.53)
  the two profiles are of different devices: /device:TPU:6 before, /device:TPU:32 now
where the time goes in v4:
time: 190 us; the launch traced here: 189 us
  waiting for transfers between devices  65.6 us (35%)
  starting transfers between devices  61.7 us (32%)
  other arithmetic  28.8 us (15%)
  between operations  14 us (7%)
  local copies, waits for them, and re-layouts  11.7 us (6%)
  matrix products  7 us (4%)
    ppermute x14, starting transfers between devices, reduced_along_z(): arrived = lax.ppermute(tuple(sends), 'tz', perm)  49.2 us
    ppermute x14, waiting for transfers between devices, reduced_along_z(): arrived = lax.ppermute(tuple(sends), 'tz', perm)  32.6 us
    ppermute x1, waiting for transfers between devices, per_device(): other = lax.ppermute(inner, 'ty', swap)  23.3 us
    add x6, other arithmetic, reduced_along_z(): sends.append(term if running[key] is None else running[key] + term)  16.5 us
    ppermute x1, waiting for transfers between devices, per_device(): received = lax.ppermute(message, 'ty', swap)  9.7 us
    ppermute x1, starting transfers between devices, per_device(): other = lax.ppermute(inner, 'ty', swap)  6.94 us
    dot_general x1, matrix products, section_update(): jnp.einsum('dab,dnbijk->naijk', jacobians, diffs, precision=lax.Precision...  5.56 us
  transfers between devices with their start and end apart: 19, of which 10 were waited for; matrix products, arithmetic and copies ran while one was open for 20% of the time, Pallas kernels for 0%

profile of v4, /device:TPU:32, one launch (start us, length us, event | category | flops | bytes accessed | tf_op | source)
XLA Modules:
  0.0 188.7 jit_solution(8163378602950517532)
XLA Ops:
  10.6 2.4 %collective-permute-start.1 = (f32[1,5,1,32,128]{4,1,0,3,2:T(8,128)}, f32[1,5,1,32,128]{4,1,0,3,2:T(8,128)}, u32[]{:S(2)}, u32[]{:S(2)}) collective-permute-start(f32[1,5,1,32,128]{4,1,0,3,2:T(8,128)} %get-tuple-element.19), channel_id=1, source_target_pairs={{0,1},{1,2},{2,3},{3,4},{4,5},{5,6},{6,7},{7,8},{8,9},{9,10},{10,1... | collective-permute-start | bytes 245768 | tf_op jit(solution)/shard_map/ppermute | solution.py:20
  14.3 6.9 %collective-permute-start.3 = (f32[1,5,8,16,128]{4,1,0,3,2:T(8,128)S(1)}, f32[1,5,8,16,128]{4,1,0,3,2:T(8,128)S(1)}, u32[]{:S(2)}, u32[]{:S(2)}) collective-permute-start(f32[1,5,8,16,128]{4,1,0,3,2:T(8,128)S(1)} %slice.288), channel_id=1, source_target_pairs={{0,32},{32,0},{1,33},{33,1},{2,34},{34,2},{3,35},{35,3},{4,36},{36... | collective-permute-start | bytes 983048 | tf_op jit(solution)/shard_map/ppermute | solution.py:115
  22.7 23.3 %collective-permute-done.3 = f32[1,5,8,16,128]{4,1,0,3,2:T(8,128)S(1)} collective-permute-done((f32[1,5,8,16,128]{4,1,0,3,2:T(8,128)S(1)}, f32[1,5,8,16,128]{4,1,0,3,2:T(8,128)S(1)}, u32[]{:S(2)}, u32[]{:S(2)}) %collective-permute-start.3) | collective-permute-done | bytes 327712 | tf_op jit(solution)/shard_map/ppermute | solution.py:115
  47.4 11.0 %collective-permute-start.8 = (f32[1,5,4,16,128]{4,1,0,3,2:T(8,128)S(1)}, f32[1,5,4,16,128]{4,1,0,3,2:T(8,128)S(1)}, u32[]{:S(2)}, u32[]{:S(2)}) collective-permute-start(f32[1,5,4,16,128]{4,1,0,3,2:T(8,128)S(1)} %multiply_add_fusion.2), channel_id=1, source_target_pairs={{0,448},{64,0},{128,64},{192,128},{256,192},{320,256},{384,320},{4... | collective-permute-start | bytes 491528 | tf_op jit(solution)/shard_map/ppermute | solution.py:93
  59.7 4.9 %collective-permute-done.8 = f32[1,5,4,16,128]{4,1,0,3,2:T(8,128)S(1)} collective-permute-done((f32[1,5,4,16,128]{4,1,0,3,2:T(8,128)S(1)}, f32[1,5,4,16,128]{4,1,0,3,2:T(8,128)S(1)}, u32[]{:S(2)}, u32[]{:S(2)}) %collective-permute-start.8) | collective-permute-done | bytes 163872 | tf_op jit(solution)/shard_map/ppermute | solution.py:93
  64.6 3.8 %add_add_fusion.6 = (f32[1,5,4,16,128]{4,1,0,3,2:T(8,128)S(1)}, f32[1,5,4,16,128]{4,1,0,3,2:T(8,128)S(1)}, f32[1,5,4,16,128]{4,1,0,3,2:T(8,128)S(1)}) fusion(f32[1,5,4,16,128]{4,1,0,3,2:T(8,128)S(1)} %collective-permute-done.8, f32[1,5,8,16,128]{4,1,0,3,2:T(8,128)S(1)} %collective-permute-done.3, f32[1,5,8,32,128]{4,1,0,3,2:T(8,128)S(1)} %copy.99, ...), kind=kLoop, calls=%fused_computation.40 | loop fusion | flops 409600 | bytes 1310744 | tf_op jit(solution)/shard_map/add | solution.py:92
  68.4 5.6 %collective-permute-start.9 = (f32[1,5,4,16,128]{4,1,0,3,2:T(8,128)S(1)}, f32[1,5,4,16,128]{4,1,0,3,2:T(8,128)S(1)}, u32[]{:S(2)}, u32[]{:S(2)}) collective-permute-start(f32[1,5,4,16,128]{4,1,0,3,2:T(8,128)S(1)} %get-tuple-element.13), channel_id=1, source_target_pairs={{0,448},{64,0},{128,64},{192,128},{256,192},{320,256},{384,320},{4... | collective-permute-start | bytes 491528 | tf_op jit(solution)/shard_map/ppermute | solution.py:93
  75.9 2.1 %collective-permute-start.4 = (f32[1,5,4,16,128]{4,1,0,3,2:T(8,128)S(1)}, f32[1,5,4,16,128]{4,1,0,3,2:T(8,128)S(1)}, u32[]{:S(2)}, u32[]{:S(2)}) collective-permute-start(f32[1,5,4,16,128]{4,1,0,3,2:T(8,128)S(1)} %get-tuple-element.15), channel_id=1, source_target_pairs={{0,64},{64,128},{128,192},{192,256},{256,320},{320,384},{384,448},... | collective-permute-start | bytes 491528 | tf_op jit(solution)/shard_map/ppermute | solution.py:93
  79.5 6.9 %collective-permute-done.11 = f32[1,5,4,16,128]{4,1,0,3,2:T(8,128)S(1)} collective-permute-done((f32[1,5,4,16,128]{4,1,0,3,2:T(8,128)S(1)}, f32[1,5,4,16,128]{4,1,0,3,2:T(8,128)S(1)}, u32[]{:S(2)}, u32[]{:S(2)}) %collective-permute-start.11) | collective-permute-done | bytes 163872 | tf_op jit(solution)/shard_map/ppermute | solution.py:93
  86.4 3.9 %collective-permute-done.4 = f32[1,5,4,16,128]{4,1,0,3,2:T(8,128)S(1)} collective-permute-done((f32[1,5,4,16,128]{4,1,0,3,2:T(8,128)S(1)}, f32[1,5,4,16,128]{4,1,0,3,2:T(8,128)S(1)}, u32[]{:S(2)}, u32[]{:S(2)}) %collective-permute-start.4) | collective-permute-done | bytes 163872 | tf_op jit(solution)/shard_map/ppermute | solution.py:93
  90.3 5.7 %add_add_fusion.5 = (f32[1,5,4,16,128]{4,1,0,3,2:T(8,128)}, f32[1,5,4,16,128]{4,1,0,3,2:T(8,128)}, f32[1,5,4,16,128]{4,1,0,3,2:T(8,128)S(1)}, f32[1,5,4,16,128]{4,1,0,3,2:T(8,128)S(1)}) fusion(f32[1,5,4,16,128]{4,1,0,3,2:T(8,128)S(1)} %collective-permute-done.9, f32[1,5,8,16,128]{4,1,0,3,2:T(8,128)S(1)} %collective-permute-done.3, ...), kind=kLoop, calls=%fused_computation.39 | loop fusion | flops 614400 | bytes 1802272 | tf_op jit(solution)/shard_map/add | solution.py:92
  98.6 2.0 %collective-permute-start.12 = (f32[1,5,4,16,128]{4,1,0,3,2:T(8,128)S(1)}, f32[1,5,4,16,128]{4,1,0,3,2:T(8,128)S(1)}, u32[]{:S(2)}, u32[]{:S(2)}) collective-permute-start(f32[1,5,4,16,128]{4,1,0,3,2:T(8,128)S(1)} %get-tuple-element.11), channel_id=1, source_target_pairs={{0,64},{64,128},{128,192},{192,256},{256,320},{320,384},{384,448},... | collective-permute-start | bytes 491528 | tf_op jit(solution)/shard_map/ppermute | solution.py:93
  100.7 5.1 %collective-permute-start.14 = (f32[1,5,4,16,128]{4,1,0,3,2:T(8,128)S(1)}, f32[1,5,4,16,128]{4,1,0,3,2:T(8,128)S(1)}, u32[]{:S(2)}, u32[]{:S(2)}) collective-permute-start(f32[1,5,4,16,128]{4,1,0,3,2:T(8,128)S(1)} %get-tuple-element.12), channel_id=1, source_target_pairs={{0,448},{64,0},{128,64},{192,128},{256,192},{320,256},{384,320},{4... | collective-permute-start | bytes 491528 | tf_op jit(solution)/shard_map/ppermute | solution.py:93
  105.8 2.7 %collective-permute-done.5 = f32[1,5,4,16,128]{4,1,0,3,2:T(8,128)S(1)} collective-permute-done((f32[1,5,4,16,128]{4,1,0,3,2:T(8,128)}, f32[1,5,4,16,128]{4,1,0,3,2:T(8,128)S(1)}, u32[]{:S(2)}, u32[]{:S(2)}) %collective-permute-start.5) | collective-permute-done | bytes 163872 | tf_op jit(solution)/shard_map/ppermute | solution.py:93
  112.3 6.9 %collective-permute-done.6 = f32[1,5,4,16,128]{4,1,0,3,2:T(8,128)S(1)} collective-permute-done((f32[1,5,4,16,128]{4,1,0,3,2:T(8,128)S(1)}, f32[1,5,4,16,128]{4,1,0,3,2:T(8,128)S(1)}, u32[]{:S(2)}, u32[]{:S(2)}) %collective-permute-start.6) | collective-permute-done | bytes 163872 | tf_op jit(solution)/shard_map/ppermute | solution.py:93
  119.2 2.6 %add_add_fusion.7 = (f32[1,5,4,16,128]{4,1,0,3,2:T(8,128)S(1)}, f32[1,5,4,16,128]{4,1,0,3,2:T(8,128)S(1)}, f32[1,5,4,16,128]{4,1,0,3,2:T(8,128)S(1)}) fusion(f32[1,5,4,16,128]{4,1,0,3,2:T(8,128)S(1)} %collective-permute-done.6, f32[1,5,8,16,128]{4,1,0,3,2:T(8,128)S(1)} %collective-permute-done.3, f32[1,5,8,32,128]{4,1,0,3,2:T(8,128)S(1)} %copy.99, ...), kind=kLoop, calls=%fused_computation.42 | loop fusion | flops 491520 | bytes 1638416 | tf_op jit(solution)/shard_map/add | solution.py:92
  123.8 6.6 %collective-permute-done.15 = f32[1,5,4,16,128]{4,1,0,3,2:T(8,128)S(1)} collective-permute-done((f32[1,5,4,16,128]{4,1,0,3,2:T(8,128)S(1)}, f32[1,5,4,16,128]{4,1,0,3,2:T(8,128)S(1)}, u32[]{:S(2)}, u32[]{:S(2)}) %collective-permute-start.15) | collective-permute-done | bytes 163872 | tf_op jit(solution)/shard_map/ppermute | solution.py:93
  131.7 2.8 %collective-permute-start.16 = (f32[1,5,4,16,128]{4,1,0,3,2:T(8,128)S(1)}, f32[1,5,4,16,128]{4,1,0,3,2:T(8,128)S(1)}, u32[]{:S(2)}, u32[]{:S(2)}) collective-permute-start(f32[1,5,4,16,128]{4,1,0,3,2:T(8,128)S(1)} %add_add_fusion.1), channel_id=1, source_target_pairs={{0,448},{64,0},{128,64},{192,128},{256,192},{320,256},{384,320},{4... | collective-permute-start | bytes 491528 | tf_op jit(solution)/shard_map/ppermute | solution.py:93
  137.9 3.9 %collective-permute-start.7 = (f32[1,5,4,16,128]{4,1,0,3,2:T(8,128)S(1)}, f32[1,5,4,16,128]{4,1,0,3,2:T(8,128)}, u32[]{:S(2)}, u32[]{:S(2)}) collective-permute-start(f32[1,5,4,16,128]{4,1,0,3,2:T(8,128)S(1)} %get-tuple-element.16), channel_id=1, source_target_pairs={{0,64},{64,128},{128,192},{192,256},{256,320},{320,384},{384,448},... | collective-permute-start | bytes 491528 | tf_op jit(solution)/shard_map/ppermute | solution.py:93
  141.8 3.1 %collective-permute-start.13 = (f32[1,5,4,16,128]{4,1,0,3,2:T(8,128)S(1)}, f32[1,5,4,16,128]{4,1,0,3,2:T(8,128)}, u32[]{:S(2)}, u32[]{:S(2)}) collective-permute-start(f32[1,5,4,16,128]{4,1,0,3,2:T(8,128)S(1)} %get-tuple-element.17), channel_id=1, source_target_pairs={{0,64},{64,128},{128,192},{192,256},{256,320},{320,384},{384,448},... | collective-permute-start | bytes 491528 | tf_op jit(solution)/shard_map/ppermute | solution.py:93
  146.8 2.2 %multiply_reduce_fusion = f32[2,5,8,16,128]{4,3,2,1,0:T(8,128)S(1)} fusion(f32[8,5,8,16,128]{4,3,2,1,0:T(8,128)} %all-gather.2.cloned.1.call-done, f32[2,8]{1,0:T(2,128)S(1)} %subtract_select_fusion), kind=kLoop, calls=%fused_computation | loop fusion | flops 2457600 | bytes 3276864 | tf_op jit(solution)/shard_map/reduce_sum | solution.py:122
  152.9 4.0 %collective-permute-start.17 = (f32[1,5,4,16,128]{4,1,0,3,2:T(8,128)S(1)}, f32[1,5,4,16,128]{4,1,0,3,2:T(8,128)S(1)}, u32[]{:S(2)}, u32[]{:S(2)}) collective-permute-start(f32[1,5,4,16,128]{4,1,0,3,2:T(8,128)S(1)} %copy-done.6), channel_id=1, source_target_pairs={{0,448},{64,0},{128,64},{192,128},{256,192},{320,256},{384,320},{4... | collective-permute-start | bytes 491528 | tf_op jit(solution)/shard_map/ppermute | solution.py:93
  163.8 9.7 %collective-permute-done.2 = f32[92160]{0:T(1024)S(1)} collective-permute-done((f32[92160]{0:T(1024)S(1)}, f32[92160]{0:T(1024)S(1)}, u32[]{:S(2)}, u32[]{:S(2)}) %collective-permute-start.2) | collective-permute-done | bytes 368672 | tf_op jit(solution)/shard_map/ppermute | solution.py:136
  175.3 5.6 %fusion.10 = f32[1,5,8,32,128]{4,1,0,3,2:T(8,128)S(1)} fusion(f32[1,5,8,32,128]{4,1,0,3,2:T(8,128)S(1)} %copy-done.5, f32[1,5,8,32,128]{4,1,0,3,2:T(8,128)S(1)} %fusion.13, f32[1,5,8,32,128]{4,1,0,3,2:T(8,128)S(1)} %fusion.14, f32[1,5,8,8,128]{4,1,0,3,2:T(8,128)S(1)} %get-tuple-element.30, f32[1,5,8,16,128]{4,1,0,3,2:T(8,128)S(1)} %maximum_add_fusion, ...), kind=kOutput, calls=%fused_computation.12 | convolution fusion | flops 33914880 | bytes 7625004 | tf_op jit(solution)/shard_map/dab,dnbijk->naijk/dot_general | solution.py:63
  (92 shorter events, 41.2 us)
Async XLA Ops:
  6.5 167.8 %copy-start = (f32[3,5,5]{2,0,1:T(4,128)S(1)}, f32[3,5,5]{2,0,1:T(4,128)}, u32[]{:S(2)}) copy-start(f32[3,5,5]{2,0,1:T(4,128)} %param.11) | copy-start | bytes 904
  6.5 140.3 %all-gather.2.cloned.1.call-start = ((), (), s32[]{:S(2)}) async-start(), calls=%async_computation | async-start | bytes 2949120 | tf_op jit(solution)/shard_map/all_gather | solution.py:119
  10.6 142.3 %collective-permute-start.1 = (f32[1,5,1,32,128]{4,1,0,3,2:T(8,128)}, f32[1,5,1,32,128]{4,1,0,3,2:T(8,128)}, u32[]{:S(2)}, u32[]{:S(2)}) collective-permute-start(f32[1,5,1,32,128]{4,1,0,3,2:T(8,128)} %get-tuple-element.19), channel_id=1, source_target_pairs={{0,1},{1,2},{2,3},{3,4},{4,5},{5,6},{6,7},{7,8},{8,9},{9,10},{10,1... | collective-permute-start | bytes 245768 | tf_op jit(solution)/shard_map/ppermute | solution.py:20
  12.9 144.0 %collective-permute-start = (f32[1,5,1,32,128]{4,1,0,3,2:T(8,128)}, f32[1,5,1,32,128]{4,1,0,3,2:T(8,128)}, u32[]{:S(2)}, u32[]{:S(2)}) collective-permute-start(f32[1,5,1,32,128]{4,1,0,3,2:T(8,128)} %get-tuple-element.20), channel_id=1, source_target_pairs={{1,0},{2,1},{3,2},{4,3},{5,4},{6,5},{7,6},{8,7},{9,8},{10,9},{11,1... | collective-permute-start | bytes 245768 | tf_op jit(solution)/shard_map/ppermute | solution.py:23
  14.3 31.7 %collective-permute-start.3 = (f32[1,5,8,16,128]{4,1,0,3,2:T(8,128)S(1)}, f32[1,5,8,16,128]{4,1,0,3,2:T(8,128)S(1)}, u32[]{:S(2)}, u32[]{:S(2)}) collective-permute-start(f32[1,5,8,16,128]{4,1,0,3,2:T(8,128)S(1)} %slice.288), channel_id=1, source_target_pairs={{0,32},{32,0},{1,33},{33,1},{2,34},{34,2},{3,35},{35,3},{4,36},{36... | collective-permute-start | bytes 983048 | tf_op jit(solution)/shard_map/ppermute | solution.py:115
  47.4 17.2 %collective-permute-start.8 = (f32[1,5,4,16,128]{4,1,0,3,2:T(8,128)S(1)}, f32[1,5,4,16,128]{4,1,0,3,2:T(8,128)S(1)}, u32[]{:S(2)}, u32[]{:S(2)}) collective-permute-start(f32[1,5,4,16,128]{4,1,0,3,2:T(8,128)S(1)} %multiply_add_fusion.2), channel_id=1, source_target_pairs={{0,448},{64,0},{128,64},{192,128},{256,192},{320,256},{384,320},{4... | collective-permute-start | bytes 491528 | tf_op jit(solution)/shard_map/ppermute | solution.py:93
  68.4 11.1 %collective-permute-start.9 = (f32[1,5,4,16,128]{4,1,0,3,2:T(8,128)S(1)}, f32[1,5,4,16,128]{4,1,0,3,2:T(8,128)S(1)}, u32[]{:S(2)}, u32[]{:S(2)}) collective-permute-start(f32[1,5,4,16,128]{4,1,0,3,2:T(8,128)S(1)} %get-tuple-element.13), channel_id=1, source_target_pairs={{0,448},{64,0},{128,64},{192,128},{256,192},{320,256},{384,320},{4... | collective-permute-start | bytes 491528 | tf_op jit(solution)/shard_map/ppermute | solution.py:93
  74.0 12.3 %collective-permute-start.11 = (f32[1,5,4,16,128]{4,1,0,3,2:T(8,128)S(1)}, f32[1,5,4,16,128]{4,1,0,3,2:T(8,128)S(1)}, u32[]{:S(2)}, u32[]{:S(2)}) collective-permute-start(f32[1,5,4,16,128]{4,1,0,3,2:T(8,128)S(1)} %get-tuple-element.14), channel_id=1, source_target_pairs={{0,64},{64,128},{128,192},{192,256},{256,320},{320,384},{384,448},... | collective-permute-start | bytes 491528 | tf_op jit(solution)/shard_map/ppermute | solution.py:93
  75.9 21.9 %copy-start.7 = (f32[8,32,128]{2,1,0:T(8,128)S(1)}, f32[8,32,128]{2,1,0:T(8,128)}, u32[]{:S(2)}) copy-start(f32[8,32,128]{2,1,0:T(8,128)} %param.9) | copy-start | bytes 393220
  75.9 14.3 %collective-permute-start.4 = (f32[1,5,4,16,128]{4,1,0,3,2:T(8,128)S(1)}, f32[1,5,4,16,128]{4,1,0,3,2:T(8,128)S(1)}, u32[]{:S(2)}, u32[]{:S(2)}) collective-permute-start(f32[1,5,4,16,128]{4,1,0,3,2:T(8,128)S(1)} %get-tuple-element.15), channel_id=1, source_target_pairs={{0,64},{64,128},{128,192},{192,256},{256,320},{320,384},{384,448},... | collective-permute-start | bytes 491528 | tf_op jit(solution)/shard_map/ppermute | solution.py:93
  79.5 32.2 %copy-start.9 = (s32[1,2,8,128]{3,2,1,0:T(8,128)S(1)}, s32[1,2,8,128]{3,2,1,0:T(8,128)}, u32[]{:S(2)}) copy-start(s32[1,2,8,128]{3,2,1,0:T(8,128)} %param.13) | copy-start | bytes 24580
  95.9 12.5 %collective-permute-start.5 = (f32[1,5,4,16,128]{4,1,0,3,2:T(8,128)}, f32[1,5,4,16,128]{4,1,0,3,2:T(8,128)S(1)}, u32[]{:S(2)}, u32[]{:S(2)}) collective-permute-start(f32[1,5,4,16,128]{4,1,0,3,2:T(8,128)} %get-tuple-element.10), channel_id=1, source_target_pairs={{0,64},{64,128},{128,192},{192,256},{256,320},{320,384},{384,448},... | collective-permute-start | bytes 491528 | tf_op jit(solution)/shard_map/ppermute | solution.py:93
  98.5 36.1 %copy-start.1 = (f32[1,5,8,32,127]{4,1,0,3,2:T(8,128)S(1)}, f32[1,5,8,32,127]{4,1,0,3,2:T(8,128)}, u32[]{:S(2)}) copy-start(f32[1,5,8,32,127]{4,1,0,3,2:T(8,128)} %get-tuple-element.24) | copy-start | bytes 1950724
  98.6 13.7 %collective-permute-start.12 = (f32[1,5,4,16,128]{4,1,0,3,2:T(8,128)S(1)}, f32[1,5,4,16,128]{4,1,0,3,2:T(8,128)S(1)}, u32[]{:S(2)}, u32[]{:S(2)}) collective-permute-start(f32[1,5,4,16,128]{4,1,0,3,2:T(8,128)S(1)} %get-tuple-element.11), channel_id=1, source_target_pairs={{0,64},{64,128},{128,192},{192,256},{256,320},{320,384},{384,448},... | collective-permute-start | bytes 491528 | tf_op jit(solution)/shard_map/ppermute | solution.py:93
  100.7 11.7 %collective-permute-start.14 = (f32[1,5,4,16,128]{4,1,0,3,2:T(8,128)S(1)}, f32[1,5,4,16,128]{4,1,0,3,2:T(8,128)S(1)}, u32[]{:S(2)}, u32[]{:S(2)}) collective-permute-start(f32[1,5,4,16,128]{4,1,0,3,2:T(8,128)S(1)} %get-tuple-element.12), channel_id=1, source_target_pairs={{0,448},{64,0},{128,64},{192,128},{256,192},{320,256},{384,320},{4... | collective-permute-start | bytes 491528 | tf_op jit(solution)/shard_map/ppermute | solution.py:93
  109.7 9.5 %collective-permute-start.6 = (f32[1,5,4,16,128]{4,1,0,3,2:T(8,128)S(1)}, f32[1,5,4,16,128]{4,1,0,3,2:T(8,128)S(1)}, u32[]{:S(2)}, u32[]{:S(2)}) collective-permute-start(f32[1,5,4,16,128]{4,1,0,3,2:T(8,128)S(1)} %add_add_fusion.8), channel_id=1, source_target_pairs={{0,64},{64,128},{128,192},{192,256},{256,320},{320,384},{384,448},... | collective-permute-start | bytes 491528 | tf_op jit(solution)/shard_map/ppermute | solution.py:93
  121.8 8.6 %collective-permute-start.15 = (f32[1,5,4,16,128]{4,1,0,3,2:T(8,128)S(1)}, f32[1,5,4,16,128]{4,1,0,3,2:T(8,128)S(1)}, u32[]{:S(2)}, u32[]{:S(2)}) collective-permute-start(f32[1,5,4,16,128]{4,1,0,3,2:T(8,128)S(1)} %get-tuple-element.18), channel_id=1, source_target_pairs={{0,448},{64,0},{128,64},{192,128},{256,192},{320,256},{384,320},{4... | collective-permute-start | bytes 491528 | tf_op jit(solution)/shard_map/ppermute | solution.py:93
  131.7 10.1 %collective-permute-start.16 = (f32[1,5,4,16,128]{4,1,0,3,2:T(8,128)S(1)}, f32[1,5,4,16,128]{4,1,0,3,2:T(8,128)S(1)}, u32[]{:S(2)}, u32[]{:S(2)}) collective-permute-start(f32[1,5,4,16,128]{4,1,0,3,2:T(8,128)S(1)} %add_add_fusion.1), channel_id=1, source_target_pairs={{0,448},{64,0},{128,64},{192,128},{256,192},{320,256},{384,320},{4... | collective-permute-start | bytes 491528 | tf_op jit(solution)/shard_map/ppermute | solution.py:93
  135.9 24.1 %collective-permute-start.10 = (f32[1,5,4,16,128]{4,1,0,3,2:T(8,128)}, f32[1,5,4,16,128]{4,1,0,3,2:T(8,128)S(1)}, u32[]{:S(2)}, u32[]{:S(2)}) collective-permute-start(f32[1,5,4,16,128]{4,1,0,3,2:T(8,128)} %get-tuple-element.9), channel_id=1, source_target_pairs={{0,448},{64,0},{128,64},{192,128},{256,192},{320,256},{384,320},{4... | collective-permute-start | bytes 491528 | tf_op jit(solution)/shard_map/ppermute | solution.py:93
  137.9 22.2 %collective-permute-start.7 = (f32[1,5,4,16,128]{4,1,0,3,2:T(8,128)S(1)}, f32[1,5,4,16,128]{4,1,0,3,2:T(8,128)}, u32[]{:S(2)}, u32[]{:S(2)}) collective-permute-start(f32[1,5,4,16,128]{4,1,0,3,2:T(8,128)S(1)} %get-tuple-element.16), channel_id=1, source_target_pairs={{0,64},{64,128},{128,192},{192,256},{256,320},{320,384},{384,448},... | collective-permute-start | bytes 491528 | tf_op jit(solution)/shard_map/ppermute | solution.py:93
  141.8 19.2 %collective-permute-start.13 = (f32[1,5,4,16,128]{4,1,0,3,2:T(8,128)S(1)}, f32[1,5,4,16,128]{4,1,0,3,2:T(8,128)}, u32[]{:S(2)}, u32[]{:S(2)}) collective-permute-start(f32[1,5,4,16,128]{4,1,0,3,2:T(8,128)S(1)} %get-tuple-element.17), channel_id=1, source_target_pairs={{0,64},{64,128},{128,192},{192,256},{256,320},{320,384},{384,448},... | collective-permute-start | bytes 491528 | tf_op jit(solution)/shard_map/ppermute | solution.py:93
  152.9 8.3 %collective-permute-start.17 = (f32[1,5,4,16,128]{4,1,0,3,2:T(8,128)S(1)}, f32[1,5,4,16,128]{4,1,0,3,2:T(8,128)S(1)}, u32[]{:S(2)}, u32[]{:S(2)}) collective-permute-start(f32[1,5,4,16,128]{4,1,0,3,2:T(8,128)S(1)} %copy-done.6), channel_id=1, source_target_pairs={{0,448},{64,0},{128,64},{192,128},{256,192},{320,256},{384,320},{4... | collective-permute-start | bytes 491528 | tf_op jit(solution)/shard_map/ppermute | solution.py:93
  157.0 16.5 %collective-permute-start.2 = (f32[92160]{0:T(1024)S(1)}, f32[92160]{0:T(1024)S(1)}, u32[]{:S(2)}, u32[]{:S(2)}) collective-permute-start(f32[92160]{0:T(1024)S(1)} %pad_maximum_fusion.4), channel_id=1, source_target_pairs={{0,32},{32,0},{1,33},{33,1},{2,34},{34,2},{3,35},{35,3},{4,36},{36... | collective-permute-start | bytes 1105928 | tf_op jit(solution)/shard_map/ppermute | solution.py:136
  162.2 11.9 %copy-start.3 = (f32[1,5,8,31,128]{4,1,0,3,2:T(8,128)S(1)}, f32[1,5,8,31,128]{4,1,0,3,2:T(8,128)}, u32[]{:S(2)}) copy-start(f32[1,5,8,31,128]{4,1,0,3,2:T(8,128)} %get-tuple-element.21) | copy-start | bytes 1904644
  (8 other events, 27.9 us)
Sparse Core Ops, SparseCore 0:
  9.4 53.8 all-gather.1

commit v5 on v3

--- a/solution.py
+++ b/solution.py
@@ -51,19 +51,24 @@
     )
 
 
-def section_update(
-    state, base, pseudo_step, eddy_visc, jacobians, up_i, down_i, low_ghost, high_ghost, time_term
-):
+def section_spatial(state, eddy_visc, jacobians, up_i, down_i, low_ghost, high_ghost):
     up_j = jnp.concatenate([state[:, :, :, 1:], high_ghost[:, :, :, None]], axis=3)
     down_j = jnp.concatenate([low_ghost[:, :, :, None], state[:, :, :, :-1]], axis=3)
     zeros = jnp.zeros(state.shape[:4] + (1,), state.dtype)
     up_k = jnp.concatenate([state[..., 1:], zeros], axis=4)
     down_k = jnp.concatenate([zeros, state[..., :-1]], axis=4)
-    diffs = jnp.stack([up_i - down_i, up_j - down_j, up_k - down_k], axis=0) * 0.5
-    flux = jnp.einsum("dab,dnbijk->naijk", jacobians, diffs, precision=lax.Precision.HIGHEST)
+    diffs = [(up_i - down_i) * 0.5, (up_j - down_j) * 0.5, (up_k - down_k) * 0.5]
+    rows = []
+    for target in range(state.shape[1]):
+        total = None
+        for direction, diff in enumerate(diffs):
+            for source in range(state.shape[1]):
+                term = jacobians[direction, target, source] * diff[:, source]
+                total = term if total is None else total + term
+        rows.append(total)
+    flux = jnp.stack(rows, axis=1)
     laplace = up_i + down_i + up_j + down_j + up_k + down_k - 6.0 * state
-    spatial = flux - eddy_visc[None, None] * laplace
-    return base - SECTION_ALPHA * pseudo_step[None, None] * (spatial + time_term)
+    return flux - eddy_visc[None, None] * laplace
 
 
 def per_device(state, base, pseudo_step, eddy_visc, jacobians, partner_radial, partner_instance):
@@ -117,18 +122,10 @@
     extended = extended_2(state, (("space", 2),), 1)
     up_i = extended[:, :, 2:]
     down_i = extended[:, :, :-2]
-    return section_update(
-        state,
-        base,
-        pseudo_step,
-        eddy_visc,
-        jacobians,
-        up_i,
-        down_i,
-        low_ghost,
-        high_ghost,
-        time_term,
+    spatial = lax.optimization_barrier(
+        section_spatial(state, eddy_visc, jacobians, up_i, down_i, low_ghost, high_ghost)
     )
+    return base - SECTION_ALPHA * pseudo_step[None, None] * (spatial + time_term)
 
 
 def solution(mesh):

time: 124 us -> 148 us (1.19)
  the two profiles are of different devices: /device:TPU:6 before, /device:TPU:18 now
where the time goes in v5:
time: 148 us; the launch traced here: 147 us
  other arithmetic  58.6 us (40%)
  waiting for transfers between devices  44.7 us (30%)
  starting transfers between devices  16.3 us (11%)
  between operations  13.7 us (9%)
  local copies, waits for them, and re-layouts  11.3 us (8%)
  matrix products  2.13 us (1%)
    unnamed x4, other arithmetic  38.5 us
    all_gather x1, waiting for transfers between devices, per_device(): held = lax.all_gather(outer, 'tz', axis=0, tiled=True)  16.6 us
    ppermute x1, waiting for transfers between devices, per_device(): other = lax.ppermute(inner, 'ty', swap)  14.4 us
    ppermute x1, waiting for transfers between devices, per_device(): received = lax.ppermute(message, 'ty', swap)  13.6 us
    another operation x1, other arithmetic, section_spatial(): flux = jnp.stack(rows, axis=1)  9.51 us
    ppermute x1, starting transfers between devices, per_device(): other = lax.ppermute(inner, 'ty', swap)  6.21 us
    ppermute x1, starting transfers between devices, per_device(): received = lax.ppermute(message, 'ty', swap)  5.66 us
  transfers between devices with their start and end apart: 6, of which 3 were waited for; matrix products, arithmetic and copies ran while one was open for 46% of the time, Pallas kernels for 0%

profile of v5, /device:TPU:18, one launch (start us, length us, event | category | flops | bytes accessed | tf_op | source)
XLA Modules:
  0.0 146.7 jit_solution(8700506637803678426)
XLA Ops:
  6.6 1.1 fusion.22
  7.7 0.7 pad_maximum_fusion.5
  8.5 1.6 %fusion.20 = (f32[1,5,1,32,128]{4,3,2,1,0:T(8,128)}, f32[1,5,1,32,128]{4,3,2,1,0:T(8,128)}) fusion(f32[1,5,8,32,128]{4,3,2,1,0:T(8,128)} %param.7), kind=kLoop, calls=%fused_computation.88 | loop fusion | bytes 327680 | tf_op jit(solution)/shard_map/slice | solution.py:21
  10.1 1.9 %collective-permute-start = (f32[1,5,1,32,128]{4,3,2,1,0:T(8,128)}, f32[1,5,1,32,128]{4,3,2,1,0:T(8,128)}, u32[]{:S(2)}, u32[]{:S(2)}) collective-permute-start(f32[1,5,1,32,128]{4,3,2,1,0:T(8,128)} %get-tuple-element.12), channel_id=1, source_target_pairs={{1,0},{2,1},{3,2},{4,3},{5,4},{6,5},{7,6},{8,7},{9,8},{10,9},{11,1... | collective-permute-start | bytes 245768 | tf_op jit(solution)/shard_map/ppermute | solution.py:23
  12.0 2.4 %collective-permute-start.1 = (f32[1,5,1,32,128]{4,3,2,1,0:T(8,128)}, f32[1,5,1,32,128]{4,3,2,1,0:T(8,128)}, u32[]{:S(2)}, u32[]{:S(2)}) collective-permute-start(f32[1,5,1,32,128]{4,3,2,1,0:T(8,128)} %get-tuple-element.11), channel_id=1, source_target_pairs={{0,1},{1,2},{2,3},{3,4},{4,5},{5,6},{6,7},{7,8},{8,9},{9,10},{10,1... | collective-permute-start | bytes 245768 | tf_op jit(solution)/shard_map/ppermute | solution.py:20
  14.4 1.9 %slice_bitcast_fusion.1 = (f32[5,8,16,128]{3,2,1,0:T(8,128)}, f32[1,5,8,16,128]{4,3,2,1,0:T(8,128)}) fusion(f32[1,5,8,32,128]{4,3,2,1,0:T(8,128)} %param.7), kind=kLoop, calls=%fused_computation.86 | loop fusion | bytes 983040 | tf_op jit(solution)/shard_map/mul | solution.py:91
  16.3 6.2 %collective-permute-start.3 = (f32[1,5,8,16,128]{4,3,2,1,0:T(8,128)}, f32[1,5,8,16,128]{4,3,2,1,0:T(8,128)}, u32[]{:S(2)}, u32[]{:S(2)}) collective-permute-start(f32[1,5,8,16,128]{4,3,2,1,0:T(8,128)} %get-tuple-element.10), channel_id=1, source_target_pairs={{0,32},{32,0},{1,33},{33,1},{2,34},{34,2},{3,35},{35,3},{4,36},{36... | collective-permute-start | bytes 983048 | tf_op jit(solution)/shard_map/ppermute | solution.py:87
  22.7 0.7 fusion.28
  25.6 14.4 %collective-permute-done.3 = f32[1,5,8,16,128]{4,3,2,1,0:T(8,128)} collective-permute-done((f32[1,5,8,16,128]{4,3,2,1,0:T(8,128)}, f32[1,5,8,16,128]{4,3,2,1,0:T(8,128)}, u32[]{:S(2)}, u32[]{:S(2)}) %collective-permute-start.3) | collective-permute-done | bytes 327712 | tf_op jit(solution)/shard_map/ppermute | solution.py:87
  40.0 2.9 %multiply_add_fusion = f32[8,5,8,16,128]{4,3,2,1,0:T(8,128)} fusion(f32[5,8,16,128]{3,2,1,0:T(8,128)} %bitcast.93, f32[8]{0:T(128)S(1)} %get-tuple-element.106, f32[5,8,16,128]{3,2,1,0:T(8,128)S(1)} %copy-done.3, f32[8]{0:T(128)S(1)} %get-tuple-element.107), kind=kLoop, calls=%fused_computation.1 | loop fusion | flops 1966080 | bytes 3276864 | tf_op jit(solution)/shard_map/add | solution.py:91
  43.0 16.6 %all-gather.2.cloned.1.call-done = f32[8,5,8,16,128]{4,3,2,1,0:T(8,128)} async-done(((f32[1,5,8,16,128]{4,3,2,1,0:T(8,128)}), f32[8,5,8,16,128]{4,3,2,1,0:T(8,128)}) %all-gather.2.cloned.1.call-update) | async-done | bytes 2621456 | tf_op jit(solution)/shard_map/all_gather | solution.py:95
  59.6 2.2 %fusion.19 = (f32[8,5,8,1,128]{4,3,2,1,0:T(1,128)S(1)}, f32[8,5,8,1,128]{4,3,2,1,0:T(1,128)S(1)}) fusion(f32[8,5,8,16,128]{4,3,2,1,0:T(8,128)} %all-gather.2.cloned.1.call-done), kind=kLoop, calls=%fused_computation.87 | loop fusion | bytes 655360 | tf_op jit(solution)/shard_map/slice | solution.py:100
  61.9 2.1 %convolution_bitcast_fusion = f32[2,5,8,128,8]{3,4,1,2,0:T(8,128)S(1)} fusion(s32[2,8,128]{2,1,0:T(8,128)} %param.12, f32[1,8,5,8,128]{4,1,2,3,0:T(8,128)S(1)} %get-tuple-element.104, f32[1,8,5,8,128]{4,1,2,3,0:T(8,128)S(1)} %get-tuple-element.105), kind=kOutput, calls=%fused_computation.2 | convolution fusion | flops 126173184 | bytes 663552 | tf_op jit(solution)/shard_map/szvir,sikr->szvik/dot_general | solution.py:105
  64.7 5.7 %collective-permute-start.2 = (f32[92160]{0:T(1024)S(1)}, f32[92160]{0:T(1024)S(1)}, u32[]{:S(2)}, u32[]{:S(2)}) collective-permute-start(f32[92160]{0:T(1024)S(1)} %pad_maximum_fusion.4), channel_id=1, source_target_pairs={{0,32},{32,0},{1,33},{33,1},{2,34},{34,2},{3,35},{35,3},{4,36},{36... | collective-permute-start | bytes 1105928 | tf_op jit(solution)/shard_map/ppermute | solution.py:112
  71.4 1.0 subtract_multiply_fusion.2
  72.4 13.6 %collective-permute-done.2 = f32[92160]{0:T(1024)S(1)} collective-permute-done((f32[92160]{0:T(1024)S(1)}, f32[92160]{0:T(1024)S(1)}, u32[]{:S(2)}, u32[]{:S(2)}) %collective-permute-start.2) | collective-permute-done | bytes 368672 | tf_op jit(solution)/shard_map/ppermute | solution.py:112
  86.2 9.5 %add_dynamic-update-slice_fusion.4 = f32[1,5,8,32,128]{4,3,2,1,0:T(8,128)S(1)} fusion(f32[1,5,8,32,128]{4,3,2,1,0:T(8,128)S(1)} %subtract_multiply_fusion, f32[1,5,8,32,128]{4,3,2,1,0:T(8,128)S(1)} %subtract_multiply_fusion.1, f32[1,5,8,32,128]{4,3,2,1,0:T(8,128)S(1)} %subtract_multiply_fusion.2, f32[]{:T(128)} %bitcast.30, f32[]{:T(128)} %bitcast.29, ...), kind=kLoop, calls=%fused_computation.30 | loop fusion | flops 950271 | bytes 2097212
  95.8 9.7 %add_dynamic-update-slice_fusion.3 = f32[1,5,8,32,128]{4,3,2,1,0:T(8,128)S(1)} fusion(f32[1,5,8,32,128]{4,3,2,1,0:T(8,128)S(1)} %add_dynamic-update-slice_fusion.4, f32[1,5,8,32,128]{4,3,2,1,0:T(8,128)S(1)} %subtract_multiply_fusion, f32[1,5,8,32,128]{4,3,2,1,0:T(8,128)S(1)} %subtract_multiply_fusion.1, ...), kind=kLoop, calls=%fused_computation.29 | loop fusion | flops 950272 | bytes 2097212
  105.5 9.5 %add_dynamic-update-slice_fusion.2 = f32[1,5,8,32,128]{4,3,2,1,0:T(8,128)S(1)} fusion(f32[1,5,8,32,128]{4,3,2,1,0:T(8,128)S(1)} %add_dynamic-update-slice_fusion.3, f32[1,5,8,32,128]{4,3,2,1,0:T(8,128)S(1)} %subtract_multiply_fusion, f32[1,5,8,32,128]{4,3,2,1,0:T(8,128)S(1)} %subtract_multiply_fusion.1, ...), kind=kLoop, calls=%fused_computation.28 | loop fusion | flops 950272 | bytes 2097212
  115.0 9.8 %add_dynamic-update-slice_fusion.1 = f32[1,5,8,32,128]{4,3,2,1,0:T(8,128)S(1)} fusion(f32[1,5,8,32,128]{4,3,2,1,0:T(8,128)S(1)} %add_dynamic-update-slice_fusion.2, f32[1,5,8,32,128]{4,3,2,1,0:T(8,128)S(1)} %subtract_multiply_fusion, f32[1,5,8,32,128]{4,3,2,1,0:T(8,128)S(1)} %subtract_multiply_fusion.1, ...), kind=kLoop, calls=%fused_computation.27 | loop fusion | flops 950272 | bytes 2097212
  124.8 9.5 %add_dynamic-update-slice_fusion = f32[1,5,8,32,128]{4,3,2,1,0:T(8,128)S(1)} fusion(f32[1,5,8,32,128]{4,3,2,1,0:T(8,128)S(1)} %add_dynamic-update-slice_fusion.1, f32[1,5,8,32,128]{4,3,2,1,0:T(8,128)S(1)} %subtract_multiply_fusion, f32[1,5,8,32,128]{4,3,2,1,0:T(8,128)S(1)} %subtract_multiply_fusion.1, f32[1,5,8,32,128]{4,3,2,1,0:T(8,128)S(1)} %subtract_multiply_fusion.2, ...), kind=kLoop, calls=%fused_computation.26 | loop fusion | flops 950272 | bytes 2097212 | tf_op jit(solution)/shard_map/stack | solution.py:69
  134.3 2.3 %multiply_subtract_fusion = f32[1,5,8,32,128]{4,3,2,1,0:T(8,128)} fusion(f32[1,5,8,32,128]{4,3,2,1,0:T(8,128)S(1)} %add_dynamic-update-slice_fusion, f32[1,5,8,32,128]{4,3,2,1,0:T(8,128)S(1)} %copy-done, f32[1,5,8,32,127]{4,3,2,1,0:T(8,128)S(1)} %get-tuple-element.18, f32[1,5,8,32,127]{4,3,2,1,0:T(8,128)S(1)} %get-tuple-element.17, ...), kind=kLoop, calls=%fused_computation.12 | loop fusion | flops 2129920 | bytes 4872192 | tf_op jit(solution)/shard_map/sub | solution.py:71
  136.8 0.9 copy-done.2
  137.9 2.0 %fusion.3 = f32[1,5,8,32,128]{4,3,2,1,0:T(8,128)} fusion(f32[1,5,8,32,128]{4,3,2,1,0:T(8,128)S(1)} %copy-done.4, f32[1,5,8,32,128]{4,3,2,1,0:T(8,128)S(1)} %copy-done.2, f32[1,5,8,8,128]{4,3,2,1,0:T(8,128)S(1)} %get-tuple-element.20, f32[1,5,8,16,128]{4,3,2,1,0:T(8,128)} %reduce-scatter.2.cloned.1.call-done, f32[1,5,8,8,128]{4,3,2,1,0:T(8,128)S(1)} %get-tuple-element.19, ...), kind=kLoop, calls=%fused_computation.11 | loop fusion | flops 819200 | bytes 2752512 | tf_op jit(solution)/shard_map/sub | solution.py:128
  (53 shorter events, 4.6 us)
Async XLA Ops:
  6.5 18.6 %copy-start = (f32[1,5,8,32,128]{4,3,2,1,0:T(8,128)S(1)}, f32[1,5,8,32,128]{4,3,2,1,0:T(8,128)}, u32[]{:S(2)}) copy-start(f32[1,5,8,32,128]{4,3,2,1,0:T(8,128)} %param.7) | copy-start | bytes 1966084
  6.5 16.1 %copy-start.5 = (f32[3,5,5]{2,0,1:T(4,128)S(1)}, f32[3,5,5]{2,0,1:T(4,128)}, u32[]{:S(2)}) copy-start(f32[3,5,5]{2,0,1:T(4,128)} %param.11) | copy-start | bytes 904
  6.5 18.4 %copy-start.8 = (s32[1,2,8,128]{3,2,1,0:T(8,128)S(1)}, s32[1,2,8,128]{3,2,1,0:T(8,128)}, u32[]{:S(2)}) copy-start(s32[1,2,8,128]{3,2,1,0:T(8,128)} %param.13) | copy-start | bytes 24580
  6.5 18.6 %copy-start.7 = (f32[8,32,128]{2,1,0:T(8,128)S(1)}, f32[8,32,128]{2,1,0:T(8,128)}, u32[]{:S(2)}) copy-start(f32[8,32,128]{2,1,0:T(8,128)} %param.9) | copy-start | bytes 393220
  6.5 53.1 %all-gather.2.cloned.1.call-start = ((), (), s32[]{:S(2)}) async-start(), calls=%async_computation.1 | async-start | bytes 2949120 | tf_op jit(solution)/shard_map/all_gather | solution.py:95
  8.4 128.3 %reduce-scatter.2.cloned.1.call-start = ((), (), s32[]{:S(2)}) async-start(), calls=%async_computation.2 | async-start | bytes 2949120 | tf_op jit(solution)/shard_map/reduce_scatter | solution.py:92
  10.1 61.2 %collective-permute-start = (f32[1,5,1,32,128]{4,3,2,1,0:T(8,128)}, f32[1,5,1,32,128]{4,3,2,1,0:T(8,128)}, u32[]{:S(2)}, u32[]{:S(2)}) collective-permute-start(f32[1,5,1,32,128]{4,3,2,1,0:T(8,128)} %get-tuple-element.12), channel_id=1, source_target_pairs={{1,0},{2,1},{3,2},{4,3},{5,4},{6,5},{7,6},{8,7},{9,8},{10,9},{11,1... | collective-permute-start | bytes 245768 | tf_op jit(solution)/shard_map/ppermute | solution.py:23
  12.0 59.3 %collective-permute-start.1 = (f32[1,5,1,32,128]{4,3,2,1,0:T(8,128)}, f32[1,5,1,32,128]{4,3,2,1,0:T(8,128)}, u32[]{:S(2)}, u32[]{:S(2)}) collective-permute-start(f32[1,5,1,32,128]{4,3,2,1,0:T(8,128)} %get-tuple-element.11), channel_id=1, source_target_pairs={{0,1},{1,2},{2,3},{3,4},{4,5},{5,6},{6,7},{7,8},{8,9},{9,10},{10,1... | collective-permute-start | bytes 245768 | tf_op jit(solution)/shard_map/ppermute | solution.py:20
  16.3 23.7 %collective-permute-start.3 = (f32[1,5,8,16,128]{4,3,2,1,0:T(8,128)}, f32[1,5,8,16,128]{4,3,2,1,0:T(8,128)}, u32[]{:S(2)}, u32[]{:S(2)}) collective-permute-start(f32[1,5,8,16,128]{4,3,2,1,0:T(8,128)} %get-tuple-element.10), channel_id=1, source_target_pairs={{0,32},{32,0},{1,33},{33,1},{2,34},{34,2},{3,35},{35,3},{4,36},{36... | collective-permute-start | bytes 983048 | tf_op jit(solution)/shard_map/ppermute | solution.py:87
  25.1 14.9 %copy-start.3 = (f32[5,8,16,128]{3,2,1,0:T(8,128)S(1)}, f32[5,8,16,128]{3,2,1,0:T(8,128)}, u32[]{:S(2)}) copy-start(f32[5,8,16,128]{3,2,1,0:T(8,128)} %get-tuple-element.9) | copy-start | bytes 983044
  59.6 4.6 %copy-start.1 = (f32[8,5,8,16,128]{4,3,2,1,0:T(8,128)S(1)}, f32[8,5,8,16,128]{4,3,2,1,0:T(8,128)}, u32[]{:S(2)}) copy-start(f32[8,5,8,16,128]{4,3,2,1,0:T(8,128)} %all-gather.2.cloned.1.call-done) | copy-start | bytes 7864324
  64.7 21.3 %collective-permute-start.2 = (f32[92160]{0:T(1024)S(1)}, f32[92160]{0:T(1024)S(1)}, u32[]{:S(2)}, u32[]{:S(2)}) collective-permute-start(f32[92160]{0:T(1024)S(1)} %pad_maximum_fusion.4), channel_id=1, source_target_pairs={{0,32},{32,0},{1,33},{33,1},{2,34},{34,2},{3,35},{35,3},{4,36},{36... | collective-permute-start | bytes 1105928 | tf_op jit(solution)/shard_map/ppermute | solution.py:112
  115.0 19.3 %copy-start.6 = (f32[8,32,128]{2,1,0:T(8,128)S(1)}, f32[8,32,128]{2,1,0:T(8,128)}, u32[]{:S(2)}) copy-start(f32[8,32,128]{2,1,0:T(8,128)} %param.10) | copy-start | bytes 393220
  136.6 1.1 copy-start.2
  136.6 1.3 copy-start.4
Sparse Core Ops, SparseCore 0:
  9.5 50.1 all-gather.1
  62.5 45.8 reduce-scatter.1

commit v6 on v5

--- a/solution.py
+++ b/solution.py
@@ -58,15 +58,12 @@
     up_k = jnp.concatenate([state[..., 1:], zeros], axis=4)
     down_k = jnp.concatenate([zeros, state[..., :-1]], axis=4)
     diffs = [(up_i - down_i) * 0.5, (up_j - down_j) * 0.5, (up_k - down_k) * 0.5]
-    rows = []
-    for target in range(state.shape[1]):
-        total = None
-        for direction, diff in enumerate(diffs):
-            for source in range(state.shape[1]):
-                term = jacobians[direction, target, source] * diff[:, source]
-                total = term if total is None else total + term
-        rows.append(total)
-    flux = jnp.stack(rows, axis=1)
+    flux = None
+    for direction, diff in enumerate(diffs):
+        for source in range(state.shape[1]):
+            column = jacobians[direction, :, source].reshape((1, -1) + (1,) * (state.ndim - 2))
+            term = column * diff[:, source : source + 1]
+            flux = term if flux is None else flux + term
     laplace = up_i + down_i + up_j + down_j + up_k + down_k - 6.0 * state
     return flux - eddy_visc[None, None] * laplace
 

time: 148 us -> 118 us (0.80)
  the two profiles are of different devices: /device:TPU:18 before, /device:TPU:6 now
where the time goes in v6:
time: 118 us; the launch traced here: 117 us
  waiting for transfers between devices  57 us (48%)
  starting transfers between devices  19.4 us (16%)
  other arithmetic  14.4 us (12%)
  between operations  13.9 us (12%)
  local copies, waits for them, and re-layouts  10.3 us (9%)
  matrix products  2.13 us (2%)
    reduce_scatter x1, waiting for transfers between devices, per_device(): lax.psum_scatter(contributions, 'tz', scatter_dimension=0, tiled=True)  21.7 us
    all_gather x1, waiting for transfers between devices, per_device(): held = lax.all_gather(outer, 'tz', axis=0, tiled=True)  19.1 us
    ppermute x1, waiting for transfers between devices, per_device(): received = lax.ppermute(message, 'ty', swap)  8.46 us
    ppermute x1, waiting for transfers between devices, per_device(): other = lax.ppermute(inner, 'ty', swap)  7.7 us
    ppermute x1, starting transfers between devices, per_device(): received = lax.ppermute(message, 'ty', swap)  7.06 us
    ppermute x1, starting transfers between devices, extended_2(): lax.ppermute(lax.slice_in_dim(block, 0, width, axis=dim), axis, backward)  5.2 us
    ppermute x1, starting transfers between devices, per_device(): other = lax.ppermute(inner, 'ty', swap)  5.16 us
    sub x1, other arithmetic, section_spatial(): return flux - eddy_visc[None, None] * laplace  2.97 us
  transfers between devices with their start and end apart: 6, of which 4 were waited for; matrix products, arithmetic and copies ran while one was open for 19% of the time, Pallas kernels for 0%

profile of v6, /device:TPU:6, one launch (start us, length us, event | category | flops | bytes accessed | tf_op | source)
XLA Modules:
  0.0 117.0 jit_solution(7916101641822765204)
XLA Ops:
  6.5 1.1 fusion.22
  7.6 0.7 pad_maximum_fusion.5
  8.5 1.6 %fusion.20 = (f32[1,5,1,32,128]{4,3,2,1,0:T(8,128)}, f32[1,5,1,32,128]{4,3,2,1,0:T(8,128)}) fusion(f32[1,5,8,32,128]{4,3,2,1,0:T(8,128)} %param.7), kind=kLoop, calls=%fused_computation.113 | loop fusion | bytes 327680 | tf_op jit(solution)/shard_map/slice | solution.py:21
  10.1 5.2 %collective-permute-start = (f32[1,5,1,32,128]{4,3,2,1,0:T(8,128)}, f32[1,5,1,32,128]{4,3,2,1,0:T(8,128)}, u32[]{:S(2)}, u32[]{:S(2)}) collective-permute-start(f32[1,5,1,32,128]{4,3,2,1,0:T(8,128)} %get-tuple-element.42), channel_id=1, source_target_pairs={{1,0},{2,1},{3,2},{4,3},{5,4},{6,5},{7,6},{8,7},{9,8},{10,9},{11,1... | collective-permute-start | bytes 245768 | tf_op jit(solution)/shard_map/ppermute | solution.py:23
  15.3 1.9 %collective-permute-start.1 = (f32[1,5,1,32,128]{4,3,2,1,0:T(8,128)}, f32[1,5,1,32,128]{4,3,2,1,0:T(8,128)}, u32[]{:S(2)}, u32[]{:S(2)}) collective-permute-start(f32[1,5,1,32,128]{4,3,2,1,0:T(8,128)} %get-tuple-element.41), channel_id=1, source_target_pairs={{0,1},{1,2},{2,3},{3,4},{4,5},{5,6},{6,7},{7,8},{8,9},{9,10},{10,1... | collective-permute-start | bytes 245768 | tf_op jit(solution)/shard_map/ppermute | solution.py:20
  17.2 1.9 %slice_bitcast_fusion.16 = (f32[5,8,16,128]{3,2,1,0:T(8,128)}, f32[1,5,8,16,128]{4,3,2,1,0:T(8,128)}) fusion(f32[1,5,8,32,128]{4,3,2,1,0:T(8,128)} %param.7), kind=kLoop, calls=%fused_computation.111 | loop fusion | bytes 983040 | tf_op jit(solution)/shard_map/mul | solution.py:88
  19.1 5.2 %collective-permute-start.3 = (f32[1,5,8,16,128]{4,3,2,1,0:T(8,128)}, f32[1,5,8,16,128]{4,3,2,1,0:T(8,128)}, u32[]{:S(2)}, u32[]{:S(2)}) collective-permute-start(f32[1,5,8,16,128]{4,3,2,1,0:T(8,128)} %get-tuple-element.25), channel_id=1, source_target_pairs={{0,32},{32,0},{1,33},{33,1},{2,34},{34,2},{3,35},{35,3},{4,36},{36... | collective-permute-start | bytes 983048 | tf_op jit(solution)/shard_map/ppermute | solution.py:84
  24.6 1.1 subtract_multiply_fusion
  25.9 0.7 compare_convert_fusion
  26.6 0.7 broadcast_multiply_fusion
  27.5 7.7 %collective-permute-done.3 = f32[1,5,8,16,128]{4,3,2,1,0:T(8,128)} collective-permute-done((f32[1,5,8,16,128]{4,3,2,1,0:T(8,128)}, f32[1,5,8,16,128]{4,3,2,1,0:T(8,128)}, u32[]{:S(2)}, u32[]{:S(2)}) %collective-permute-start.3) | collective-permute-done | bytes 327712 | tf_op jit(solution)/shard_map/ppermute | solution.py:84
  35.2 2.9 %multiply_add_fusion = f32[8,5,8,16,128]{4,3,2,1,0:T(8,128)} fusion(f32[5,8,16,128]{3,2,1,0:T(8,128)} %bitcast.33, f32[8]{0:T(128)S(1)} %get-tuple-element.61, f32[5,8,16,128]{3,2,1,0:T(8,128)S(1)} %copy-done.3, f32[8]{0:T(128)S(1)} %get-tuple-element.62), kind=kLoop, calls=%fused_computation.1 | loop fusion | flops 1966080 | bytes 3276864 | tf_op jit(solution)/shard_map/add | solution.py:88
  38.2 0.9 slice_reduce_fusion.14
  39.1 1.9 %slice_bitcast_fusion.4 = (f32[8,32,128]{2,1,0:T(8,128)S(1)}, f32[8,32,128]{2,1,0:T(8,128)S(1)}, f32[8,32,128]{2,1,0:T(8,128)}, f32[8,32,128]{2,1,0:T(8,128)}, f32[8,32,128]{2,1,0:T(8,128)}) fusion(f32[1,5,8,32,128]{4,3,2,1,0:T(8,128)} %subtract_multiply_fusion), kind=kLoop, calls=%fused_computation.30 | loop fusion | bytes 1310720 | tf_op jit(solution)/shard_map/mul | solution.py:65
  41.0 19.1 %all-gather.2.cloned.1.call-done = f32[8,5,8,16,128]{4,3,2,1,0:T(8,128)} async-done(((f32[1,5,8,16,128]{4,3,2,1,0:T(8,128)}), f32[8,5,8,16,128]{4,3,2,1,0:T(8,128)}) %all-gather.2.cloned.1.call-update) | async-done | bytes 2621456 | tf_op jit(solution)/shard_map/all_gather | solution.py:92
  60.1 2.2 %fusion.19 = (f32[8,5,8,1,128]{4,3,2,1,0:T(1,128)S(1)}, f32[8,5,8,1,128]{4,3,2,1,0:T(1,128)S(1)}) fusion(f32[8,5,8,16,128]{4,3,2,1,0:T(8,128)} %all-gather.2.cloned.1.call-done), kind=kLoop, calls=%fused_computation.112 | loop fusion | bytes 655360 | tf_op jit(solution)/shard_map/slice | solution.py:97
  62.3 2.1 %convolution_bitcast_fusion = f32[2,5,8,128,8]{3,4,1,2,0:T(8,128)S(1)} fusion(s32[2,8,128]{2,1,0:T(8,128)} %param.12, f32[1,8,5,8,128]{4,1,2,3,0:T(8,128)S(1)} %get-tuple-element.59, f32[1,8,5,8,128]{4,1,2,3,0:T(8,128)S(1)} %get-tuple-element.60), kind=kOutput, calls=%fused_computation.2 | convolution fusion | flops 126173184 | bytes 663552 | tf_op jit(solution)/shard_map/szvir,sikr->szvik/dot_general | solution.py:102
  64.5 1.1 multiply_reduce_fusion.1
  66.1 7.1 %collective-permute-start.2 = (f32[92160]{0:T(1024)S(1)}, f32[92160]{0:T(1024)S(1)}, u32[]{:S(2)}, u32[]{:S(2)}) collective-permute-start(f32[92160]{0:T(1024)S(1)} %pad_maximum_fusion.4), channel_id=1, source_target_pairs={{0,32},{32,0},{1,33},{33,1},{2,34},{34,2},{3,35},{35,3},{4,36},{36... | collective-permute-start | bytes 1105928 | tf_op jit(solution)/shard_map/ppermute | solution.py:109
  73.2 1.0 subtract_multiply_fusion.2
  74.5 8.5 %collective-permute-done.2 = f32[92160]{0:T(1024)S(1)} collective-permute-done((f32[92160]{0:T(1024)S(1)}, f32[92160]{0:T(1024)S(1)}, u32[]{:S(2)}, u32[]{:S(2)}) %collective-permute-start.2) | collective-permute-done | bytes 368672 | tf_op jit(solution)/shard_map/ppermute | solution.py:109
  83.4 3.0 %multiply_subtract_fusion = f32[1,5,8,32,128]{4,3,2,1,0:T(8,128)} fusion(f32[1,5,8,32,128]{4,3,2,1,0:T(8,128)S(1)} %copy-done, f32[1,5,8,32,127]{4,3,2,1,0:T(8,128)S(1)} %get-tuple-element.48, f32[1,5,8,32,127]{4,3,2,1,0:T(8,128)S(1)} %get-tuple-element.47, f32[1,5,8,31,128]{4,3,2,1,0:T(8,128)S(1)} %get-tuple-element.44, ...), kind=kLoop, calls=%fused_computation.12 | loop fusion | flops 6881280 | bytes 6183212 | tf_op jit(solution)/shard_map/sub | solution.py:68
  86.5 21.7 %reduce-scatter.2.cloned.1.call-done = f32[1,5,8,16,128]{4,3,2,1,0:T(8,128)} async-done(((f32[8,5,8,16,128]{4,3,2,1,0:T(8,128)}), f32[1,5,8,16,128]{4,3,2,1,0:T(8,128)}) %reduce-scatter.2.cloned.1.call-update) | async-done | bytes 327696 | tf_op jit(solution)/shard_map/reduce_scatter | solution.py:89
  108.2 2.0 %fusion.3 = f32[1,5,8,32,128]{4,3,2,1,0:T(8,128)} fusion(f32[1,5,8,32,128]{4,3,2,1,0:T(8,128)S(1)} %copy-done.4, f32[1,5,8,32,128]{4,3,2,1,0:T(8,128)S(1)} %copy-done.2, f32[1,5,8,8,128]{4,3,2,1,0:T(8,128)S(1)} %get-tuple-element.50, f32[1,5,8,16,128]{4,3,2,1,0:T(8,128)} %reduce-scatter.2.cloned.1.call-done, f32[1,5,8,8,128]{4,3,2,1,0:T(8,128)S(1)} %get-tuple-element.49, ...), kind=kLoop, calls=%fused_computation.11 | loop fusion | flops 819200 | bytes 2752512 | tf_op jit(solution)/shard_map/sub | solution.py:125
  (78 shorter events, 1.9 us)
Async XLA Ops:
  6.5 17.8 %copy-start = (f32[1,5,8,32,128]{4,3,2,1,0:T(8,128)S(1)}, f32[1,5,8,32,128]{4,3,2,1,0:T(8,128)}, u32[]{:S(2)}) copy-start(f32[1,5,8,32,128]{4,3,2,1,0:T(8,128)} %param.7) | copy-start | bytes 1966084
  6.5 53.6 %all-gather.2.cloned.1.call-start = ((), (), s32[]{:S(2)}) async-start(), calls=%async_computation.1 | async-start | bytes 2949120 | tf_op jit(solution)/shard_map/all_gather | solution.py:92
  8.4 99.7 %reduce-scatter.2.cloned.1.call-start = ((), (), s32[]{:S(2)}) async-start(), calls=%async_computation.2 | async-start | bytes 2949120 | tf_op jit(solution)/shard_map/reduce_scatter | solution.py:89
  10.1 63.1 %collective-permute-start = (f32[1,5,1,32,128]{4,3,2,1,0:T(8,128)}, f32[1,5,1,32,128]{4,3,2,1,0:T(8,128)}, u32[]{:S(2)}, u32[]{:S(2)}) collective-permute-start(f32[1,5,1,32,128]{4,3,2,1,0:T(8,128)} %get-tuple-element.42), channel_id=1, source_target_pairs={{1,0},{2,1},{3,2},{4,3},{5,4},{6,5},{7,6},{8,7},{9,8},{10,9},{11,1... | collective-permute-start | bytes 245768 | tf_op jit(solution)/shard_map/ppermute | solution.py:23
  15.3 10.5 %copy-start.11 = (s32[1,2,8,128]{3,2,1,0:T(8,128)S(1)}, s32[1,2,8,128]{3,2,1,0:T(8,128)}, u32[]{:S(2)}) copy-start(s32[1,2,8,128]{3,2,1,0:T(8,128)} %param.13) | copy-start | bytes 24580
  15.3 57.9 %collective-permute-start.1 = (f32[1,5,1,32,128]{4,3,2,1,0:T(8,128)}, f32[1,5,1,32,128]{4,3,2,1,0:T(8,128)}, u32[]{:S(2)}, u32[]{:S(2)}) collective-permute-start(f32[1,5,1,32,128]{4,3,2,1,0:T(8,128)} %get-tuple-element.41), channel_id=1, source_target_pairs={{0,1},{1,2},{2,3},{3,4},{4,5},{5,6},{6,7},{7,8},{8,9},{9,10},{10,1... | collective-permute-start | bytes 245768 | tf_op jit(solution)/shard_map/ppermute | solution.py:20
  19.1 16.1 %collective-permute-start.3 = (f32[1,5,8,16,128]{4,3,2,1,0:T(8,128)}, f32[1,5,8,16,128]{4,3,2,1,0:T(8,128)}, u32[]{:S(2)}, u32[]{:S(2)}) collective-permute-start(f32[1,5,8,16,128]{4,3,2,1,0:T(8,128)} %get-tuple-element.25), channel_id=1, source_target_pairs={{0,32},{32,0},{1,33},{33,1},{2,34},{34,2},{3,35},{35,3},{4,36},{36... | collective-permute-start | bytes 983048 | tf_op jit(solution)/shard_map/ppermute | solution.py:84
  24.6 10.6 %copy-start.3 = (f32[5,8,16,128]{3,2,1,0:T(8,128)S(1)}, f32[5,8,16,128]{3,2,1,0:T(8,128)}, u32[]{:S(2)}) copy-start(f32[5,8,16,128]{3,2,1,0:T(8,128)} %get-tuple-element.24) | copy-start | bytes 983044
  66.1 16.8 %collective-permute-start.2 = (f32[92160]{0:T(1024)S(1)}, f32[92160]{0:T(1024)S(1)}, u32[]{:S(2)}, u32[]{:S(2)}) collective-permute-start(f32[92160]{0:T(1024)S(1)} %pad_maximum_fusion.4), channel_id=1, source_target_pairs={{0,32},{32,0},{1,33},{33,1},{2,34},{34,2},{3,35},{35,3},{4,36},{36... | collective-permute-start | bytes 1105928 | tf_op jit(solution)/shard_map/ppermute | solution.py:109
  74.2 9.0 %copy-start.5 = (f32[8,32,128]{2,1,0:T(8,128)S(1)}, f32[8,32,128]{2,1,0:T(8,128)}, u32[]{:S(2)}) copy-start(f32[8,32,128]{2,1,0:T(8,128)} %get-tuple-element.38) | copy-start | bytes 393220
  74.2 9.0 %copy-start.6 = (f32[8,32,128]{2,1,0:T(8,128)S(1)}, f32[8,32,128]{2,1,0:T(8,128)}, u32[]{:S(2)}) copy-start(f32[8,32,128]{2,1,0:T(8,128)} %get-tuple-element.39) | copy-start | bytes 393220
  74.3 9.0 %copy-start.7 = (f32[8,32,128]{2,1,0:T(8,128)S(1)}, f32[8,32,128]{2,1,0:T(8,128)}, u32[]{:S(2)}) copy-start(f32[8,32,128]{2,1,0:T(8,128)} %get-tuple-element.40) | copy-start | bytes 393220
  74.3 9.0 %copy-start.9 = (f32[8,32,128]{2,1,0:T(8,128)S(1)}, f32[8,32,128]{2,1,0:T(8,128)}, u32[]{:S(2)}) copy-start(f32[8,32,128]{2,1,0:T(8,128)} %param.10) | copy-start | bytes 393220
  74.3 9.0 %copy-start.12 = (f32[5]{0:T(128)S(1)}, f32[5]{0:T(128)}, u32[]{:S(2)}) copy-start(f32[5]{0:T(128)} %get-tuple-element.8) | copy-start | bytes 64
  74.3 9.0 %copy-start.13 = (f32[5]{0:T(128)S(1)}, f32[5]{0:T(128)}, u32[]{:S(2)}) copy-start(f32[5]{0:T(128)} %get-tuple-element.9) | copy-start | bytes 64
  74.3 9.0 %copy-start.14 = (f32[5]{0:T(128)S(1)}, f32[5]{0:T(128)}, u32[]{:S(2)}) copy-start(f32[5]{0:T(128)} %get-tuple-element.10) | copy-start | bytes 64
  74.3 9.0 %copy-start.15 = (f32[5]{0:T(128)S(1)}, f32[5]{0:T(128)}, u32[]{:S(2)}) copy-start(f32[5]{0:T(128)} %get-tuple-element.11) | copy-start | bytes 64
  74.3 9.0 %copy-start.16 = (f32[5]{0:T(128)S(1)}, f32[5]{0:T(128)}, u32[]{:S(2)}) copy-start(f32[5]{0:T(128)} %get-tuple-element.12) | copy-start | bytes 64
  74.3 9.0 %copy-start.17 = (f32[5]{0:T(128)S(1)}, f32[5]{0:T(128)}, u32[]{:S(2)}) copy-start(f32[5]{0:T(128)} %get-tuple-element.13) | copy-start | bytes 64
  74.3 9.0 %copy-start.18 = (f32[5]{0:T(128)S(1)}, f32[5]{0:T(128)}, u32[]{:S(2)}) copy-start(f32[5]{0:T(128)} %get-tuple-element.14) | copy-start | bytes 64
  74.3 9.0 %copy-start.19 = (f32[5]{0:T(128)S(1)}, f32[5]{0:T(128)}, u32[]{:S(2)}) copy-start(f32[5]{0:T(128)} %get-tuple-element.15) | copy-start | bytes 64
  74.4 9.0 %copy-start.20 = (f32[5]{0:T(128)S(1)}, f32[5]{0:T(128)}, u32[]{:S(2)}) copy-start(f32[5]{0:T(128)} %get-tuple-element.16) | copy-start | bytes 64
  86.4 21.8 %copy-start.2 = (f32[1,5,8,32,128]{4,3,2,1,0:T(8,128)S(1)}, f32[1,5,8,32,128]{4,3,2,1,0:T(8,128)}, u32[]{:S(2)}) copy-start(f32[1,5,8,32,128]{4,3,2,1,0:T(8,128)} %multiply_subtract_fusion) | copy-start | bytes 1966084
  86.4 21.8 %copy-start.4 = (f32[1,5,8,32,128]{4,3,2,1,0:T(8,128)S(1)}, f32[1,5,8,32,128]{4,3,2,1,0:T(8,128)}, u32[]{:S(2)}) copy-start(f32[1,5,8,32,128]{4,3,2,1,0:T(8,128)} %param.8) | copy-start | bytes 1966084
  (6 other events, 43.0 us)
Sparse Core Ops, SparseCore 0:
  9.4 50.6 all-gather.1
  63.0 45.1 reduce-scatter.1

commit v7 on v6

--- a/solution.py
+++ b/solution.py
@@ -68,6 +68,35 @@
     return flux - eddy_visc[None, None] * laplace
 
 
+def reduced_along_z(own_block, partner_block, y, total_count):
+    ring = lax.axis_size("tz")
+    forward = [(i, (i + 1) % ring) for i in range(ring)]
+    backward = [(i, (i - 1) % ring) for i in range(ring)]
+    offsets = jnp.arange(ring, dtype=jnp.int32)
+    expand = (ring,) + (1,) * own_block.ndim
+    own_weights = time_weights(Y_PARTS * offsets, total_count).reshape(expand)
+    partner_weights = time_weights(Y_PARTS * offsets + 2 * y - 1, total_count).reshape(expand)
+    terms = own_weights * own_block[None] + partner_weights * partner_block[None]
+    half = own_block.shape[2] // 2
+    depth = ring // 2
+
+    def addend(first, second):
+        return jnp.concatenate([terms[first][:, :, :half], terms[second][:, :, half:]], axis=2)
+
+    ahead = None
+    behind = None
+    for step in range(1, depth):
+        sent = addend(depth - step + 1, depth - step)
+        ahead = lax.ppermute(sent if ahead is None else ahead + sent, "tz", forward)
+        sent = addend(ring - depth + step, ring - depth - 1 + step)
+        behind = lax.ppermute(sent if behind is None else behind + sent, "tz", backward)
+    far_ahead = lax.ppermute(ahead[:, :, :half] + terms[1][:, :, :half], "tz", forward)
+    far_behind = lax.ppermute(behind[:, :, half:] + terms[ring - 1][:, :, half:], "tz", backward)
+    first = far_ahead + behind[:, :, :half]
+    second = ahead[:, :, half:] + far_behind
+    return terms[0] + jnp.concatenate([first, second], axis=2)
+
+
 def per_device(state, base, pseudo_step, eddy_visc, jacobians, partner_radial, partner_instance):
     ring = lax.axis_size("tz")
     total_count = ring * Y_PARTS
@@ -82,11 +111,7 @@
 
     inner = state[:, :, :, edge : pitch - edge]
     other = lax.ppermute(inner, "ty", swap)
-    expand = (ring,) + (1,) * (inner.ndim - 1)
-    own_weights = time_weights(ring_ids - own, total_count).reshape(expand)
-    partner_weights = time_weights(ring_ids - partner, total_count).reshape(expand)
-    contributions = own_weights * inner + partner_weights * other
-    inner_term = lax.psum_scatter(contributions, "tz", scatter_dimension=0, tiled=True)
+    inner_term = reduced_along_z(inner, other, y, total_count)
 
     outer = jnp.concatenate([state[:, :, :, :edge], state[:, :, :, pitch - edge :]], axis=3)
     held = lax.all_gather(outer, "tz", axis=0, tiled=True)

time: 118 us -> 141 us (1.19)
  the two profiles are of different devices: /device:TPU:6 before, /device:TPU:26 now
where the time goes in v7:
time: 141 us; the launch traced here: 140 us
  waiting for transfers between devices  56 us (40%)
  starting transfers between devices  44.5 us (32%)
  between operations  14.3 us (10%)
  local copies, waits for them, and re-layouts  13 us (9%)
  other arithmetic  10.5 us (7%)
  matrix products  2.13 us (2%)
    ppermute x3, waiting for transfers between devices, reduced_along_z(): ahead = lax.ppermute(sent if ahead is None else ahead + sent, 'tz', forward)  23.8 us
    ppermute x3, starting transfers between devices, reduced_along_z(): lax.ppermute(sent if behind is None else behind + sent, 'tz', backward)  18.8 us
    ppermute x1, waiting for transfers between devices, per_device(): received = lax.ppermute(message, 'ty', swap)  17.3 us
    ppermute x1, waiting for transfers between devices, per_device(): other = lax.ppermute(inner, 'ty', swap)  9.19 us
    ppermute x3, starting transfers between devices, reduced_along_z(): ahead = lax.ppermute(sent if ahead is None else ahead + sent, 'tz', forward)  8.13 us
    ppermute x1, waiting for transfers between devices, reduced_along_z(): lax.ppermute(ahead[:, :, :half] + terms[1][:, :, :half], 'tz', forward)  5.63 us
    ppermute x1, starting transfers between devices, per_device(): other = lax.ppermute(inner, 'ty', swap)  5.45 us
    ppermute x1, starting transfers between devices, per_device(): received = lax.ppermute(message, 'ty', swap)  3.97 us
  transfers between devices with their start and end apart: 13, of which 6 were waited for; matrix products, arithmetic and copies ran while one was open for 14% of the time, Pallas kernels for 0%

profile of v7, /device:TPU:26, one launch (start us, length us, event | category | flops | bytes accessed | tf_op | source)
XLA Modules:
  0.0 140.5 jit_solution(9456971820608461801)
XLA Ops:
  8.4 1.6 %fusion.22 = (f32[1,5,1,32,128]{4,3,2,1,0:T(8,128)}, f32[1,5,1,32,128]{4,3,2,1,0:T(8,128)}) fusion(f32[1,5,8,32,128]{4,3,2,1,0:T(8,128)} %param.7), kind=kLoop, calls=%fused_computation.133 | loop fusion | bytes 327680 | tf_op jit(solution)/shard_map/slice | solution.py:21
  10.1 1.9 %collective-permute-start = (f32[1,5,1,32,128]{4,3,2,1,0:T(8,128)}, f32[1,5,1,32,128]{4,3,2,1,0:T(8,128)S(1)}, u32[]{:S(2)}, u32[]{:S(2)}) collective-permute-start(f32[1,5,1,32,128]{4,3,2,1,0:T(8,128)} %get-tuple-element.49), channel_id=1, source_target_pairs={{1,0},{2,1},{3,2},{4,3},{5,4},{6,5},{7,6},{8,7},{9,8},{10,9},{11,1... | collective-permute-start | bytes 245768 | tf_op jit(solution)/shard_map/ppermute | solution.py:23
  12.0 2.4 %collective-permute-start.1 = (f32[1,5,1,32,128]{4,3,2,1,0:T(8,128)}, f32[1,5,1,32,128]{4,3,2,1,0:T(8,128)S(1)}, u32[]{:S(2)}, u32[]{:S(2)}) collective-permute-start(f32[1,5,1,32,128]{4,3,2,1,0:T(8,128)} %get-tuple-element.48), channel_id=1, source_target_pairs={{0,1},{1,2},{2,3},{3,4},{4,5},{5,6},{6,7},{7,8},{8,9},{9,10},{10,1... | collective-permute-start | bytes 245768 | tf_op jit(solution)/shard_map/ppermute | solution.py:20
  14.4 1.8 %slice_bitcast_fusion.24 = (f32[5,8,16,128]{3,2,1,0:T(8,128)}, f32[1,5,8,16,128]{4,3,2,1,0:T(8,128)S(1)}) fusion(f32[1,5,8,32,128]{4,3,2,1,0:T(8,128)} %param.7), kind=kLoop, calls=%fused_computation.131 | loop fusion | bytes 983040 | tf_op jit(solution)/shard_map/mul | solution.py:79
  16.2 5.4 %collective-permute-start.3 = (f32[1,5,8,16,128]{4,3,2,1,0:T(8,128)S(1)}, f32[1,5,8,16,128]{4,3,2,1,0:T(8,128)S(1)}, u32[]{:S(2)}, u32[]{:S(2)}) collective-permute-start(f32[1,5,8,16,128]{4,3,2,1,0:T(8,128)S(1)} %get-tuple-element.32), channel_id=1, source_target_pairs={{0,32},{32,0},{1,33},{33,1},{2,34},{34,2},{3,35},{35,3},{4,36},{36... | collective-permute-start | bytes 983048 | tf_op jit(solution)/shard_map/ppermute | solution.py:113
  27.0 9.2 %collective-permute-done.3 = f32[1,5,8,16,128]{4,3,2,1,0:T(8,128)S(1)} collective-permute-done((f32[1,5,8,16,128]{4,3,2,1,0:T(8,128)S(1)}, f32[1,5,8,16,128]{4,3,2,1,0:T(8,128)S(1)}, u32[]{:S(2)}, u32[]{:S(2)}) %collective-permute-start.3) | collective-permute-done | bytes 327712 | tf_op jit(solution)/shard_map/ppermute | solution.py:113
  36.9 1.4 multiply_add_fusion
  38.6 4.3 %collective-permute-start.4 = (f32[1,5,8,16,128]{4,3,2,1,0:T(8,128)S(1)}, f32[1,5,8,16,128]{4,3,2,1,0:T(8,128)S(1)}, u32[]{:S(2)}, u32[]{:S(2)}) collective-permute-start(f32[1,5,8,16,128]{4,3,2,1,0:T(8,128)S(1)} %pad_maximum_fusion.6), channel_id=1, source_target_pairs={{0,64},{64,128},{128,192},{192,256},{256,320},{320,384},{384,448},... | collective-permute-start | bytes 983048 | tf_op jit(solution)/shard_map/ppermute | solution.py:90
  42.9 8.6 %collective-permute-start.8 = (f32[1,5,8,16,128]{4,3,2,1,0:T(8,128)S(1)}, f32[1,5,8,16,128]{4,3,2,1,0:T(8,128)S(1)}, u32[]{:S(2)}, u32[]{:S(2)}) collective-permute-start(f32[1,5,8,16,128]{4,3,2,1,0:T(8,128)S(1)} %pad_maximum_fusion.7), channel_id=1, source_target_pairs={{0,448},{64,0},{128,64},{192,128},{256,192},{320,256},{384,320},{4... | collective-permute-start | bytes 983048 | tf_op jit(solution)/shard_map/ppermute | solution.py:92
  51.6 12.1 %collective-permute-done.4 = f32[1,5,8,16,128]{4,3,2,1,0:T(8,128)S(1)} collective-permute-done((f32[1,5,8,16,128]{4,3,2,1,0:T(8,128)S(1)}, f32[1,5,8,16,128]{4,3,2,1,0:T(8,128)S(1)}, u32[]{:S(2)}, u32[]{:S(2)}) %collective-permute-start.4) | collective-permute-done | bytes 327712 | tf_op jit(solution)/shard_map/ppermute | solution.py:90
  63.7 1.9 %collective-permute-start.5 = (f32[1,5,8,16,128]{4,3,2,1,0:T(8,128)S(1)}, f32[1,5,8,16,128]{4,3,2,1,0:T(8,128)S(1)}, u32[]{:S(2)}, u32[]{:S(2)}) collective-permute-start(f32[1,5,8,16,128]{4,3,2,1,0:T(8,128)S(1)} %maximum_add_fusion.1), channel_id=1, source_target_pairs={{0,64},{64,128},{128,192},{192,256},{256,320},{320,384},{384,448},... | collective-permute-start | bytes 983048 | tf_op jit(solution)/shard_map/ppermute | solution.py:90
  65.7 5.1 %collective-permute-start.9 = (f32[1,5,8,16,128]{4,3,2,1,0:T(8,128)S(1)}, f32[1,5,8,16,128]{4,3,2,1,0:T(8,128)S(1)}, u32[]{:S(2)}, u32[]{:S(2)}) collective-permute-start(f32[1,5,8,16,128]{4,3,2,1,0:T(8,128)S(1)} %maximum_add_fusion.3), channel_id=1, source_target_pairs={{0,448},{64,0},{128,64},{192,128},{256,192},{320,256},{384,320},{4... | collective-permute-start | bytes 983048 | tf_op jit(solution)/shard_map/ppermute | solution.py:92
  70.9 6.3 %collective-permute-done.5 = f32[1,5,8,16,128]{4,3,2,1,0:T(8,128)S(1)} collective-permute-done((f32[1,5,8,16,128]{4,3,2,1,0:T(8,128)S(1)}, f32[1,5,8,16,128]{4,3,2,1,0:T(8,128)S(1)}, u32[]{:S(2)}, u32[]{:S(2)}) %collective-permute-start.5) | collective-permute-done | bytes 327712 | tf_op jit(solution)/shard_map/ppermute | solution.py:90
  77.2 1.9 %collective-permute-start.6 = (f32[1,5,8,16,128]{4,3,2,1,0:T(8,128)S(1)}, f32[1,5,8,16,128]{4,3,2,1,0:T(8,128)S(1)}, u32[]{:S(2)}, u32[]{:S(2)}) collective-permute-start(f32[1,5,8,16,128]{4,3,2,1,0:T(8,128)S(1)} %maximum_add_fusion.2), channel_id=1, source_target_pairs={{0,64},{64,128},{128,192},{192,256},{256,320},{320,384},{384,448},... | collective-permute-start | bytes 983048 | tf_op jit(solution)/shard_map/ppermute | solution.py:90
  79.4 5.1 %collective-permute-start.10 = (f32[1,5,8,16,128]{4,3,2,1,0:T(8,128)S(1)}, f32[1,5,8,16,128]{4,3,2,1,0:T(8,128)S(1)}, u32[]{:S(2)}, u32[]{:S(2)}) collective-permute-start(f32[1,5,8,16,128]{4,3,2,1,0:T(8,128)S(1)} %maximum_add_fusion.4), channel_id=1, source_target_pairs={{0,448},{64,0},{128,64},{192,128},{256,192},{320,256},{384,320},{4... | collective-permute-start | bytes 983048 | tf_op jit(solution)/shard_map/ppermute | solution.py:92
  84.5 5.4 %collective-permute-done.6 = f32[1,5,8,16,128]{4,3,2,1,0:T(8,128)S(1)} collective-permute-done((f32[1,5,8,16,128]{4,3,2,1,0:T(8,128)S(1)}, f32[1,5,8,16,128]{4,3,2,1,0:T(8,128)S(1)}, u32[]{:S(2)}, u32[]{:S(2)}) %collective-permute-start.6) | collective-permute-done | bytes 327712 | tf_op jit(solution)/shard_map/ppermute | solution.py:90
  89.9 1.9 %collective-permute-start.7 = (f32[1,5,4,16,128]{4,3,2,1,0:T(8,128)S(1)}, f32[1,5,4,16,128]{4,3,2,1,0:T(8,128)S(1)}, u32[]{:S(2)}, u32[]{:S(2)}) collective-permute-start(f32[1,5,4,16,128]{4,3,2,1,0:T(8,128)S(1)} %slice_add_fusion.4), channel_id=1, source_target_pairs={{0,64},{64,128},{128,192},{192,256},{256,320},{320,384},{384,448},... | collective-permute-start | bytes 491528 | tf_op jit(solution)/shard_map/ppermute | solution.py:93
  92.7 5.6 %collective-permute-done.7 = f32[1,5,4,16,128]{4,3,2,1,0:T(8,128)S(1)} collective-permute-done((f32[1,5,4,16,128]{4,3,2,1,0:T(8,128)S(1)}, f32[1,5,4,16,128]{4,3,2,1,0:T(8,128)S(1)}, u32[]{:S(2)}, u32[]{:S(2)}) %collective-permute-start.7) | collective-permute-done | bytes 163872 | tf_op jit(solution)/shard_map/ppermute | solution.py:93
  99.1 1.9 %collective-permute-start.11 = (f32[1,5,4,16,128]{4,3,2,1,0:T(8,128)}, f32[1,5,4,16,128]{4,3,2,1,0:T(8,128)}, u32[]{:S(2)}, u32[]{:S(2)}) collective-permute-start(f32[1,5,4,16,128]{4,3,2,1,0:T(8,128)} %get-tuple-element.59), channel_id=1, source_target_pairs={{0,448},{64,0},{128,64},{192,128},{256,192},{320,256},{384,320},{4... | collective-permute-start | bytes 491528 | tf_op jit(solution)/shard_map/ppermute | solution.py:94
  101.0 2.2 %fusion.21 = (f32[8,5,8,1,128]{4,3,2,1,0:T(1,128)S(1)}, f32[8,5,8,1,128]{4,3,2,1,0:T(1,128)S(1)}) fusion(f32[8,5,8,16,128]{4,3,2,1,0:T(8,128)} %all-gather.2.cloned.1.call-done), kind=kLoop, calls=%fused_computation.132 | loop fusion | bytes 655360 | tf_op jit(solution)/shard_map/slice | solution.py:122
  103.3 2.1 %convolution_bitcast_fusion = f32[2,5,8,128,8]{3,4,1,2,0:T(8,128)S(1)} fusion(s32[2,8,128]{2,1,0:T(8,128)} %param.12, f32[1,8,5,8,128]{4,1,2,3,0:T(8,128)S(1)} %get-tuple-element.78, f32[1,8,5,8,128]{4,1,2,3,0:T(8,128)S(1)} %get-tuple-element.79), kind=kOutput, calls=%fused_computation.2 | convolution fusion | flops 126173184 | bytes 663552 | tf_op jit(solution)/shard_map/szvir,sikr->szvik/dot_general | solution.py:127
  107.3 4.0 %collective-permute-start.2 = (f32[92160]{0:T(1024)S(1)}, f32[92160]{0:T(1024)S(1)}, u32[]{:S(2)}, u32[]{:S(2)}) collective-permute-start(f32[92160]{0:T(1024)S(1)} %pad_maximum_fusion.4), channel_id=1, source_target_pairs={{0,32},{32,0},{1,33},{33,1},{2,34},{34,2},{3,35},{35,3},{4,36},{36... | collective-permute-start | bytes 1105928 | tf_op jit(solution)/shard_map/ppermute | solution.py:134
  112.3 17.3 %collective-permute-done.2 = f32[92160]{0:T(1024)S(1)} collective-permute-done((f32[92160]{0:T(1024)S(1)}, f32[92160]{0:T(1024)S(1)}, u32[]{:S(2)}, u32[]{:S(2)}) %collective-permute-start.2) | collective-permute-done | bytes 368672 | tf_op jit(solution)/shard_map/ppermute | solution.py:134
  130.2 1.3 multiply_subtract_fusion
  (137 shorter events, 15.3 us)
Async XLA Ops:
  6.5 94.5 %all-gather.2.cloned.1.call-start = ((), (), s32[]{:S(2)}) async-start(), calls=%async_computation | async-start | bytes 2949120 | tf_op jit(solution)/shard_map/all_gather | solution.py:117
  10.1 69.1 %collective-permute-start = (f32[1,5,1,32,128]{4,3,2,1,0:T(8,128)}, f32[1,5,1,32,128]{4,3,2,1,0:T(8,128)S(1)}, u32[]{:S(2)}, u32[]{:S(2)}) collective-permute-start(f32[1,5,1,32,128]{4,3,2,1,0:T(8,128)} %get-tuple-element.49), channel_id=1, source_target_pairs={{1,0},{2,1},{3,2},{4,3},{5,4},{6,5},{7,6},{8,7},{9,8},{10,9},{11,1... | collective-permute-start | bytes 245768 | tf_op jit(solution)/shard_map/ppermute | solution.py:23
  12.0 67.2 %collective-permute-start.1 = (f32[1,5,1,32,128]{4,3,2,1,0:T(8,128)}, f32[1,5,1,32,128]{4,3,2,1,0:T(8,128)S(1)}, u32[]{:S(2)}, u32[]{:S(2)}) collective-permute-start(f32[1,5,1,32,128]{4,3,2,1,0:T(8,128)} %get-tuple-element.48), channel_id=1, source_target_pairs={{0,1},{1,2},{2,3},{3,4},{4,5},{5,6},{6,7},{7,8},{8,9},{9,10},{10,1... | collective-permute-start | bytes 245768 | tf_op jit(solution)/shard_map/ppermute | solution.py:20
  16.2 20.0 %collective-permute-start.3 = (f32[1,5,8,16,128]{4,3,2,1,0:T(8,128)S(1)}, f32[1,5,8,16,128]{4,3,2,1,0:T(8,128)S(1)}, u32[]{:S(2)}, u32[]{:S(2)}) collective-permute-start(f32[1,5,8,16,128]{4,3,2,1,0:T(8,128)S(1)} %get-tuple-element.32), channel_id=1, source_target_pairs={{0,32},{32,0},{1,33},{33,1},{2,34},{34,2},{3,35},{35,3},{4,36},{36... | collective-permute-start | bytes 983048 | tf_op jit(solution)/shard_map/ppermute | solution.py:113
  38.6 25.1 %collective-permute-start.4 = (f32[1,5,8,16,128]{4,3,2,1,0:T(8,128)S(1)}, f32[1,5,8,16,128]{4,3,2,1,0:T(8,128)S(1)}, u32[]{:S(2)}, u32[]{:S(2)}) collective-permute-start(f32[1,5,8,16,128]{4,3,2,1,0:T(8,128)S(1)} %pad_maximum_fusion.6), channel_id=1, source_target_pairs={{0,64},{64,128},{128,192},{192,256},{256,320},{320,384},{384,448},... | collective-permute-start | bytes 983048 | tf_op jit(solution)/shard_map/ppermute | solution.py:90
  42.9 22.7 %collective-permute-start.8 = (f32[1,5,8,16,128]{4,3,2,1,0:T(8,128)S(1)}, f32[1,5,8,16,128]{4,3,2,1,0:T(8,128)S(1)}, u32[]{:S(2)}, u32[]{:S(2)}) collective-permute-start(f32[1,5,8,16,128]{4,3,2,1,0:T(8,128)S(1)} %pad_maximum_fusion.7), channel_id=1, source_target_pairs={{0,448},{64,0},{128,64},{192,128},{256,192},{320,256},{384,320},{4... | collective-permute-start | bytes 983048 | tf_op jit(solution)/shard_map/ppermute | solution.py:92
  63.7 13.5 %collective-permute-start.5 = (f32[1,5,8,16,128]{4,3,2,1,0:T(8,128)S(1)}, f32[1,5,8,16,128]{4,3,2,1,0:T(8,128)S(1)}, u32[]{:S(2)}, u32[]{:S(2)}) collective-permute-start(f32[1,5,8,16,128]{4,3,2,1,0:T(8,128)S(1)} %maximum_add_fusion.1), channel_id=1, source_target_pairs={{0,64},{64,128},{128,192},{192,256},{256,320},{320,384},{384,448},... | collective-permute-start | bytes 983048 | tf_op jit(solution)/shard_map/ppermute | solution.py:90
  65.7 13.6 %collective-permute-start.9 = (f32[1,5,8,16,128]{4,3,2,1,0:T(8,128)S(1)}, f32[1,5,8,16,128]{4,3,2,1,0:T(8,128)S(1)}, u32[]{:S(2)}, u32[]{:S(2)}) collective-permute-start(f32[1,5,8,16,128]{4,3,2,1,0:T(8,128)S(1)} %maximum_add_fusion.3), channel_id=1, source_target_pairs={{0,448},{64,0},{128,64},{192,128},{256,192},{320,256},{384,320},{4... | collective-permute-start | bytes 983048 | tf_op jit(solution)/shard_map/ppermute | solution.py:92
  77.2 12.7 %collective-permute-start.6 = (f32[1,5,8,16,128]{4,3,2,1,0:T(8,128)S(1)}, f32[1,5,8,16,128]{4,3,2,1,0:T(8,128)S(1)}, u32[]{:S(2)}, u32[]{:S(2)}) collective-permute-start(f32[1,5,8,16,128]{4,3,2,1,0:T(8,128)S(1)} %maximum_add_fusion.2), channel_id=1, source_target_pairs={{0,64},{64,128},{128,192},{192,256},{256,320},{320,384},{384,448},... | collective-permute-start | bytes 983048 | tf_op jit(solution)/shard_map/ppermute | solution.py:90
  79.4 13.3 %collective-permute-start.10 = (f32[1,5,8,16,128]{4,3,2,1,0:T(8,128)S(1)}, f32[1,5,8,16,128]{4,3,2,1,0:T(8,128)S(1)}, u32[]{:S(2)}, u32[]{:S(2)}) collective-permute-start(f32[1,5,8,16,128]{4,3,2,1,0:T(8,128)S(1)} %maximum_add_fusion.4), channel_id=1, source_target_pairs={{0,448},{64,0},{128,64},{192,128},{256,192},{320,256},{384,320},{4... | collective-permute-start | bytes 983048 | tf_op jit(solution)/shard_map/ppermute | solution.py:92
  89.9 8.4 %collective-permute-start.7 = (f32[1,5,4,16,128]{4,3,2,1,0:T(8,128)S(1)}, f32[1,5,4,16,128]{4,3,2,1,0:T(8,128)S(1)}, u32[]{:S(2)}, u32[]{:S(2)}) collective-permute-start(f32[1,5,4,16,128]{4,3,2,1,0:T(8,128)S(1)} %slice_add_fusion.4), channel_id=1, source_target_pairs={{0,64},{64,128},{128,192},{192,256},{256,320},{320,384},{384,448},... | collective-permute-start | bytes 491528 | tf_op jit(solution)/shard_map/ppermute | solution.py:93
  99.1 12.2 %collective-permute-start.11 = (f32[1,5,4,16,128]{4,3,2,1,0:T(8,128)}, f32[1,5,4,16,128]{4,3,2,1,0:T(8,128)}, u32[]{:S(2)}, u32[]{:S(2)}) collective-permute-start(f32[1,5,4,16,128]{4,3,2,1,0:T(8,128)} %get-tuple-element.59), channel_id=1, source_target_pairs={{0,448},{64,0},{128,64},{192,128},{256,192},{320,256},{384,320},{4... | collective-permute-start | bytes 491528 | tf_op jit(solution)/shard_map/ppermute | solution.py:94
  106.6 23.1 %copy-start.1 = (f32[1,5,8,31,128]{4,3,2,1,0:T(8,128)S(1)}, f32[1,5,8,31,128]{4,3,2,1,0:T(8,128)}, u32[]{:S(2)}) copy-start(f32[1,5,8,31,128]{4,3,2,1,0:T(8,128)} %get-tuple-element.50) | copy-start | bytes 1904644
  106.6 23.1 %copy-start.2 = (f32[1,5,8,31,128]{4,3,2,1,0:T(8,128)S(1)}, f32[1,5,8,31,128]{4,3,2,1,0:T(8,128)}, u32[]{:S(2)}) copy-start(f32[1,5,8,31,128]{4,3,2,1,0:T(8,128)} %get-tuple-element.51) | copy-start | bytes 1904644
  107.1 22.9 %copy-start.4 = (f32[1,5,8,32,127]{4,3,2,1,0:T(8,128)S(1)}, f32[1,5,8,32,127]{4,3,2,1,0:T(8,128)}, u32[]{:S(2)}) copy-start(f32[1,5,8,32,127]{4,3,2,1,0:T(8,128)} %copy-done.3) | copy-start | bytes 1950724
  107.1 22.9 %copy-start.6 = (f32[1,5,8,32,127]{4,3,2,1,0:T(8,128)S(1)}, f32[1,5,8,32,127]{4,3,2,1,0:T(8,128)}, u32[]{:S(2)}) copy-start(f32[1,5,8,32,127]{4,3,2,1,0:T(8,128)} %copy-done.5) | copy-start | bytes 1950724
  107.1 22.9 %copy-start.10 = (f32[8,32,128]{2,1,0:T(8,128)S(1)}, f32[8,32,128]{2,1,0:T(8,128)}, u32[]{:S(2)}) copy-start(f32[8,32,128]{2,1,0:T(8,128)} %get-tuple-element.43) | copy-start | bytes 393220
  107.2 22.9 %copy-start.11 = (f32[8,32,128]{2,1,0:T(8,128)S(1)}, f32[8,32,128]{2,1,0:T(8,128)}, u32[]{:S(2)}) copy-start(f32[8,32,128]{2,1,0:T(8,128)} %get-tuple-element.44) | copy-start | bytes 393220
  107.2 22.9 %copy-start.12 = (f32[8,32,128]{2,1,0:T(8,128)S(1)}, f32[8,32,128]{2,1,0:T(8,128)}, u32[]{:S(2)}) copy-start(f32[8,32,128]{2,1,0:T(8,128)} %get-tuple-element.45) | copy-start | bytes 393220
  107.2 22.9 %copy-start.13 = (f32[8,32,128]{2,1,0:T(8,128)S(1)}, f32[8,32,128]{2,1,0:T(8,128)}, u32[]{:S(2)}) copy-start(f32[8,32,128]{2,1,0:T(8,128)} %get-tuple-element.46) | copy-start | bytes 393220
  107.2 22.9 %copy-start.14 = (f32[8,32,128]{2,1,0:T(8,128)S(1)}, f32[8,32,128]{2,1,0:T(8,128)}, u32[]{:S(2)}) copy-start(f32[8,32,128]{2,1,0:T(8,128)} %get-tuple-element.47) | copy-start | bytes 393220
  107.2 22.9 %copy-start.15 = (f32[8,32,128]{2,1,0:T(8,128)S(1)}, f32[8,32,128]{2,1,0:T(8,128)}, u32[]{:S(2)}) copy-start(f32[8,32,128]{2,1,0:T(8,128)} %get-tuple-element.33) | copy-start | bytes 393220
  107.2 22.9 %copy-start.16 = (f32[8,32,128]{2,1,0:T(8,128)S(1)}, f32[8,32,128]{2,1,0:T(8,128)}, u32[]{:S(2)}) copy-start(f32[8,32,128]{2,1,0:T(8,128)} %get-tuple-element.34) | copy-start | bytes 393220
  107.3 22.3 %collective-permute-start.2 = (f32[92160]{0:T(1024)S(1)}, f32[92160]{0:T(1024)S(1)}, u32[]{:S(2)}, u32[]{:S(2)}) collective-permute-start(f32[92160]{0:T(1024)S(1)} %pad_maximum_fusion.4), channel_id=1, source_target_pairs={{0,32},{32,0},{1,33},{33,1},{2,34},{34,2},{3,35},{35,3},{4,36},{36... | collective-permute-start | bytes 1105928 | tf_op jit(solution)/shard_map/ppermute | solution.py:134
  (27 other events, 410.7 us)
Sparse Core Ops, SparseCore 0:
  9.4 55.8 all-gather.1

commit v8 on v7

--- a/solution.py
+++ b/solution.py
@@ -111,7 +111,13 @@
 
     inner = state[:, :, :, edge : pitch - edge]
     other = lax.ppermute(inner, "ty", swap)
-    inner_term = reduced_along_z(inner, other, y, total_count)
+    expand = (ring,) + (1,) * (inner.ndim - 1)
+    own_weights = time_weights(ring_ids - own, total_count).reshape(expand)
+    partner_weights = time_weights(ring_ids - partner, total_count).reshape(expand)
+    contributions = own_weights * inner[:, :, :, :edge] + partner_weights * other[:, :, :, :edge]
+    scattered_term = lax.psum_scatter(contributions, "tz", scatter_dimension=0, tiled=True)
+    ring_term = reduced_along_z(inner[:, :, :, edge:], other[:, :, :, edge:], y, total_count)
+    inner_term = jnp.concatenate([scattered_term, ring_term], axis=3)
 
     outer = jnp.concatenate([state[:, :, :, :edge], state[:, :, :, pitch - edge :]], axis=3)
     held = lax.all_gather(outer, "tz", axis=0, tiled=True)

time: 141 us -> 139 us (0.986)
  the two profiles are of different devices: /device:TPU:26 before, /device:TPU:6 now
where the time goes in v8:
time: 139 us; the launch traced here: 137 us
  starting transfers between devices  54.1 us (39%)
  waiting for transfers between devices  37.7 us (27%)
  other arithmetic  16.3 us (12%)
  between operations  14.2 us (10%)
  local copies, waits for them, and re-layouts  12.9 us (9%)
  matrix products  2.13 us (2%)
    ppermute x3, starting transfers between devices, reduced_along_z(): lax.ppermute(sent if behind is None else behind + sent, 'tz', backward)  21.2 us
    ppermute x3, waiting for transfers between devices, reduced_along_z(): ahead = lax.ppermute(sent if ahead is None else ahead + sent, 'tz', forward)  15 us
    ppermute x1, waiting for transfers between devices, per_device(): received = lax.ppermute(message, 'ty', swap)  11.9 us
    ppermute x1, starting transfers between devices, per_device(): other = lax.ppermute(inner, 'ty', swap)  7.72 us
    ppermute x1, starting transfers between devices, per_device(): received = lax.ppermute(message, 'ty', swap)  7.3 us
    ppermute x1, starting transfers between devices, extended_2(): lax.ppermute(lax.slice_in_dim(block, 0, width, axis=dim), axis, backward)  6.34 us
    ppermute x3, starting transfers between devices, reduced_along_z(): ahead = lax.ppermute(sent if ahead is None else ahead + sent, 'tz', forward)  5.76 us
    ppermute x1, waiting for transfers between devices, reduced_along_z(): lax.ppermute(ahead[:, :, :half] + terms[1][:, :, :half], 'tz', forward)  4.56 us
  transfers between devices with their start and end apart: 14, of which 7 were waited for; matrix products, arithmetic and copies ran while one was open for 18% of the time, Pallas kernels for 0%

profile of v8, /device:TPU:6, one launch (start us, length us, event | category | flops | bytes accessed | tf_op | source)
XLA Modules:
  0.0 137.3 jit_solution(10082762660342417819)
XLA Ops:
  8.2 1.9 %collective-permute-start.1 = (f32[1,5,1,32,128]{4,3,2,1,0:T(8,128)}, f32[1,5,1,32,128]{4,3,2,1,0:T(8,128)S(1)}, u32[]{:S(2)}, u32[]{:S(2)}) collective-permute-start(f32[1,5,1,32,128]{4,3,2,1,0:T(8,128)} %get-tuple-element.50), channel_id=1, source_target_pairs={{0,1},{1,2},{2,3},{3,4},{4,5},{5,6},{6,7},{7,8},{8,9},{9,10},{10,1... | collective-permute-start | bytes 245768 | tf_op jit(solution)/shard_map/ppermute | solution.py:20
  10.1 6.3 %collective-permute-start = (f32[1,5,1,32,128]{4,3,2,1,0:T(8,128)}, f32[1,5,1,32,128]{4,3,2,1,0:T(8,128)}, u32[]{:S(2)}, u32[]{:S(2)}) collective-permute-start(f32[1,5,1,32,128]{4,3,2,1,0:T(8,128)} %get-tuple-element.51), channel_id=1, source_target_pairs={{1,0},{2,1},{3,2},{4,3},{5,4},{6,5},{7,6},{8,7},{9,8},{10,9},{11,1... | collective-permute-start | bytes 245768 | tf_op jit(solution)/shard_map/ppermute | solution.py:23
  16.5 1.7 %slice.363 = f32[1,5,8,16,128]{4,3,2,1,0:T(8,128)} slice(f32[1,5,8,32,128]{4,3,2,1,0:T(8,128)} %param.7), slice={[0:1], [0:5], [0:8], [8:24], [0:128]} | slice | bytes 655360 | tf_op jit(solution)/shard_map/slice | solution.py:112
  18.2 7.7 %collective-permute-start.3 = (f32[1,5,8,16,128]{4,3,2,1,0:T(8,128)}, f32[1,5,8,16,128]{4,3,2,1,0:T(8,128)}, u32[]{:S(2)}, u32[]{:S(2)}) collective-permute-start(f32[1,5,8,16,128]{4,3,2,1,0:T(8,128)} %slice.363), channel_id=1, source_target_pairs={{0,32},{32,0},{1,33},{33,1},{2,34},{34,2},{3,35},{35,3},{4,36},{36... | collective-permute-start | bytes 983048 | tf_op jit(solution)/shard_map/ppermute | solution.py:113
  33.9 1.7 %collective-permute-done.3 = f32[1,5,8,16,128]{4,3,2,1,0:T(8,128)} collective-permute-done((f32[1,5,8,16,128]{4,3,2,1,0:T(8,128)}, f32[1,5,8,16,128]{4,3,2,1,0:T(8,128)}, u32[]{:S(2)}, u32[]{:S(2)}) %collective-permute-start.3) | collective-permute-done | bytes 327712 | tf_op jit(solution)/shard_map/ppermute | solution.py:113
  38.0 11.0 %collective-permute-start.8 = (f32[1,5,8,8,128]{4,3,2,1,0:T(8,128)S(1)}, f32[1,5,8,8,128]{4,3,2,1,0:T(8,128)S(1)}, u32[]{:S(2)}, u32[]{:S(2)}) collective-permute-start(f32[1,5,8,8,128]{4,3,2,1,0:T(8,128)S(1)} %pad_maximum_fusion.7), channel_id=1, source_target_pairs={{0,448},{64,0},{128,64},{192,128},{256,192},{320,256},{384,320},{4... | collective-permute-start | bytes 491528 | tf_op jit(solution)/shard_map/ppermute | solution.py:92
  49.0 1.9 %collective-permute-start.4 = (f32[1,5,8,8,128]{4,3,2,1,0:T(8,128)S(1)}, f32[1,5,8,8,128]{4,3,2,1,0:T(8,128)S(1)}, u32[]{:S(2)}, u32[]{:S(2)}) collective-permute-start(f32[1,5,8,8,128]{4,3,2,1,0:T(8,128)S(1)} %pad_maximum_fusion.6), channel_id=1, source_target_pairs={{0,64},{64,128},{128,192},{192,256},{256,320},{320,384},{384,448},... | collective-permute-start | bytes 491528 | tf_op jit(solution)/shard_map/ppermute | solution.py:90
  51.0 9.9 %collective-permute-done.4 = f32[1,5,8,8,128]{4,3,2,1,0:T(8,128)S(1)} collective-permute-done((f32[1,5,8,8,128]{4,3,2,1,0:T(8,128)S(1)}, f32[1,5,8,8,128]{4,3,2,1,0:T(8,128)S(1)}, u32[]{:S(2)}, u32[]{:S(2)}) %collective-permute-start.4) | collective-permute-done | bytes 163872 | tf_op jit(solution)/shard_map/ppermute | solution.py:90
  60.9 1.9 %collective-permute-start.5 = (f32[1,5,8,8,128]{4,3,2,1,0:T(8,128)S(1)}, f32[1,5,8,8,128]{4,3,2,1,0:T(8,128)S(1)}, u32[]{:S(2)}, u32[]{:S(2)}) collective-permute-start(f32[1,5,8,8,128]{4,3,2,1,0:T(8,128)S(1)} %maximum_add_fusion.1), channel_id=1, source_target_pairs={{0,64},{64,128},{128,192},{192,256},{256,320},{320,384},{384,448},... | collective-permute-start | bytes 491528 | tf_op jit(solution)/shard_map/ppermute | solution.py:90
  62.9 5.1 %collective-permute-start.9 = (f32[1,5,8,8,128]{4,3,2,1,0:T(8,128)S(1)}, f32[1,5,8,8,128]{4,3,2,1,0:T(8,128)S(1)}, u32[]{:S(2)}, u32[]{:S(2)}) collective-permute-start(f32[1,5,8,8,128]{4,3,2,1,0:T(8,128)S(1)} %maximum_add_fusion.3), channel_id=1, source_target_pairs={{0,448},{64,0},{128,64},{192,128},{256,192},{320,256},{384,320},{4... | collective-permute-start | bytes 491528 | tf_op jit(solution)/shard_map/ppermute | solution.py:92
  68.0 4.4 %collective-permute-done.5 = f32[1,5,8,8,128]{4,3,2,1,0:T(8,128)S(1)} collective-permute-done((f32[1,5,8,8,128]{4,3,2,1,0:T(8,128)S(1)}, f32[1,5,8,8,128]{4,3,2,1,0:T(8,128)S(1)}, u32[]{:S(2)}, u32[]{:S(2)}) %collective-permute-start.5) | collective-permute-done | bytes 163872 | tf_op jit(solution)/shard_map/ppermute | solution.py:90
  72.5 1.9 %collective-permute-start.6 = (f32[1,5,8,8,128]{4,3,2,1,0:T(8,128)S(1)}, f32[1,5,8,8,128]{4,3,2,1,0:T(8,128)S(1)}, u32[]{:S(2)}, u32[]{:S(2)}) collective-permute-start(f32[1,5,8,8,128]{4,3,2,1,0:T(8,128)S(1)} %maximum_add_fusion.2), channel_id=1, source_target_pairs={{0,64},{64,128},{128,192},{192,256},{256,320},{320,384},{384,448},... | collective-permute-start | bytes 491528 | tf_op jit(solution)/shard_map/ppermute | solution.py:90
  75.1 5.1 %collective-permute-start.10 = (f32[1,5,8,8,128]{4,3,2,1,0:T(8,128)}, f32[1,5,8,8,128]{4,3,2,1,0:T(8,128)}, u32[]{:S(2)}, u32[]{:S(2)}) collective-permute-start(f32[1,5,8,8,128]{4,3,2,1,0:T(8,128)} %maximum_add_fusion.4), channel_id=1, source_target_pairs={{0,448},{64,0},{128,64},{192,128},{256,192},{320,256},{384,320},{4... | collective-permute-start | bytes 491528 | tf_op jit(solution)/shard_map/ppermute | solution.py:92
  81.6 1.9 %collective-permute-start.7 = (f32[1,5,4,8,128]{4,3,2,1,0:T(8,128)}, f32[1,5,4,8,128]{4,3,2,1,0:T(8,128)}, u32[]{:S(2)}, u32[]{:S(2)}) collective-permute-start(f32[1,5,4,8,128]{4,3,2,1,0:T(8,128)} %slice_add_fusion.4), channel_id=1, source_target_pairs={{0,64},{64,128},{128,192},{192,256},{256,320},{320,384},{384,448},... | collective-permute-start | bytes 245768 | tf_op jit(solution)/shard_map/ppermute | solution.py:93
  84.9 4.6 %collective-permute-done.7 = f32[1,5,4,8,128]{4,3,2,1,0:T(8,128)} collective-permute-done((f32[1,5,4,8,128]{4,3,2,1,0:T(8,128)}, f32[1,5,4,8,128]{4,3,2,1,0:T(8,128)}, u32[]{:S(2)}, u32[]{:S(2)}) %collective-permute-start.7) | collective-permute-done | bytes 81952 | tf_op jit(solution)/shard_map/ppermute | solution.py:93
  89.5 1.7 %slice_add_fusion.3 = (f32[1,5,4,8,128]{4,3,2,1,0:T(8,128)}, f32[1,5,4,8,128]{4,3,2,1,0:T(8,128)}) fusion(f32[1,5,4,8,128]{4,3,2,1,0:T(8,128)} %collective-permute-done.7, f32[1,5,8,8,128]{4,3,2,1,0:T(8,128)} %collective-permute-done.10, f32[1,5,8,8,128]{4,3,2,1,0:T(8,128)S(1)} %get-tuple-element.25), kind=kLoop, calls=%fused_computation.64 | loop fusion | flops 40960 | bytes 491520 | tf_op jit(solution)/shard_map/add | solution.py:95
  91.2 1.9 %collective-permute-start.11 = (f32[1,5,4,8,128]{4,3,2,1,0:T(8,128)}, f32[1,5,4,8,128]{4,3,2,1,0:T(8,128)S(1)}, u32[]{:S(2)}, u32[]{:S(2)}) collective-permute-start(f32[1,5,4,8,128]{4,3,2,1,0:T(8,128)} %get-tuple-element.61), channel_id=1, source_target_pairs={{0,448},{64,0},{128,64},{192,128},{256,192},{320,256},{384,320},{4... | collective-permute-start | bytes 245768 | tf_op jit(solution)/shard_map/ppermute | solution.py:94
  93.1 2.2 %fusion.27 = (f32[8,5,8,1,128]{4,3,2,1,0:T(1,128)S(1)}, f32[8,5,8,1,128]{4,3,2,1,0:T(1,128)S(1)}) fusion(f32[8,5,8,16,128]{4,3,2,1,0:T(8,128)} %all-gather.2.cloned.1.call-done), kind=kLoop, calls=%fused_computation.160 | loop fusion | bytes 655360 | tf_op jit(solution)/shard_map/slice | solution.py:128
  95.3 2.1 %convolution_bitcast_fusion = f32[2,5,8,128,8]{3,4,1,2,0:T(8,128)S(1)} fusion(s32[2,8,128]{2,1,0:T(8,128)} %param.12, f32[1,8,5,8,128]{4,1,2,3,0:T(8,128)S(1)} %get-tuple-element.80, f32[1,8,5,8,128]{4,1,2,3,0:T(8,128)S(1)} %get-tuple-element.81), kind=kOutput, calls=%fused_computation.3 | convolution fusion | flops 126173184 | bytes 663552 | tf_op jit(solution)/shard_map/szvir,sikr->szvik/dot_general | solution.py:133
  99.1 7.3 %collective-permute-start.2 = (f32[92160]{0:T(1024)S(1)}, f32[92160]{0:T(1024)S(1)}, u32[]{:S(2)}, u32[]{:S(2)}) collective-permute-start(f32[92160]{0:T(1024)S(1)} %pad_maximum_fusion.4), channel_id=1, source_target_pairs={{0,32},{32,0},{1,33},{33,1},{2,34},{34,2},{3,35},{35,3},{4,36},{36... | collective-permute-start | bytes 1105928 | tf_op jit(solution)/shard_map/ppermute | solution.py:140
  107.4 11.9 %collective-permute-done.2 = f32[92160]{0:T(1024)S(1)} collective-permute-done((f32[92160]{0:T(1024)S(1)}, f32[92160]{0:T(1024)S(1)}, u32[]{:S(2)}, u32[]{:S(2)}) %collective-permute-start.2) | collective-permute-done | bytes 368672 | tf_op jit(solution)/shard_map/ppermute | solution.py:140
  120.9 3.0 %multiply_subtract_fusion = f32[1,5,8,32,128]{4,3,2,1,0:T(8,128)} fusion(f32[1,5,8,32,128]{4,3,2,1,0:T(8,128)S(1)} %copy-done, f32[1,5,8,32,127]{4,3,2,1,0:T(8,128)S(1)} %get-tuple-element.55, f32[1,5,8,32,127]{4,3,2,1,0:T(8,128)S(1)} %get-tuple-element.54, f32[1,5,8,31,128]{4,3,2,1,0:T(8,128)S(1)} %get-tuple-element.53, ...), kind=kLoop, calls=%fused_computation.13 | loop fusion | flops 6881280 | bytes 6183212 | tf_op jit(solution)/shard_map/sub | solution.py:68
  124.0 4.5 %reduce-scatter.2.cloned.1.call-done = f32[1,5,8,8,128]{4,3,2,1,0:T(8,128)} async-done(((f32[8,5,8,8,128]{4,3,2,1,0:T(8,128)}), f32[1,5,8,8,128]{4,3,2,1,0:T(8,128)}) %reduce-scatter.2.cloned.1.call-update) | async-done | bytes 163856 | tf_op jit(solution)/shard_map/reduce_scatter | solution.py:118
  128.5 1.9 %fusion.3 = f32[1,5,8,32,128]{4,3,2,1,0:T(8,128)} fusion(f32[1,5,8,32,128]{4,3,2,1,0:T(8,128)S(1)} %copy-done.4, f32[1,5,8,32,128]{4,3,2,1,0:T(8,128)S(1)} %copy-done.3, f32[1,5,8,8,128]{4,3,2,1,0:T(8,128)S(1)} %get-tuple-element.57, f32[1,5,8,8,128]{4,3,2,1,0:T(8,128)S(1)} %fusion.8, f32[1,5,8,8,128]{4,3,2,1,0:T(8,128)} %reduce-scatter.2.cloned.1.call-done, ...), kind=kLoop, calls=%fused_computation.12 | loop fusion | flops 983040 | bytes 2752512 | tf_op jit(solution)/shard_map/sub | solution.py:156
  (132 shorter events, 19.5 us)
Async XLA Ops:
  6.5 19.4 %copy-start = (f32[1,5,8,32,128]{4,3,2,1,0:T(8,128)S(1)}, f32[1,5,8,32,128]{4,3,2,1,0:T(8,128)}, u32[]{:S(2)}) copy-start(f32[1,5,8,32,128]{4,3,2,1,0:T(8,128)} %param.7) | copy-start | bytes 1966084
  6.5 86.5 %all-gather.2.cloned.1.call-start = ((), (), s32[]{:S(2)}) async-start(), calls=%async_computation.1 | async-start | bytes 2949120 | tf_op jit(solution)/shard_map/all_gather | solution.py:123
  8.2 23.9 %collective-permute-start.1 = (f32[1,5,1,32,128]{4,3,2,1,0:T(8,128)}, f32[1,5,1,32,128]{4,3,2,1,0:T(8,128)S(1)}, u32[]{:S(2)}, u32[]{:S(2)}) collective-permute-start(f32[1,5,1,32,128]{4,3,2,1,0:T(8,128)} %get-tuple-element.50), channel_id=1, source_target_pairs={{0,1},{1,2},{2,3},{3,4},{4,5},{5,6},{6,7},{7,8},{8,9},{9,10},{10,1... | collective-permute-start | bytes 245768 | tf_op jit(solution)/shard_map/ppermute | solution.py:20
  10.1 22.0 %collective-permute-start = (f32[1,5,1,32,128]{4,3,2,1,0:T(8,128)}, f32[1,5,1,32,128]{4,3,2,1,0:T(8,128)}, u32[]{:S(2)}, u32[]{:S(2)}) collective-permute-start(f32[1,5,1,32,128]{4,3,2,1,0:T(8,128)} %get-tuple-element.51), channel_id=1, source_target_pairs={{1,0},{2,1},{3,2},{4,3},{5,4},{6,5},{7,6},{8,7},{9,8},{10,9},{11,1... | collective-permute-start | bytes 245768 | tf_op jit(solution)/shard_map/ppermute | solution.py:23
  18.2 17.4 %collective-permute-start.3 = (f32[1,5,8,16,128]{4,3,2,1,0:T(8,128)}, f32[1,5,8,16,128]{4,3,2,1,0:T(8,128)}, u32[]{:S(2)}, u32[]{:S(2)}) collective-permute-start(f32[1,5,8,16,128]{4,3,2,1,0:T(8,128)} %slice.363), channel_id=1, source_target_pairs={{0,32},{32,0},{1,33},{33,1},{2,34},{34,2},{3,35},{35,3},{4,36},{36... | collective-permute-start | bytes 983048 | tf_op jit(solution)/shard_map/ppermute | solution.py:113
  27.4 101.1 %reduce-scatter.2.cloned.1.call-start = ((), (), s32[]{:S(2)}) async-start(), calls=%async_computation.2 | async-start | bytes 1474560 | tf_op jit(solution)/shard_map/reduce_scatter | solution.py:118
  27.5 1.8 %copy-start.23 = (s32[1,2,8,128]{3,2,1,0:T(8,128)S(1)}, s32[1,2,8,128]{3,2,1,0:T(8,128)}, u32[]{:S(2)}) copy-start(s32[1,2,8,128]{3,2,1,0:T(8,128)} %param.13) | copy-start | bytes 24580
  27.5 2.6 %copy-start.22 = (f32[8,32,128]{2,1,0:T(8,128)S(1)}, f32[8,32,128]{2,1,0:T(8,128)}, u32[]{:S(2)}) copy-start(f32[8,32,128]{2,1,0:T(8,128)} %param.9) | copy-start | bytes 393220
  38.0 24.9 %collective-permute-start.8 = (f32[1,5,8,8,128]{4,3,2,1,0:T(8,128)S(1)}, f32[1,5,8,8,128]{4,3,2,1,0:T(8,128)S(1)}, u32[]{:S(2)}, u32[]{:S(2)}) collective-permute-start(f32[1,5,8,8,128]{4,3,2,1,0:T(8,128)S(1)} %pad_maximum_fusion.7), channel_id=1, source_target_pairs={{0,448},{64,0},{128,64},{192,128},{256,192},{320,256},{384,320},{4... | collective-permute-start | bytes 491528 | tf_op jit(solution)/shard_map/ppermute | solution.py:92
  49.0 11.9 %collective-permute-start.4 = (f32[1,5,8,8,128]{4,3,2,1,0:T(8,128)S(1)}, f32[1,5,8,8,128]{4,3,2,1,0:T(8,128)S(1)}, u32[]{:S(2)}, u32[]{:S(2)}) collective-permute-start(f32[1,5,8,8,128]{4,3,2,1,0:T(8,128)S(1)} %pad_maximum_fusion.6), channel_id=1, source_target_pairs={{0,64},{64,128},{128,192},{192,256},{256,320},{320,384},{384,448},... | collective-permute-start | bytes 491528 | tf_op jit(solution)/shard_map/ppermute | solution.py:90
  50.9 32.6 %copy-start.5 = (f32[5,8,8,128]{3,2,1,0:T(8,128)S(1)}, f32[5,8,8,128]{3,2,1,0:T(8,128)}, u32[]{:S(2)}) copy-start(f32[5,8,8,128]{3,2,1,0:T(8,128)} %get-tuple-element.31) | copy-start | bytes 491524
  60.9 11.5 %collective-permute-start.5 = (f32[1,5,8,8,128]{4,3,2,1,0:T(8,128)S(1)}, f32[1,5,8,8,128]{4,3,2,1,0:T(8,128)S(1)}, u32[]{:S(2)}, u32[]{:S(2)}) collective-permute-start(f32[1,5,8,8,128]{4,3,2,1,0:T(8,128)S(1)} %maximum_add_fusion.1), channel_id=1, source_target_pairs={{0,64},{64,128},{128,192},{192,256},{256,320},{320,384},{384,448},... | collective-permute-start | bytes 491528 | tf_op jit(solution)/shard_map/ppermute | solution.py:90
  62.9 11.5 %collective-permute-start.9 = (f32[1,5,8,8,128]{4,3,2,1,0:T(8,128)S(1)}, f32[1,5,8,8,128]{4,3,2,1,0:T(8,128)S(1)}, u32[]{:S(2)}, u32[]{:S(2)}) collective-permute-start(f32[1,5,8,8,128]{4,3,2,1,0:T(8,128)S(1)} %maximum_add_fusion.3), channel_id=1, source_target_pairs={{0,448},{64,0},{128,64},{192,128},{256,192},{320,256},{384,320},{4... | collective-permute-start | bytes 491528 | tf_op jit(solution)/shard_map/ppermute | solution.py:92
  72.5 8.4 %collective-permute-start.6 = (f32[1,5,8,8,128]{4,3,2,1,0:T(8,128)S(1)}, f32[1,5,8,8,128]{4,3,2,1,0:T(8,128)S(1)}, u32[]{:S(2)}, u32[]{:S(2)}) collective-permute-start(f32[1,5,8,8,128]{4,3,2,1,0:T(8,128)S(1)} %maximum_add_fusion.2), channel_id=1, source_target_pairs={{0,64},{64,128},{128,192},{192,256},{256,320},{320,384},{384,448},... | collective-permute-start | bytes 491528 | tf_op jit(solution)/shard_map/ppermute | solution.py:90
  75.1 9.8 %collective-permute-start.10 = (f32[1,5,8,8,128]{4,3,2,1,0:T(8,128)}, f32[1,5,8,8,128]{4,3,2,1,0:T(8,128)}, u32[]{:S(2)}, u32[]{:S(2)}) collective-permute-start(f32[1,5,8,8,128]{4,3,2,1,0:T(8,128)} %maximum_add_fusion.4), channel_id=1, source_target_pairs={{0,448},{64,0},{128,64},{192,128},{256,192},{320,256},{384,320},{4... | collective-permute-start | bytes 491528 | tf_op jit(solution)/shard_map/ppermute | solution.py:92
  81.6 7.8 %collective-permute-start.7 = (f32[1,5,4,8,128]{4,3,2,1,0:T(8,128)}, f32[1,5,4,8,128]{4,3,2,1,0:T(8,128)}, u32[]{:S(2)}, u32[]{:S(2)}) collective-permute-start(f32[1,5,4,8,128]{4,3,2,1,0:T(8,128)} %slice_add_fusion.4), channel_id=1, source_target_pairs={{0,64},{64,128},{128,192},{192,256},{256,320},{320,384},{384,448},... | collective-permute-start | bytes 245768 | tf_op jit(solution)/shard_map/ppermute | solution.py:93
  91.2 15.3 %collective-permute-start.11 = (f32[1,5,4,8,128]{4,3,2,1,0:T(8,128)}, f32[1,5,4,8,128]{4,3,2,1,0:T(8,128)S(1)}, u32[]{:S(2)}, u32[]{:S(2)}) collective-permute-start(f32[1,5,4,8,128]{4,3,2,1,0:T(8,128)} %get-tuple-element.61), channel_id=1, source_target_pairs={{0,448},{64,0},{128,64},{192,128},{256,192},{320,256},{384,320},{4... | collective-permute-start | bytes 245768 | tf_op jit(solution)/shard_map/ppermute | solution.py:94
  93.1 5.5 %copy-start.2 = (f32[8,5,8,16,128]{4,3,2,1,0:T(8,128)S(1)}, f32[8,5,8,16,128]{4,3,2,1,0:T(8,128)}, u32[]{:S(2)}) copy-start(f32[8,5,8,16,128]{4,3,2,1,0:T(8,128)} %all-gather.2.cloned.1.call-done) | copy-start | bytes 7864324
  99.0 7.4 %copy-start.19 = (f32[1,5,8,8,128]{4,3,2,1,0:T(8,128)S(1)}, f32[1,5,8,8,128]{4,3,2,1,0:T(8,128)}, u32[]{:S(2)}) copy-start(f32[1,5,8,8,128]{4,3,2,1,0:T(8,128)} %copy-done.18) | copy-start | bytes 491524
  99.0 7.4 %copy-start.17 = (f32[1,5,4,8,128]{4,3,2,1,0:T(8,128)S(1)}, f32[1,5,4,8,128]{4,3,2,1,0:T(8,128)}, u32[]{:S(2)}) copy-start(f32[1,5,4,8,128]{4,3,2,1,0:T(8,128)} %get-tuple-element.60) | copy-start | bytes 245764
  99.1 20.2 %collective-permute-start.2 = (f32[92160]{0:T(1024)S(1)}, f32[92160]{0:T(1024)S(1)}, u32[]{:S(2)}, u32[]{:S(2)}) collective-permute-start(f32[92160]{0:T(1024)S(1)} %pad_maximum_fusion.4), channel_id=1, source_target_pairs={{0,32},{32,0},{1,33},{33,1},{2,34},{34,2},{3,35},{35,3},{4,36},{36... | collective-permute-start | bytes 1105928 | tf_op jit(solution)/shard_map/ppermute | solution.py:140
  123.9 4.7 %copy-start.3 = (f32[1,5,8,32,128]{4,3,2,1,0:T(8,128)S(1)}, f32[1,5,8,32,128]{4,3,2,1,0:T(8,128)}, u32[]{:S(2)}) copy-start(f32[1,5,8,32,128]{4,3,2,1,0:T(8,128)} %multiply_subtract_fusion) | copy-start | bytes 1966084
  123.9 4.7 %copy-start.4 = (f32[1,5,8,32,128]{4,3,2,1,0:T(8,128)S(1)}, f32[1,5,8,32,128]{4,3,2,1,0:T(8,128)}, u32[]{:S(2)}) copy-start(f32[1,5,8,32,128]{4,3,2,1,0:T(8,128)} %param.8) | copy-start | bytes 1966084
  123.9 4.7 %copy-start.16 = (f32[8,32,128]{2,1,0:T(8,128)S(1)}, f32[8,32,128]{2,1,0:T(8,128)}, u32[]{:S(2)}) copy-start(f32[8,32,128]{2,1,0:T(8,128)} %broadcast_multiply_fusion) | copy-start | bytes 393220
  (22 other events, 25.5 us)
Sparse Core Ops, SparseCore 0:
  27.6 52.0 all-gather.1
  85.0 43.4 reduce-scatter.1

commit v9 on v6

--- a/solution.py
+++ b/solution.py
@@ -88,7 +88,9 @@
     contributions = own_weights * inner + partner_weights * other
     inner_term = lax.psum_scatter(contributions, "tz", scatter_dimension=0, tiled=True)
 
-    outer = jnp.concatenate([state[:, :, :, :edge], state[:, :, :, pitch - edge :]], axis=3)
+    groups = pitch // edge
+    grouped = state.reshape(state.shape[:3] + (groups, edge, state.shape[4]))
+    outer = grouped[:, :, :, :: groups - 1].reshape(state.shape[:3] + (2 * edge, state.shape[4]))
     held = lax.all_gather(outer, "tz", axis=0, tiled=True)
     targets = jnp.stack([own, partner])
     weights = time_weights(targets[:, None] - ring_ids[None, :], total_count)
@@ -110,8 +112,8 @@
     split = partial[0].size
     outer_term = partial[:1] + received[:split].reshape((1,) + partial.shape[1:])
     ghosts = picked[0] + received[split:].reshape(picked.shape[1:])
-    time_term = jnp.concatenate(
-        [outer_term[:, :, :, :edge], inner_term, outer_term[:, :, :, edge:]], axis=3
+    early_term = jnp.concatenate(
+        [outer_term[:, :, :, :edge], jnp.zeros_like(inner_term), outer_term[:, :, :, edge:]], axis=3
     )
     low_ghost = rotate_velocity(ghosts[0][None], -1.0)
     high_ghost = rotate_velocity(ghosts[1][None], 1.0)
@@ -119,10 +121,12 @@
     extended = extended_2(state, (("space", 2),), 1)
     up_i = extended[:, :, 2:]
     down_i = extended[:, :, :-2]
-    spatial = lax.optimization_barrier(
-        section_spatial(state, eddy_visc, jacobians, up_i, down_i, low_ghost, high_ghost)
-    )
-    return base - SECTION_ALPHA * pseudo_step[None, None] * (spatial + time_term)
+    spatial = section_spatial(state, eddy_visc, jacobians, up_i, down_i, low_ghost, high_ghost)
+    step = SECTION_ALPHA * pseudo_step[None, None]
+    early, spatial = lax.optimization_barrier((base - step * (spatial + early_term), spatial))
+    rows = slice(edge, pitch - edge)
+    inner_out = base[:, :, :, rows] - step[:, :, :, rows] * (spatial[:, :, :, rows] + inner_term)
+    return early.at[:, :, :, rows].set(inner_out)
 
 
 def solution(mesh):

time: 118 us -> 118 us (level)
  local copies, waits for them, and re-layouts: 10.3 us -> 13.1 us
  waiting for transfers between devices: 57 us -> 54.6 us
    ppermute x1, waiting for transfers between devices: 7.7 us -> 4.4 us  [per_device(): other = lax.ppermute(inner, 'ty', swap)]
    scatter x0 -> x1, other arithmetic: none -> 1.97 us  [per_device(): return early.at[:, :, :, rows].set(inner_out)]
    reshape x0 -> x1, local copies, waits for them, and re-layouts: none -> 1.8 us  [per_device(): grouped[:, :, :, ::groups - 1]]
    all_gather x1, waiting for transfers between devices: 19.1 us -> 20.7 us  [per_device(): held = lax.all_gather(outer, 'tz', axis=0, tiled=True)]
    sub x2 -> x1, other arithmetic: 5 us -> 3.44 us  [per_device(): base - step * (spatial + early_term)]
    slice x1, local copies, waits for them, and re-layouts: 0.88 us -> 2.16 us  [section_spatial(): jacobians[direction, :, source].reshape((1, -1) + (1,) * (state.ndim - 2))]
    slice x2 -> x1, local copies, waits for them, and re-layouts: 2.69 us -> 1.61 us  [extended_2(): lax.slice_in_dim(block, 0, width, axis=dim)]
  transfers between devices with their start and end apart: 6 -> 6, of which waited for: 4 -> 4; matrix products, arithmetic and copies ran while one was open for 19% -> 21% of each run, Pallas kernels for 0% -> 0%
where the time goes in v9:
time: 118 us; the launch traced here: 117 us
  waiting for transfers between devices  54.6 us (46%)
  starting transfers between devices  19.6 us (17%)
  between operations  13.9 us (12%)
  other arithmetic  13.8 us (12%)
  local copies, waits for them, and re-layouts  13.1 us (11%)
  matrix products  2.13 us (2%)
    reduce_scatter x1, waiting for transfers between devices, per_device(): lax.psum_scatter(contributions, 'tz', scatter_dimension=0, tiled=True)  20.7 us
    all_gather x1, waiting for transfers between devices, per_device(): held = lax.all_gather(outer, 'tz', axis=0, tiled=True)  20.7 us
    ppermute x1, waiting for transfers between devices, per_device(): received = lax.ppermute(message, 'ty', swap)  8.71 us
    ppermute x1, starting transfers between devices, per_device(): received = lax.ppermute(message, 'ty', swap)  7.27 us
    ppermute x1, starting transfers between devices, extended_2(): lax.ppermute(lax.slice_in_dim(block, 0, width, axis=dim), axis, backward)  5.2 us
    ppermute x1, starting transfers between devices, per_device(): other = lax.ppermute(inner, 'ty', swap)  5.03 us
    ppermute x1, waiting for transfers between devices, per_device(): other = lax.ppermute(inner, 'ty', swap)  4.4 us
    sub x1, other arithmetic, per_device(): base - step * (spatial + early_term)  3.44 us
  transfers between devices with their start and end apart: 6, of which 4 were waited for; matrix products, arithmetic and copies ran while one was open for 21% of the time, Pallas kernels for 0%

profile of v9, /device:TPU:6, one launch (start us, length us, event | category | flops | bytes accessed | tf_op | source)
XLA Modules:
  0.0 117.2 jit_solution(775488761759843716)
XLA Ops:
  6.5 1.8 %slice_bitcast_fusion = f32[1,5,8,16,128]{4,3,2,1,0:T(8,128)} fusion(f32[1,5,8,4,8,128]{5,4,3,2,1,0:T(8,128)} %bitcast.68), kind=kLoop, calls=%fused_computation.24 | loop fusion | bytes 655360 | tf_op jit(solution)/shard_map/reshape | solution.py:93
  8.4 1.6 %fusion.21 = (f32[1,5,1,32,128]{4,3,2,1,0:T(8,128)}, f32[1,5,1,32,128]{4,3,2,1,0:T(8,128)}) fusion(f32[1,5,8,32,128]{4,3,2,1,0:T(8,128)} %param.9), kind=kLoop, calls=%fused_computation.116 | loop fusion | bytes 327680 | tf_op jit(solution)/shard_map/slice | solution.py:23
  10.0 5.2 %collective-permute-start = (f32[1,5,1,32,128]{4,3,2,1,0:T(8,128)}, f32[1,5,1,32,128]{4,3,2,1,0:T(8,128)}, u32[]{:S(2)}, u32[]{:S(2)}) collective-permute-start(f32[1,5,1,32,128]{4,3,2,1,0:T(8,128)} %get-tuple-element.59), channel_id=1, source_target_pairs={{1,0},{2,1},{3,2},{4,3},{5,4},{6,5},{7,6},{8,7},{9,8},{10,9},{11,1... | collective-permute-start | bytes 245768 | tf_op jit(solution)/shard_map/ppermute | solution.py:23
  15.3 2.1 %collective-permute-start.1 = (f32[1,5,1,32,128]{4,3,2,1,0:T(8,128)}, f32[1,5,1,32,128]{4,3,2,1,0:T(8,128)}, u32[]{:S(2)}, u32[]{:S(2)}) collective-permute-start(f32[1,5,1,32,128]{4,3,2,1,0:T(8,128)} %get-tuple-element.60), channel_id=1, source_target_pairs={{0,1},{1,2},{2,3},{3,4},{4,5},{5,6},{6,7},{7,8},{8,9},{9,10},{10,1... | collective-permute-start | bytes 245768 | tf_op jit(solution)/shard_map/ppermute | solution.py:20
  17.3 1.9 %slice_bitcast_fusion.18 = (f32[5,8,16,128]{3,2,1,0:T(8,128)}, f32[1,5,8,16,128]{4,3,2,1,0:T(8,128)}) fusion(f32[1,5,8,32,128]{4,3,2,1,0:T(8,128)} %param.9), kind=kLoop, calls=%fused_computation.114 | loop fusion | bytes 983040 | tf_op jit(solution)/shard_map/mul | solution.py:88
  19.2 5.0 %collective-permute-start.3 = (f32[1,5,8,16,128]{4,3,2,1,0:T(8,128)}, f32[1,5,8,16,128]{4,3,2,1,0:T(8,128)}, u32[]{:S(2)}, u32[]{:S(2)}) collective-permute-start(f32[1,5,8,16,128]{4,3,2,1,0:T(8,128)} %get-tuple-element.43), channel_id=1, source_target_pairs={{0,32},{32,0},{1,33},{33,1},{2,34},{34,2},{3,35},{35,3},{4,36},{36... | collective-permute-start | bytes 983048 | tf_op jit(solution)/shard_map/ppermute | solution.py:84
  24.3 0.7 broadcast_subtract_fusion
  24.9 2.2 %slice_reduce_fusion.14 = (f32[5]{0:T(128)S(1)}, f32[5]{0:T(128)S(1)}, f32[5]{0:T(128)S(1)}, f32[5]{0:T(128)}, f32[5]{0:T(128)}, /*index=5*/f32[5]{0:T(128)}, f3...) fusion(f32[3,5,5]{2,0,1:T(4,128)} %param.13), kind=kLoop, calls=%fused_computation.73 | loop fusion | bytes 600 | tf_op jit(solution)/shard_map/slice | solution.py:64
  28.4 0.7 compare_convert_fusion
  29.1 0.8 slice_bitcast_fusion.5
  30.0 0.6 pad.5.clone
  30.8 4.4 %collective-permute-done.3 = f32[1,5,8,16,128]{4,3,2,1,0:T(8,128)} collective-permute-done((f32[1,5,8,16,128]{4,3,2,1,0:T(8,128)}, f32[1,5,8,16,128]{4,3,2,1,0:T(8,128)}, u32[]{:S(2)}, u32[]{:S(2)}) %collective-permute-start.3) | collective-permute-done | bytes 327712 | tf_op jit(solution)/shard_map/ppermute | solution.py:84
  35.2 2.9 %multiply_add_fusion = f32[8,5,8,16,128]{4,3,2,1,0:T(8,128)} fusion(f32[5,8,16,128]{3,2,1,0:T(8,128)} %bitcast.37, f32[8]{0:T(128)S(1)} %get-tuple-element.79, f32[5,8,16,128]{3,2,1,0:T(8,128)S(1)} %copy-done.3, f32[8]{0:T(128)S(1)} %get-tuple-element.80), kind=kLoop, calls=%fused_computation.1 | loop fusion | flops 1966080 | bytes 3276864 | tf_op jit(solution)/shard_map/add | solution.py:88
  38.2 0.8 subtract_select_fusion
  39.0 20.7 %all-gather.2.cloned.1.call-done = f32[8,5,8,16,128]{4,3,2,1,0:T(8,128)} async-done(((f32[1,5,8,16,128]{4,3,2,1,0:T(8,128)}), f32[8,5,8,16,128]{4,3,2,1,0:T(8,128)}) %all-gather.2.cloned.1.call-update) | async-done | bytes 2621456 | tf_op jit(solution)/shard_map/all_gather | solution.py:94
  59.7 2.2 %fusion.20 = (f32[8,5,8,1,128]{4,3,2,1,0:T(1,128)S(1)}, f32[8,5,8,1,128]{4,3,2,1,0:T(1,128)S(1)}) fusion(f32[8,5,8,16,128]{4,3,2,1,0:T(8,128)} %all-gather.2.cloned.1.call-done), kind=kLoop, calls=%fused_computation.115 | loop fusion | bytes 655360 | tf_op jit(solution)/shard_map/slice | solution.py:99
  61.9 2.1 %convolution_bitcast_fusion = f32[2,5,8,128,8]{3,4,1,2,0:T(8,128)S(1)} fusion(s32[2,8,128]{2,1,0:T(8,128)} %param.14, f32[1,8,5,8,128]{4,1,2,3,0:T(8,128)S(1)} %get-tuple-element.77, f32[1,8,5,8,128]{4,1,2,3,0:T(8,128)S(1)} %get-tuple-element.78), kind=kOutput, calls=%fused_computation.2 | convolution fusion | flops 126173184 | bytes 663552 | tf_op jit(solution)/shard_map/szvir,sikr->szvik/dot_general | solution.py:104
  64.1 1.1 multiply_reduce_fusion.1
  65.7 7.3 %collective-permute-start.2 = (f32[92160]{0:T(1024)S(1)}, f32[92160]{0:T(1024)S(1)}, u32[]{:S(2)}, u32[]{:S(2)}) collective-permute-start(f32[92160]{0:T(1024)S(1)} %pad_maximum_fusion.4), channel_id=1, source_target_pairs={{0,32},{32,0},{1,33},{33,1},{2,34},{34,2},{3,35},{35,3},{4,36},{36... | collective-permute-start | bytes 1105928 | tf_op jit(solution)/shard_map/ppermute | solution.py:111
  73.0 1.0 subtract_multiply_fusion.2
  74.1 8.7 %collective-permute-done.2 = f32[92160]{0:T(1024)S(1)} collective-permute-done((f32[92160]{0:T(1024)S(1)}, f32[92160]{0:T(1024)S(1)}, u32[]{:S(2)}, u32[]{:S(2)}) %collective-permute-start.2) | collective-permute-done | bytes 368672 | tf_op jit(solution)/shard_map/ppermute | solution.py:111
  84.2 3.4 %fusion.3 = (f32[1,5,8,32,128]{4,3,2,1,0:T(8,128)}, f32[1,5,8,32,128]{4,3,2,1,0:T(8,128)}) fusion(f32[1,5,8,32,128]{4,3,2,1,0:T(8,128)S(1)} %copy-done.2, f32[1,5,8,8,128]{4,3,2,1,0:T(8,128)S(1)} %get-tuple-element.66, f32[1,5,8,8,128]{4,3,2,1,0:T(8,128)S(1)} %get-tuple-element.65, f32[32]{0:T(128)S(1)} %copy-done.24, ...), kind=kLoop, calls=%fused_computation.11 | loop fusion | flops 7700480 | bytes 7952812 | tf_op jit(solution)/shard_map/sub | solution.py:126
  87.7 20.7 %reduce-scatter.2.cloned.1.call-done = f32[1,5,8,16,128]{4,3,2,1,0:T(8,128)} async-done(((f32[8,5,8,16,128]{4,3,2,1,0:T(8,128)}), f32[1,5,8,16,128]{4,3,2,1,0:T(8,128)}) %reduce-scatter.2.cloned.1.call-update) | async-done | bytes 327696 | tf_op jit(solution)/shard_map/reduce_scatter | solution.py:89
  108.4 2.0 %subtract_dynamic-update-slice_fusion = f32[1,5,8,32,128]{4,3,2,1,0:T(8,128)} fusion(f32[1,5,8,32,128]{4,3,2,1,0:T(8,128)} %get-tuple-element.19, f32[1,5,8,16,128]{4,3,2,1,0:T(8,128)} %reduce-scatter.2.cloned.1.call-done, f32[1,5,8,32,128]{4,3,2,1,0:T(8,128)} %get-tuple-element.20, f32[1,5,8,32,128]{4,3,2,1,0:T(8,128)} %param.10, ...), kind=kLoop, calls=%fused_computation.23 | loop fusion | flops 245760 | bytes 1376256 | tf_op jit(solution)/shard_map/scatter | solution.py:129
  (82 shorter events, 3.2 us)
Async XLA Ops:
  6.5 20.6 %copy-start = (f32[1,5,8,32,128]{4,3,2,1,0:T(8,128)S(1)}, f32[1,5,8,32,128]{4,3,2,1,0:T(8,128)}, u32[]{:S(2)}) copy-start(f32[1,5,8,32,128]{4,3,2,1,0:T(8,128)} %param.9) | copy-start | bytes 1966084
  6.5 53.2 %all-gather.2.cloned.1.call-start = ((), (), s32[]{:S(2)}) async-start(), calls=%async_computation.1 | async-start | bytes 2949120 | tf_op jit(solution)/shard_map/all_gather | solution.py:94
  8.4 100.0 %reduce-scatter.2.cloned.1.call-start = ((), (), s32[]{:S(2)}) async-start(), calls=%async_computation.2 | async-start | bytes 2949120 | tf_op jit(solution)/shard_map/reduce_scatter | solution.py:89
  10.0 63.0 %collective-permute-start = (f32[1,5,1,32,128]{4,3,2,1,0:T(8,128)}, f32[1,5,1,32,128]{4,3,2,1,0:T(8,128)}, u32[]{:S(2)}, u32[]{:S(2)}) collective-permute-start(f32[1,5,1,32,128]{4,3,2,1,0:T(8,128)} %get-tuple-element.59), channel_id=1, source_target_pairs={{1,0},{2,1},{3,2},{4,3},{5,4},{6,5},{7,6},{8,7},{9,8},{10,9},{11,1... | collective-permute-start | bytes 245768 | tf_op jit(solution)/shard_map/ppermute | solution.py:23
  15.2 12.4 %copy-start.10 = (s32[1,2,8,128]{3,2,1,0:T(8,128)S(1)}, s32[1,2,8,128]{3,2,1,0:T(8,128)}, u32[]{:S(2)}) copy-start(s32[1,2,8,128]{3,2,1,0:T(8,128)} %param.15) | copy-start | bytes 24580
  15.2 12.5 %copy-start.9 = (f32[8,32,128]{2,1,0:T(8,128)S(1)}, f32[8,32,128]{2,1,0:T(8,128)}, u32[]{:S(2)}) copy-start(f32[8,32,128]{2,1,0:T(8,128)} %param.11) | copy-start | bytes 393220
  15.3 57.7 %collective-permute-start.1 = (f32[1,5,1,32,128]{4,3,2,1,0:T(8,128)}, f32[1,5,1,32,128]{4,3,2,1,0:T(8,128)}, u32[]{:S(2)}, u32[]{:S(2)}) collective-permute-start(f32[1,5,1,32,128]{4,3,2,1,0:T(8,128)} %get-tuple-element.60), channel_id=1, source_target_pairs={{0,1},{1,2},{2,3},{3,4},{4,5},{5,6},{6,7},{7,8},{8,9},{9,10},{10,1... | collective-permute-start | bytes 245768 | tf_op jit(solution)/shard_map/ppermute | solution.py:20
  19.2 16.0 %collective-permute-start.3 = (f32[1,5,8,16,128]{4,3,2,1,0:T(8,128)}, f32[1,5,8,16,128]{4,3,2,1,0:T(8,128)}, u32[]{:S(2)}, u32[]{:S(2)}) collective-permute-start(f32[1,5,8,16,128]{4,3,2,1,0:T(8,128)} %get-tuple-element.43), channel_id=1, source_target_pairs={{0,32},{32,0},{1,33},{33,1},{2,34},{34,2},{3,35},{35,3},{4,36},{36... | collective-permute-start | bytes 983048 | tf_op jit(solution)/shard_map/ppermute | solution.py:84
  24.3 4.8 %copy-start.23 = (s32[8]{0:T(128)}, s32[8]{0:T(128)S(1)}, u32[]{:S(2)}) copy-start(s32[8]{0:T(128)S(1)} %multiply_add_fusion.3) | copy-start | bytes 100
  27.6 7.6 %copy-start.3 = (f32[5,8,16,128]{3,2,1,0:T(8,128)S(1)}, f32[5,8,16,128]{3,2,1,0:T(8,128)}, u32[]{:S(2)}) copy-start(f32[5,8,16,128]{3,2,1,0:T(8,128)} %get-tuple-element.42) | copy-start | bytes 983044
  59.7 5.5 %copy-start.1 = (f32[8,5,8,16,128]{4,3,2,1,0:T(8,128)S(1)}, f32[8,5,8,16,128]{4,3,2,1,0:T(8,128)}, u32[]{:S(2)}) copy-start(f32[8,5,8,16,128]{4,3,2,1,0:T(8,128)} %all-gather.2.cloned.1.call-done) | copy-start | bytes 7864324
  65.7 17.1 %collective-permute-start.2 = (f32[92160]{0:T(1024)S(1)}, f32[92160]{0:T(1024)S(1)}, u32[]{:S(2)}, u32[]{:S(2)}) collective-permute-start(f32[92160]{0:T(1024)S(1)} %pad_maximum_fusion.4), channel_id=1, source_target_pairs={{0,32},{32,0},{1,33},{33,1},{2,34},{34,2},{3,35},{35,3},{4,36},{36... | collective-permute-start | bytes 1105928 | tf_op jit(solution)/shard_map/ppermute | solution.py:111
  82.9 1.2 %copy-start.7 = (f32[8,32,128]{2,1,0:T(8,128)S(1)}, f32[8,32,128]{2,1,0:T(8,128)}, u32[]{:S(2)}) copy-start(f32[8,32,128]{2,1,0:T(8,128)} %get-tuple-element.58) | copy-start | bytes 393220
  82.9 1.2 %copy-start.8 = (f32[8,32,128]{2,1,0:T(8,128)S(1)}, f32[8,32,128]{2,1,0:T(8,128)}, u32[]{:S(2)}) copy-start(f32[8,32,128]{2,1,0:T(8,128)} %param.12) | copy-start | bytes 393220
  82.9 1.2 %copy-start.11 = (f32[5]{0:T(128)S(1)}, f32[5]{0:T(128)}, u32[]{:S(2)}) copy-start(f32[5]{0:T(128)} %get-tuple-element.24) | copy-start | bytes 64
  82.9 1.2 %copy-start.12 = (f32[5]{0:T(128)S(1)}, f32[5]{0:T(128)}, u32[]{:S(2)}) copy-start(f32[5]{0:T(128)} %get-tuple-element.25) | copy-start | bytes 64
  82.9 1.2 %copy-start.13 = (f32[5]{0:T(128)S(1)}, f32[5]{0:T(128)}, u32[]{:S(2)}) copy-start(f32[5]{0:T(128)} %get-tuple-element.26) | copy-start | bytes 64
  82.9 1.2 %copy-start.14 = (f32[5]{0:T(128)S(1)}, f32[5]{0:T(128)}, u32[]{:S(2)}) copy-start(f32[5]{0:T(128)} %get-tuple-element.27) | copy-start | bytes 64
  82.9 1.2 %copy-start.15 = (f32[5]{0:T(128)S(1)}, f32[5]{0:T(128)}, u32[]{:S(2)}) copy-start(f32[5]{0:T(128)} %get-tuple-element.28) | copy-start | bytes 64
  83.0 1.2 %copy-start.16 = (f32[5]{0:T(128)S(1)}, f32[5]{0:T(128)}, u32[]{:S(2)}) copy-start(f32[5]{0:T(128)} %get-tuple-element.29) | copy-start | bytes 64
  83.0 1.2 %copy-start.17 = (f32[5]{0:T(128)S(1)}, f32[5]{0:T(128)}, u32[]{:S(2)}) copy-start(f32[5]{0:T(128)} %get-tuple-element.30) | copy-start | bytes 64
  83.0 1.2 %copy-start.18 = (f32[5]{0:T(128)S(1)}, f32[5]{0:T(128)}, u32[]{:S(2)}) copy-start(f32[5]{0:T(128)} %get-tuple-element.31) | copy-start | bytes 64
  83.0 1.2 %copy-start.19 = (f32[5]{0:T(128)S(1)}, f32[5]{0:T(128)}, u32[]{:S(2)}) copy-start(f32[5]{0:T(128)} %get-tuple-element.32) | copy-start | bytes 64
  83.0 1.2 %copy-start.20 = (f32[5]{0:T(128)S(1)}, f32[5]{0:T(128)}, u32[]{:S(2)}) copy-start(f32[5]{0:T(128)} %get-tuple-element.33) | copy-start | bytes 64
  (7 other events, 8.1 us)
Sparse Core Ops, SparseCore 0:
  9.4 50.2 all-gather.1
  62.5 45.8 reduce-scatter.1

commit v10 on v9

--- a/solution.py
+++ b/solution.py
@@ -80,7 +80,7 @@
     pitch = state.shape[3]
     edge = pitch // 4
 
-    inner = state[:, :, :, edge : pitch - edge]
+    inner = state[:, :, :, edge : 2 * edge]
     other = lax.ppermute(inner, "ty", swap)
     expand = (ring,) + (1,) * (inner.ndim - 1)
     own_weights = time_weights(ring_ids - own, total_count).reshape(expand)
@@ -88,9 +88,7 @@
     contributions = own_weights * inner + partner_weights * other
     inner_term = lax.psum_scatter(contributions, "tz", scatter_dimension=0, tiled=True)
 
-    groups = pitch // edge
-    grouped = state.reshape(state.shape[:3] + (groups, edge, state.shape[4]))
-    outer = grouped[:, :, :, :: groups - 1].reshape(state.shape[:3] + (2 * edge, state.shape[4]))
+    outer = jnp.concatenate([state[:, :, :, :edge], state[:, :, :, 2 * edge :]], axis=3)
     held = lax.all_gather(outer, "tz", axis=0, tiled=True)
     targets = jnp.stack([own, partner])
     weights = time_weights(targets[:, None] - ring_ids[None, :], total_count)
@@ -124,7 +122,7 @@
     spatial = section_spatial(state, eddy_visc, jacobians, up_i, down_i, low_ghost, high_ghost)
     step = SECTION_ALPHA * pseudo_step[None, None]
     early, spatial = lax.optimization_barrier((base - step * (spatial + early_term), spatial))
-    rows = slice(edge, pitch - edge)
+    rows = slice(edge, 2 * edge)
     inner_out = base[:, :, :, rows] - step[:, :, :, rows] * (spatial[:, :, :, rows] + inner_term)
     return early.at[:, :, :, rows].set(inner_out)
 

time: 118 us -> 123 us (1.042)
  waiting for transfers between devices: 54.6 us -> 64.3 us
  local copies, waits for them, and re-layouts: 13.1 us -> 8.54 us
    all_gather x1, waiting for transfers between devices: 20.7 us -> 37.3 us  [per_device(): held = lax.all_gather(outer, 'tz', axis=0, tiled=True)]
    reduce_scatter x1, waiting for transfers between devices: 20.7 us -> 6.34 us  [per_device(): lax.psum_scatter(contributions, 'tz', scatter_dimension=0, tiled=True)]
    ppermute x1, waiting for transfers between devices: 8.71 us -> 16 us  [per_device(): received = lax.ppermute(message, 'ty', swap)]
    reduce_sum x1, other arithmetic: 0.43 us -> 2.85 us  [per_device(): jnp.sum(weights.reshape((2, ring) + (1,) * (held.ndim - 1)) * held[None],...]
    slice x1, local copies, waits for them, and re-layouts: 2.16 us -> 0.31 us  [section_spatial(): jacobians[direction, :, source].reshape((1, -1) + (1,) * (state.ndim - 2))]
    reshape x1 -> x0, local copies, waits for them, and re-layouts: 1.8 us -> none  [per_device(): grouped[:, :, :, ::groups - 1]]
  transfers between devices with their start and end apart: 6 -> 6, of which waited for: 4 -> 4; matrix products, arithmetic and copies ran while one was open for 21% -> 15% of each run, Pallas kernels for 0% -> 0%
where the time goes in v10:
time: 123 us; the launch traced here: 122 us
  waiting for transfers between devices  64.3 us (52%)
  starting transfers between devices  19.6 us (16%)
  other arithmetic  14.6 us (12%)
  between operations  13.8 us (11%)
  local copies, waits for them, and re-layouts  8.54 us (7%)
  matrix products  1.43 us (1%)
    all_gather x1, waiting for transfers between devices, per_device(): held = lax.all_gather(outer, 'tz', axis=0, tiled=True)  37.3 us
    ppermute x1, waiting for transfers between devices, per_device(): received = lax.ppermute(message, 'ty', swap)  16 us
    ppermute x1, starting transfers between devices, per_device(): received = lax.ppermute(message, 'ty', swap)  7.37 us
    reduce_scatter x1, waiting for transfers between devices, per_device(): lax.psum_scatter(contributions, 'tz', scatter_dimension=0, tiled=True)  6.34 us
    ppermute x1, starting transfers between devices, extended_2(): lax.ppermute(lax.slice_in_dim(block, 0, width, axis=dim), axis, backward)  5.2 us
    ppermute x1, starting transfers between devices, per_device(): other = lax.ppermute(inner, 'ty', swap)  5.04 us
    ppermute x1, waiting for transfers between devices, per_device(): other = lax.ppermute(inner, 'ty', swap)  4.57 us
    sub x1, other arithmetic, per_device(): base - step * (spatial + early_term)  3.37 us
  transfers between devices with their start and end apart: 6, of which 4 were waited for; matrix products, arithmetic and copies ran while one was open for 15% of the time, Pallas kernels for 0%

profile of v10, /device:TPU:6, one launch (start us, length us, event | category | flops | bytes accessed | tf_op | source)
XLA Modules:
  0.0 122.2 jit_solution(15425733781177143373)
XLA Ops:
  6.5 1.8 %slice_bitcast_fusion.17 = (f32[5,8,8,128]{3,2,1,0:T(8,128)S(1)}, f32[1,5,8,8,128]{4,3,2,1,0:T(8,128)S(1)}, f32[1,5,8,8,128]{4,3,2,1,0:T(8,128)}) fusion(f32[1,5,8,32,128]{4,3,2,1,0:T(8,128)} %param.9), kind=kLoop, calls=%fused_computation.114 | loop fusion | bytes 819200 | tf_op jit(solution)/shard_map/mul | solution.py:88
  8.3 0.8 pad_maximum_fusion.5
  9.2 0.7 fusion.21
  9.9 5.2 %collective-permute-start = (f32[1,5,1,32,128]{4,3,2,1,0:T(8,128)}, f32[1,5,1,32,128]{4,3,2,1,0:T(8,128)}, u32[]{:S(2)}, u32[]{:S(2)}) collective-permute-start(f32[1,5,1,32,128]{4,3,2,1,0:T(8,128)} %get-tuple-element.60), channel_id=1, source_target_pairs={{1,0},{2,1},{3,2},{4,3},{5,4},{6,5},{7,6},{8,7},{9,8},{10,9},{11,1... | collective-permute-start | bytes 245768 | tf_op jit(solution)/shard_map/ppermute | solution.py:23
  15.1 1.9 %collective-permute-start.1 = (f32[1,5,1,32,128]{4,3,2,1,0:T(8,128)}, f32[1,5,1,32,128]{4,3,2,1,0:T(8,128)}, u32[]{:S(2)}, u32[]{:S(2)}) collective-permute-start(f32[1,5,1,32,128]{4,3,2,1,0:T(8,128)} %get-tuple-element.61), channel_id=1, source_target_pairs={{0,1},{1,2},{2,3},{3,4},{4,5},{5,6},{6,7},{7,8},{8,9},{9,10},{10,1... | collective-permute-start | bytes 245768 | tf_op jit(solution)/shard_map/ppermute | solution.py:20
  17.0 5.0 %collective-permute-start.3 = (f32[1,5,8,8,128]{4,3,2,1,0:T(8,128)}, f32[1,5,8,8,128]{4,3,2,1,0:T(8,128)}, u32[]{:S(2)}, u32[]{:S(2)}) collective-permute-start(f32[1,5,8,8,128]{4,3,2,1,0:T(8,128)} %get-tuple-element.44), channel_id=1, source_target_pairs={{0,32},{32,0},{1,33},{33,1},{2,34},{34,2},{3,35},{35,3},{4,36},{36... | collective-permute-start | bytes 491528 | tf_op jit(solution)/shard_map/ppermute | solution.py:84
  22.7 0.5 copy-done.9
  23.3 0.7 compare_convert_fusion
  24.0 0.7 fusion.19
  24.7 0.7 slice_bitcast_fusion.4
  25.7 4.6 %collective-permute-done.3 = f32[1,5,8,8,128]{4,3,2,1,0:T(8,128)} collective-permute-done((f32[1,5,8,8,128]{4,3,2,1,0:T(8,128)}, f32[1,5,8,8,128]{4,3,2,1,0:T(8,128)}, u32[]{:S(2)}, u32[]{:S(2)}) %collective-permute-start.3) | collective-permute-done | bytes 163872 | tf_op jit(solution)/shard_map/ppermute | solution.py:84
  30.3 2.3 %multiply_add_fusion = f32[8,5,8,8,128]{4,3,2,1,0:T(8,128)} fusion(f32[5,8,8,128]{3,2,1,0:T(8,128)} %bitcast.35, f32[8]{0:T(128)S(1)} %get-tuple-element.78, f32[5,8,8,128]{3,2,1,0:T(8,128)S(1)} %get-tuple-element.42, f32[8]{0:T(128)S(1)} %get-tuple-element.79), kind=kLoop, calls=%fused_computation.1 | loop fusion | flops 983040 | bytes 1638464 | tf_op jit(solution)/shard_map/add | solution.py:88
  32.6 37.3 %all-gather.2.cloned.1.call-done = f32[8,5,8,24,128]{4,3,2,1,0:T(8,128)} async-done(((f32[1,5,8,24,128]{4,3,2,1,0:T(8,128)}), f32[8,5,8,24,128]{4,3,2,1,0:T(8,128)}) %all-gather.2.cloned.1.call-update) | async-done | bytes 3932176 | tf_op jit(solution)/shard_map/all_gather | solution.py:92
  69.9 2.0 %fusion.20 = (f32[8,5,8,1,128]{4,3,2,1,0:T(1,128)S(1)}, f32[8,5,8,1,128]{4,3,2,1,0:T(1,128)S(1)}) fusion(f32[8,5,8,24,128]{4,3,2,1,0:T(8,128)} %all-gather.2.cloned.1.call-done), kind=kLoop, calls=%fused_computation.115 | loop fusion | bytes 655360 | tf_op jit(solution)/shard_map/slice | solution.py:97
  72.0 1.4 %convolution_bitcast_fusion = f32[2,5,8,128,8]{3,4,1,2,0:T(8,128)S(1)} fusion(s32[2,8,128]{2,1,0:T(8,128)S(1)} %copy-done.10, f32[1,8,5,8,128]{4,1,2,3,0:T(8,128)S(1)} %get-tuple-element.76, f32[1,8,5,8,128]{4,1,2,3,0:T(8,128)S(1)} %get-tuple-element.77), kind=kOutput, calls=%fused_computation.2 | convolution fusion | flops 126173184 | bytes 663552 | tf_op jit(solution)/shard_map/szvir,sikr->szvik/dot_general | solution.py:102
  73.6 2.9 %multiply_reduce_fusion = f32[2,5,8,24,128]{4,3,2,1,0:T(8,128)S(1)} fusion(f32[8,5,8,24,128]{4,3,2,1,0:T(8,128)} %all-gather.2.cloned.1.call-done, f32[2,8]{1,0:T(2,128)S(1)} %subtract_select_fusion), kind=kLoop, calls=%fused_computation | loop fusion | flops 3686400 | bytes 4915264 | tf_op jit(solution)/shard_map/reduce_sum | solution.py:95
  76.6 7.4 %collective-permute-start.2 = (f32[133120]{0:T(1024)S(1)}, f32[133120]{0:T(1024)S(1)}, u32[]{:S(2)}, u32[]{:S(2)}) collective-permute-start(f32[133120]{0:T(1024)S(1)} %pad_maximum_fusion.4), channel_id=1, source_target_pairs={{0,32},{32,0},{1,33},{33,1},{2,34},{34,2},{3,35},{35,3},{4,36},{36... | collective-permute-start | bytes 1597448 | tf_op jit(solution)/shard_map/ppermute | solution.py:109
  84.0 0.8 slice_bitcast_fusion.16
  85.1 1.0 subtract_multiply_fusion.2
  86.2 16.0 %collective-permute-done.2 = f32[133120]{0:T(1024)S(1)} collective-permute-done((f32[133120]{0:T(1024)S(1)}, f32[133120]{0:T(1024)S(1)}, u32[]{:S(2)}, u32[]{:S(2)}) %collective-permute-start.2) | collective-permute-done | bytes 532512 | tf_op jit(solution)/shard_map/ppermute | solution.py:109
  102.8 0.8 copy-done.2
  103.8 3.4 %fusion.3 = (f32[1,5,8,32,128]{4,3,2,1,0:T(8,128)}, f32[1,5,8,32,128]{4,3,2,1,0:T(8,128)}) fusion(f32[1,5,8,32,128]{4,3,2,1,0:T(8,128)S(1)} %copy-done.3, f32[1,5,8,16,128]{4,3,2,1,0:T(8,128)S(1)} %slice.341, f32[1,5,8,8,128]{4,3,2,1,0:T(8,128)S(1)} %slice.340, f32[32]{0:T(128)S(1)} %pad.5.clone, f32[8,32,128]{2,1,0:T(8,128)S(1)} %get-tuple-element.67, ...), kind=kLoop, calls=%fused_computation.11 | loop fusion | flops 7700480 | bytes 8116652 | tf_op jit(solution)/shard_map/sub | solution.py:124
  107.2 6.3 %reduce-scatter.2.cloned.1.call-done = f32[1,5,8,8,128]{4,3,2,1,0:T(8,128)} async-done(((f32[8,5,8,8,128]{4,3,2,1,0:T(8,128)}), f32[1,5,8,8,128]{4,3,2,1,0:T(8,128)}) %reduce-scatter.2.cloned.1.call-update) | async-done | bytes 163856 | tf_op jit(solution)/shard_map/reduce_scatter | solution.py:89
  113.6 1.8 %subtract_dynamic-update-slice_fusion = f32[1,5,8,32,128]{4,3,2,1,0:T(8,128)} fusion(f32[1,5,8,32,128]{4,3,2,1,0:T(8,128)} %get-tuple-element.19, f32[1,5,8,8,128]{4,3,2,1,0:T(8,128)} %reduce-scatter.2.cloned.1.call-done, f32[1,5,8,32,128]{4,3,2,1,0:T(8,128)} %get-tuple-element.20, f32[1,5,8,32,128]{4,3,2,1,0:T(8,128)} %param.10, ...), kind=kLoop, calls=%fused_computation.26 | loop fusion | flops 122880 | bytes 688128 | tf_op jit(solution)/shard_map/scatter | solution.py:127
  (57 shorter events, 2.5 us)
Async XLA Ops:
  6.5 1.8 %slice-start = ((f32[1,5,8,32,128]{4,3,2,1,0:T(8,128)}), f32[1,5,8,16,128]{4,3,2,1,0:T(8,128)S(1)}, s32[]{:S(2)}) async-start(f32[1,5,8,32,128]{4,3,2,1,0:T(8,128)} %param.9), calls=%async_computation.3 | async-start | bytes 655360 | tf_op jit(solution)/shard_map/slice | solution.py:91
  6.5 63.3 %all-gather.2.cloned.1.call-start = ((), (), s32[]{:S(2)}) async-start(), calls=%async_computation.1 | async-start | bytes 4423680 | tf_op jit(solution)/shard_map/all_gather | solution.py:92
  6.5 2.7 %copy-start = (f32[1,5,8,32,128]{4,3,2,1,0:T(8,128)S(1)}, f32[1,5,8,32,128]{4,3,2,1,0:T(8,128)}, u32[]{:S(2)}) copy-start(f32[1,5,8,32,128]{4,3,2,1,0:T(8,128)} %param.9) | copy-start | bytes 1966084
  9.2 104.4 %reduce-scatter.2.cloned.1.call-start = ((), (), s32[]{:S(2)}) async-start(), calls=%async_computation.2 | async-start | bytes 1474560 | tf_op jit(solution)/shard_map/reduce_scatter | solution.py:89
  9.9 75.2 %collective-permute-start = (f32[1,5,1,32,128]{4,3,2,1,0:T(8,128)}, f32[1,5,1,32,128]{4,3,2,1,0:T(8,128)}, u32[]{:S(2)}, u32[]{:S(2)}) collective-permute-start(f32[1,5,1,32,128]{4,3,2,1,0:T(8,128)} %get-tuple-element.60), channel_id=1, source_target_pairs={{1,0},{2,1},{3,2},{4,3},{5,4},{6,5},{7,6},{8,7},{9,8},{10,9},{11,1... | collective-permute-start | bytes 245768 | tf_op jit(solution)/shard_map/ppermute | solution.py:23
  15.1 70.0 %collective-permute-start.1 = (f32[1,5,1,32,128]{4,3,2,1,0:T(8,128)}, f32[1,5,1,32,128]{4,3,2,1,0:T(8,128)}, u32[]{:S(2)}, u32[]{:S(2)}) collective-permute-start(f32[1,5,1,32,128]{4,3,2,1,0:T(8,128)} %get-tuple-element.61), channel_id=1, source_target_pairs={{0,1},{1,2},{2,3},{3,4},{4,5},{5,6},{6,7},{7,8},{8,9},{9,10},{10,1... | collective-permute-start | bytes 245768 | tf_op jit(solution)/shard_map/ppermute | solution.py:20
  17.0 13.2 %collective-permute-start.3 = (f32[1,5,8,8,128]{4,3,2,1,0:T(8,128)}, f32[1,5,8,8,128]{4,3,2,1,0:T(8,128)}, u32[]{:S(2)}, u32[]{:S(2)}) collective-permute-start(f32[1,5,8,8,128]{4,3,2,1,0:T(8,128)} %get-tuple-element.44), channel_id=1, source_target_pairs={{0,32},{32,0},{1,33},{33,1},{2,34},{34,2},{3,35},{35,3},{4,36},{36... | collective-permute-start | bytes 491528 | tf_op jit(solution)/shard_map/ppermute | solution.py:84
  22.4 2.2 %copy-start.1 = (f32[1,5,8,32,127]{4,3,2,1,0:T(8,128)}, f32[1,5,8,32,127]{4,3,2,1,0:T(8,128)S(1)}, u32[]{:S(2)}) copy-start(f32[1,5,8,32,127]{4,3,2,1,0:T(8,128)S(1)} %get-tuple-element.65) | copy-start | bytes 1950724
  22.4 0.7 copy-start.9
  22.5 1.5 %copy-start.8 = (f32[8,32,128]{2,1,0:T(8,128)S(1)}, f32[8,32,128]{2,1,0:T(8,128)}, u32[]{:S(2)}) copy-start(f32[8,32,128]{2,1,0:T(8,128)} %param.11) | copy-start | bytes 393220
  32.5 39.4 %copy-start.10 = (s32[2,8,128]{2,1,0:T(8,128)S(1)}, s32[2,8,128]{2,1,0:T(8,128)}, u32[]{:S(2)}) copy-start(s32[2,8,128]{2,1,0:T(8,128)} %param.14) | copy-start | bytes 24580
  32.6 40.8 %copy-start.5 = (f32[2,2,8,128,8]{3,4,2,1,0:T(8,128)S(1)}, f32[2,2,8,128,8]{3,4,2,1,0:T(8,128)}, u32[]{:S(2)}) copy-start(f32[2,2,8,128,8]{3,4,2,1,0:T(8,128)} %compare_convert_fusion) | copy-start | bytes 393220
  76.5 8.3 %copy-start.6 = (f32[3,5,5]{2,0,1:T(4,128)S(1)}, f32[3,5,5]{2,0,1:T(4,128)}, u32[]{:S(2)}) copy-start(f32[3,5,5]{2,0,1:T(4,128)} %param.13) | copy-start | bytes 904
  76.6 25.7 %collective-permute-start.2 = (f32[133120]{0:T(1024)S(1)}, f32[133120]{0:T(1024)S(1)}, u32[]{:S(2)}, u32[]{:S(2)}) collective-permute-start(f32[133120]{0:T(1024)S(1)} %pad_maximum_fusion.4), channel_id=1, source_target_pairs={{0,32},{32,0},{1,33},{33,1},{2,34},{34,2},{3,35},{35,3},{4,36},{36... | collective-permute-start | bytes 1597448 | tf_op jit(solution)/shard_map/ppermute | solution.py:109
  102.5 1.1 copy-start.2
  102.5 1.3 %copy-start.3 = (f32[1,5,8,32,128]{4,3,2,1,0:T(8,128)S(1)}, f32[1,5,8,32,128]{4,3,2,1,0:T(8,128)}, u32[]{:S(2)}) copy-start(f32[1,5,8,32,128]{4,3,2,1,0:T(8,128)} %param.10) | copy-start | bytes 1966084
  102.5 1.3 %copy-start.4 = (f32[8,32,128]{2,1,0:T(8,128)S(1)}, f32[8,32,128]{2,1,0:T(8,128)}, u32[]{:S(2)}) copy-start(f32[8,32,128]{2,1,0:T(8,128)} %get-tuple-element.59) | copy-start | bytes 393220
  102.5 1.3 %copy-start.7 = (f32[8,32,128]{2,1,0:T(8,128)S(1)}, f32[8,32,128]{2,1,0:T(8,128)}, u32[]{:S(2)}) copy-start(f32[8,32,128]{2,1,0:T(8,128)} %param.12) | copy-start | bytes 393220
Sparse Core Ops, SparseCore 0:
  9.4 60.3 all-gather.1
  72.7 40.8 reduce-scatter.1

commit v11 on v6

--- a/solution.py
+++ b/solution.py
@@ -80,21 +80,17 @@
     pitch = state.shape[3]
     edge = pitch // 4
 
-    inner = state[:, :, :, edge : pitch - edge]
-    other = lax.ppermute(inner, "ty", swap)
-    expand = (ring,) + (1,) * (inner.ndim - 1)
+    other = lax.ppermute(state, "ty", swap)
+    expand = (ring,) + (1,) * (state.ndim - 1)
     own_weights = time_weights(ring_ids - own, total_count).reshape(expand)
     partner_weights = time_weights(ring_ids - partner, total_count).reshape(expand)
-    contributions = own_weights * inner + partner_weights * other
-    inner_term = lax.psum_scatter(contributions, "tz", scatter_dimension=0, tiled=True)
+    contributions = own_weights * state + partner_weights * other
+    time_term = lax.psum_scatter(contributions, "tz", scatter_dimension=0, tiled=True)
 
-    outer = jnp.concatenate([state[:, :, :, :edge], state[:, :, :, pitch - edge :]], axis=3)
-    held = lax.all_gather(outer, "tz", axis=0, tiled=True)
+    faces_here = jnp.stack([state[:, :, :, -1, :], state[:, :, :, 0, :]], axis=1)
+    faces = jnp.moveaxis(lax.all_gather(faces_here, "tz", axis=0, tiled=True), 1, 0)
     targets = jnp.stack([own, partner])
-    weights = time_weights(targets[:, None] - ring_ids[None, :], total_count)
-    partial = jnp.sum(weights.reshape((2, ring) + (1,) * (held.ndim - 1)) * held[None], axis=1)
 
-    faces = jnp.stack([held[:, :, :, -1, :], held[:, :, :, 0, :]], axis=0)
     radial_count = partner_radial.shape[2]
     radial_hot = (partner_radial[..., None] == jnp.arange(radial_count, dtype=jnp.int32)).astype(
         jnp.float32
@@ -104,15 +100,7 @@
     sources = (partner_instance[0][None] + shifts) % total_count
     instance_hot = (sources[..., None] == ring_ids).astype(jnp.float32)
     picked = jnp.sum(instance_hot[:, :, None] * jnp.moveaxis(remapped, 1, -1)[None], axis=-1)
-
-    message = jnp.concatenate([partial[1].reshape(-1), picked[1].reshape(-1)])
-    received = lax.ppermute(message, "ty", swap)
-    split = partial[0].size
-    outer_term = partial[:1] + received[:split].reshape((1,) + partial.shape[1:])
-    ghosts = picked[0] + received[split:].reshape(picked.shape[1:])
-    time_term = jnp.concatenate(
-        [outer_term[:, :, :, :edge], inner_term, outer_term[:, :, :, edge:]], axis=3
-    )
+    ghosts = picked[0] + lax.ppermute(picked[1], "ty", swap)
     low_ghost = rotate_velocity(ghosts[0][None], -1.0)
     high_ghost = rotate_velocity(ghosts[1][None], 1.0)
 

time: 118 us -> 132 us (1.12)
  blocking collectives: 0 us -> 32 us
  local copies, waits for them, and re-layouts: 10.3 us -> 0.94 us
  other arithmetic: 14.4 us -> 8.69 us
  waiting for transfers between devices: 57 us -> 53.5 us
    all_gather x0 -> x1, blocking collectives: none -> 32 us  [per_device(): lax.all_gather(faces_here, 'tz', axis=0, tiled=True)]
    all_gather x1 -> x0, waiting for transfers between devices: 19.1 us -> none  [per_device(): held = lax.all_gather(outer, 'tz', axis=0, tiled=True)]
    ppermute x2, waiting for transfers between devices: 16.2 us -> 28.3 us  [the longest x1 28.3 us: per_device(): other = lax.ppermute(state, 'ty', swap)]
    ppermute x1, waiting for transfers between devices: 0.01 us -> 4.64 us  [extended_2(): lax.ppermute(lax.slice_in_dim(block, block.shape[dim] - width, None, axis...]
    ppermute x2, starting transfers between devices: 12.2 us -> 16.1 us  [the longest x1 8.35 us: per_device(): ghosts = picked[0] + lax.ppermute(picked[1], 'ty', swap)]
    slice x7 -> x1, local copies, waits for them, and re-layouts: 3.32 us -> 0.03 us  [per_device(): state[:, :, :, -1, :]]
    ppermute x1, starting transfers between devices: 5.2 us -> 1.92 us  [extended_2(): lax.ppermute(lax.slice_in_dim(block, 0, width, axis=dim), axis, backward)]
    mul x1 -> x0, local copies, waits for them, and re-layouts: 1.88 us -> none  [per_device(): contributions = own_weights * inner + partner_weights * other]
  transfers between devices with their start and end apart: 6 -> 5, of which waited for: 4 -> 3; matrix products, arithmetic and copies ran while one was open for 19% -> 4% of each run, Pallas kernels for 0% -> 0%
where the time goes in v11:
time: 132 us; the launch traced here: 131 us
  waiting for transfers between devices  53.5 us (41%)
  blocking collectives  32 us (24%)
  starting transfers between devices  20.4 us (15%)
  between operations  13.7 us (10%)
  other arithmetic  8.69 us (7%)
  matrix products  1.43 us (1%)
    all_gather x1, blocking collectives, per_device(): lax.all_gather(faces_here, 'tz', axis=0, tiled=True)  32 us
    ppermute x1, waiting for transfers between devices, per_device(): other = lax.ppermute(state, 'ty', swap)  28.3 us
    reduce_scatter x1, waiting for transfers between devices, per_device(): lax.psum_scatter(contributions, 'tz', scatter_dimension=0, tiled=True)  20.5 us
    ppermute x1, starting transfers between devices, per_device(): ghosts = picked[0] + lax.ppermute(picked[1], 'ty', swap)  8.35 us
    ppermute x1, starting transfers between devices, per_device(): other = lax.ppermute(state, 'ty', swap)  7.72 us
    ppermute x1, waiting for transfers between devices, extended_2(): lax.ppermute(lax.slice_in_dim(block, block.shape[dim] - width, None, axis...  4.64 us
    add x1, other arithmetic, per_device(): contributions = own_weights * state + partner_weights * other  4.31 us
  transfers between devices with their start and end apart: 5, of which 3 were waited for; matrix products, arithmetic and copies ran while one was open for 4% of the time, Pallas kernels for 0%

profile of v11, /device:TPU:6, one launch (start us, length us, event | category | flops | bytes accessed | tf_op | source)
XLA Modules:
  0.0 130.5 jit_solution(11863097195909009485)
XLA Ops:
  6.5 7.7 %collective-permute-start.3 = (f32[1,5,8,32,128]{4,3,2,1,0:T(8,128)}, f32[1,5,8,32,128]{4,3,2,1,0:T(8,128)S(1)}, u32[]{:S(2)}, u32[]{:S(2)}) collective-permute-start(f32[1,5,8,32,128]{4,3,2,1,0:T(8,128)} %param.7), channel_id=1, source_target_pairs={{0,32},{32,0},{1,33},{33,1},{2,34},{34,2},{3,35},{35,3},{4,36},{36... | collective-permute-start | bytes 1966088 | tf_op jit(solution)/shard_map/ppermute | solution.py:83
  14.3 0.1 compare_select_fusion.10
  14.3 28.3 %collective-permute-done.3 = f32[1,5,8,32,128]{4,3,2,1,0:T(8,128)S(1)} collective-permute-done((f32[1,5,8,32,128]{4,3,2,1,0:T(8,128)}, f32[1,5,8,32,128]{4,3,2,1,0:T(8,128)S(1)}, u32[]{:S(2)}, u32[]{:S(2)}) %collective-permute-start.3) | collective-permute-done | bytes 655392 | tf_op jit(solution)/shard_map/ppermute | solution.py:83
  42.7 4.3 %multiply_add_fusion = f32[8,5,8,32,128]{4,3,2,1,0:T(8,128)} fusion(f32[5,8,32,128]{3,2,1,0:T(8,128)S(1)} %bitcast.64, f32[8]{0:T(128)S(1)} %get-tuple-element.51, f32[5,8,32,128]{3,2,1,0:T(8,128)} %bitcast.63, f32[8]{0:T(128)S(1)} %get-tuple-element.52), kind=kLoop, calls=%fused_computation | loop fusion | flops 3932160 | bytes 6553664 | tf_op jit(solution)/shard_map/add | solution.py:87
  47.0 0.1 add_subtract_fusion
  47.2 32.0 %all_gather.3 = f32[8,2,5,8,128]{4,3,2,1,0:T(8,128)S(1)} all-gather(f32[1,2,5,8,128]{4,3,2,1,0:T(8,128)S(1)} %pad_maximum_fusion.4), channel_id=1, replica_groups=mesh['tz'=8,'ty'=2,'space'=32] {'tz'}, dimensions={0}, use_global_device_ids=true | all-gather | bytes 368640 | tf_op jit(solution)/shard_map/all_gather | solution.py:91
  79.1 0.1 add_select_fusion.1
  79.2 0.1 compare_convert_fusion
  79.3 1.4 %convolution_bitcast_fusion = f32[2,5,8,128,8]{3,4,1,2,0:T(8,128)S(1)} fusion(s32[2,8,128]{2,1,0:T(8,128)S(1)} %copy-done.6, f32[8,2,5,8,128]{4,3,2,1,0:T(8,128)S(1)} %all_gather.3), kind=kOutput, calls=%fused_computation.1 | convolution fusion | flops 126091264 | bytes 663552 | tf_op jit(solution)/shard_map/szvir,sikr->szvik/dot_general | solution.py:98
  80.8 0.2 multiply_reduce_fusion
  81.0 8.3 %collective-permute-start.2 = (f32[2,5,8,128]{3,2,1,0:T(8,128)S(1)}, f32[2,5,8,128]{3,2,1,0:T(8,128)S(1)}, u32[]{:S(2)}, u32[]{:S(2)}) collective-permute-start(f32[2,5,8,128]{3,2,1,0:T(8,128)S(1)} %slice_bitcast_fusion.15), channel_id=1, source_target_pairs={{0,32},{32,0},{1,33},{33,1},{2,34},{34,2},{3,35},{35,3},{4,36},{36... | collective-permute-start | bytes 122888 | tf_op jit(solution)/shard_map/ppermute | solution.py:103
  89.3 1.9 %collective-permute-start = (f32[1,5,1,32,128]{4,3,2,1,0:T(8,128)S(1)}, f32[1,5,1,32,128]{4,3,2,1,0:T(8,128)S(1)}, u32[]{:S(2)}, u32[]{:S(2)}) collective-permute-start(f32[1,5,1,32,128]{4,3,2,1,0:T(8,128)S(1)} %get-tuple-element.36), channel_id=1, source_target_pairs={{1,0},{2,1},{3,2},{4,3},{5,4},{6,5},{7,6},{8,7},{9,8},{10,9},{11,1... | collective-permute-start | bytes 245768 | tf_op jit(solution)/shard_map/ppermute | solution.py:23
  91.3 2.4 %collective-permute-start.1 = (f32[1,5,1,32,128]{4,3,2,1,0:T(8,128)S(1)}, f32[1,5,1,32,128]{4,3,2,1,0:T(8,128)S(1)}, u32[]{:S(2)}, u32[]{:S(2)}) collective-permute-start(f32[1,5,1,32,128]{4,3,2,1,0:T(8,128)S(1)} %get-tuple-element.35), channel_id=1, source_target_pairs={{0,1},{1,2},{2,3},{3,4},{4,5},{5,6},{6,7},{7,8},{8,9},{9,10},{10,1... | collective-permute-start | bytes 245768 | tf_op jit(solution)/shard_map/ppermute | solution.py:20
  93.7 0.2 fusion.16
  93.9 0.2 subtract_multiply_fusion
  94.3 0.1 fusion.14
  94.4 0.3 slice_reduce_fusion.14
  94.8 0.2 subtract_multiply_fusion.1
  95.0 0.1 slice_bitcast_fusion.9
  95.1 4.6 %collective-permute-done.1 = f32[1,5,1,32,128]{4,3,2,1,0:T(8,128)S(1)} collective-permute-done((f32[1,5,1,32,128]{4,3,2,1,0:T(8,128)S(1)}, f32[1,5,1,32,128]{4,3,2,1,0:T(8,128)S(1)}, u32[]{:S(2)}, u32[]{:S(2)}) %collective-permute-start.1) | collective-permute-done | bytes 81952 | tf_op jit(solution)/shard_map/ppermute | solution.py:20
  99.7 0.1 subtract_multiply_fusion.2
  99.9 1.2 multiply_subtract_fusion.1
  101.1 20.5 %reduce-scatter.2.cloned.1.call-done = f32[1,5,8,32,128]{4,3,2,1,0:T(8,128)} async-done(((f32[8,5,8,32,128]{4,3,2,1,0:T(8,128)}), f32[1,5,8,32,128]{4,3,2,1,0:T(8,128)}) %reduce-scatter.2.cloned.1.call-update) | async-done | bytes 655376 | tf_op jit(solution)/shard_map/reduce_scatter | solution.py:88
  121.6 2.1 %multiply_subtract_fusion = f32[1,5,8,32,128]{4,3,2,1,0:T(8,128)} fusion(f32[1,5,8,32,128]{4,3,2,1,0:T(8,128)S(1)} %copy-done.1, f32[1,5,8,32,128]{4,3,2,1,0:T(8,128)S(1)} %multiply_subtract_fusion.1, f32[1,5,8,32,128]{4,3,2,1,0:T(8,128)} %reduce-scatter.2.cloned.1.call-done, f32[8,32,128]{2,1,0:T(8,128)S(1)} %broadcast_multiply_fusion), kind=kLoop, calls=%fused_computation.8 | loop fusion | flops 491520 | bytes 2752512 | tf_op jit(solution)/shard_map/sub | solution.py:113
  (30 shorter events, 0.3 us)
Async XLA Ops:
  6.5 115.0 %reduce-scatter.2.cloned.1.call-start = ((), (), s32[]{:S(2)}) async-start(), calls=%async_computation.1 | async-start | bytes 5898240 | tf_op jit(solution)/shard_map/reduce_scatter | solution.py:88
  6.5 36.1 %collective-permute-start.3 = (f32[1,5,8,32,128]{4,3,2,1,0:T(8,128)}, f32[1,5,8,32,128]{4,3,2,1,0:T(8,128)S(1)}, u32[]{:S(2)}, u32[]{:S(2)}) collective-permute-start(f32[1,5,8,32,128]{4,3,2,1,0:T(8,128)} %param.7), channel_id=1, source_target_pairs={{0,32},{32,0},{1,33},{33,1},{2,34},{34,2},{3,35},{35,3},{4,36},{36... | collective-permute-start | bytes 1966088 | tf_op jit(solution)/shard_map/ppermute | solution.py:83
  42.7 4.4 %copy-start = (f32[1,5,8,32,128]{4,3,2,1,0:T(8,128)S(1)}, f32[1,5,8,32,128]{4,3,2,1,0:T(8,128)}, u32[]{:S(2)}) copy-start(f32[1,5,8,32,128]{4,3,2,1,0:T(8,128)} %param.7) | copy-start | bytes 1966084
  42.7 36.4 %copy-start.5 = (s32[1,2,8,128]{3,2,1,0:T(8,128)S(1)}, s32[1,2,8,128]{3,2,1,0:T(8,128)}, u32[]{:S(2)}) copy-start(s32[1,2,8,128]{3,2,1,0:T(8,128)} %param.13) | copy-start | bytes 24580
  42.7 36.6 %copy-start.6 = (s32[2,8,128]{2,1,0:T(8,128)S(1)}, s32[2,8,128]{2,1,0:T(8,128)}, u32[]{:S(2)}) copy-start(s32[2,8,128]{2,1,0:T(8,128)} %param.12) | copy-start | bytes 24580
  47.0 47.2 %copy-start.4 = (f32[8,32,128]{2,1,0:T(8,128)S(1)}, f32[8,32,128]{2,1,0:T(8,128)}, u32[]{:S(2)}) copy-start(f32[8,32,128]{2,1,0:T(8,128)} %param.9) | copy-start | bytes 393220
  79.2 15.2 %copy-start.2 = (f32[3,5,5]{2,0,1:T(4,128)S(1)}, f32[3,5,5]{2,0,1:T(4,128)}, u32[]{:S(2)}) copy-start(f32[3,5,5]{2,0,1:T(4,128)} %param.11) | copy-start | bytes 904
  81.0 13.8 %collective-permute-start.2 = (f32[2,5,8,128]{3,2,1,0:T(8,128)S(1)}, f32[2,5,8,128]{3,2,1,0:T(8,128)S(1)}, u32[]{:S(2)}, u32[]{:S(2)}) collective-permute-start(f32[2,5,8,128]{3,2,1,0:T(8,128)S(1)} %slice_bitcast_fusion.15), channel_id=1, source_target_pairs={{0,32},{32,0},{1,33},{33,1},{2,34},{34,2},{3,35},{35,3},{4,36},{36... | collective-permute-start | bytes 122888 | tf_op jit(solution)/shard_map/ppermute | solution.py:103
  89.3 5.7 %collective-permute-start = (f32[1,5,1,32,128]{4,3,2,1,0:T(8,128)S(1)}, f32[1,5,1,32,128]{4,3,2,1,0:T(8,128)S(1)}, u32[]{:S(2)}, u32[]{:S(2)}) collective-permute-start(f32[1,5,1,32,128]{4,3,2,1,0:T(8,128)S(1)} %get-tuple-element.36), channel_id=1, source_target_pairs={{1,0},{2,1},{3,2},{4,3},{5,4},{6,5},{7,6},{8,7},{9,8},{10,9},{11,1... | collective-permute-start | bytes 245768 | tf_op jit(solution)/shard_map/ppermute | solution.py:23
  91.3 8.5 %collective-permute-start.1 = (f32[1,5,1,32,128]{4,3,2,1,0:T(8,128)S(1)}, f32[1,5,1,32,128]{4,3,2,1,0:T(8,128)S(1)}, u32[]{:S(2)}, u32[]{:S(2)}) collective-permute-start(f32[1,5,1,32,128]{4,3,2,1,0:T(8,128)S(1)} %get-tuple-element.35), channel_id=1, source_target_pairs={{0,1},{1,2},{2,3},{3,4},{4,5},{5,6},{6,7},{7,8},{8,9},{9,10},{10,1... | collective-permute-start | bytes 245768 | tf_op jit(solution)/shard_map/ppermute | solution.py:20
  94.2 5.7 %copy-start.3 = (f32[8,32,128]{2,1,0:T(8,128)S(1)}, f32[8,32,128]{2,1,0:T(8,128)}, u32[]{:S(2)}) copy-start(f32[8,32,128]{2,1,0:T(8,128)} %param.10) | copy-start | bytes 393220
  95.0 26.6 %copy-start.1 = (f32[1,5,8,32,128]{4,3,2,1,0:T(8,128)S(1)}, f32[1,5,8,32,128]{4,3,2,1,0:T(8,128)}, u32[]{:S(2)}) copy-start(f32[1,5,8,32,128]{4,3,2,1,0:T(8,128)} %param.8) | copy-start | bytes 1966084
Sparse Core Ops, SparseCore 0:
  47.1 74.3 reduce-scatter.1
